TPU v7x, 768 devices: a whole 4x8x12 slice. The times are simulated.
768 devices in a mesh: dp: 16 (over x_hi, y), blk: 48 (over z, x_lo, core).
Axes of the slice: x: 4 (x_hi: 2, x_lo: 2; x = x_hi * 2 + x_lo), y: 8, z: 12, core: 2. Of those that a mesh axis runs over, the one named last changes fastest.
Arguments:
- tokens: bfloat16 [16, 48, 128, 4096], P('dp', 'blk'), may hold values from -6 to 6
- cotangent: bfloat16 [16, 48, 128, 4096], P('dp', 'blk'), may hold values from -6 to 6
- gate_weight: bfloat16 [4096, 14784], P(None, 'blk'), may hold values from -0.09375 to 0.09375
- up_weight: bfloat16 [4096, 14784], P(None, 'blk'), may hold values from -0.09375 to 0.09375
- down_weight: bfloat16 [4096, 14784], P(None, 'blk'), may hold values from -0.046875 to 0.046875
- counts: int32 [16, 48], P('dp', 'blk'), may hold values from 64 to 128, as said below
- seg_ids: int32 [16, 48, 128], P('dp', 'blk'), may hold values from 0 to 3, never falling along the last dimension, each value on 1 to 64 neighbouring positions
- pair_side: int32 [16, 48, 4], P('dp', 'blk'), may hold values 0 or 1
Outputs:
- grad_tokens: bfloat16 [16, 48, 128, 4096], P('dp', 'blk')
- panel_grads: float32 [3, 4096, 14784], P(None, 'dp', 'blk')
Inputs may be any that keep to these rules, and one draw needn't show every extreme that they name: `counts`: each device's count lies between 64 and 128; in every draw some device's count is exactly 128.
All inputs are finite; a program needn't handle non-finite values. No bound on the sum of `pair_side` on one device may be relied on, other than what follows from the above.
Results may differ from a plain program's by a relative error of at most 0.017.
Values may be sent and summed in bfloat16 or wider, within the bound.
No kernel may reach another device: no remote copies, remote signals or barrier semaphores. Data moves between devices by JAX's collectives and lax.ppermute only.
A program may use at most 64 MiB of HBM per device.

v0:
```python
import jax
import jax.numpy as jnp
from jax import lax
from jax.sharding import PartitionSpec as P

CAP = 128
SEQS = 4


def shifted(block, axis, distance):
    devices = range(lax.axis_size(axis))
    route = [((i - distance) % len(devices), i) for i in devices]
    return lax.ppermute(block, axis, route)


def token_weights(counts, seg_ids, pair_side):
    positions = jnp.arange(seg_ids.shape[-1], dtype=jnp.int32)
    valid_rows = positions[None, None, :] < counts[:, :, None]
    member = (seg_ids[..., None] == jnp.arange(SEQS, dtype=jnp.int32)) & valid_rows[..., None]
    member_f = member.astype(jnp.float32)
    length = jnp.sum(member_f, axis=2)
    half_span = jnp.float32(CAP) / jnp.float32(SEQS)
    seq_weight = (2.0 * pair_side.astype(jnp.float32) - 1.0) * half_span / (length + half_span)
    return jnp.sum(member_f * seq_weight[:, :, None, :], axis=3)


def contract_rows(left, right):
    return lax.dot_general(
        left, right, (((0,), (0,)), ((), ())), preferred_element_type=jnp.float32
    )


def contract_cols(left, right):
    return lax.dot_general(
        left, right, (((1,), (1,)), ((), ())), preferred_element_type=jnp.float32
    )


def backward_core(tok_rows, grad_rows, w_gate, w_up, w_down):
    gate_pre = jnp.dot(tok_rows, w_gate, preferred_element_type=jnp.float32)
    up_pre = jnp.dot(tok_rows, w_up, preferred_element_type=jnp.float32)
    sigmoid_gate = jax.nn.sigmoid(gate_pre)
    gate_act = gate_pre * sigmoid_gate
    hidden = (gate_act * up_pre).astype(jnp.bfloat16)
    d_hidden = jnp.dot(grad_rows, w_down, preferred_element_type=jnp.float32)
    d_gate = (d_hidden * up_pre * sigmoid_gate * (1.0 + gate_pre * (1.0 - sigmoid_gate))).astype(
        jnp.bfloat16
    )
    d_up = (d_hidden * gate_act).astype(jnp.bfloat16)
    grad_tok = (contract_cols(d_gate, w_gate) + contract_cols(d_up, w_up)).astype(jnp.bfloat16)
    grad_gate = contract_rows(tok_rows, d_gate)
    grad_up = contract_rows(tok_rows, d_up)
    grad_down = contract_rows(grad_rows, hidden)
    summed = lax.psum_scatter(
        jnp.stack([grad_gate, grad_up, grad_down]).astype(jnp.bfloat16),
        "dp",
        scatter_dimension=1,
        tiled=True,
    ).astype(jnp.float32)
    return (grad_tok, summed / lax.axis_size("dp"))


def shards(tokens, cotangent, gate_weight, up_weight, down_weight, counts, seg_ids, pair_side):
    weights = token_weights(counts, seg_ids, pair_side)
    upstream = (cotangent.astype(jnp.float32) * weights[..., None]).astype(jnp.bfloat16)
    width = tokens.shape[-1]
    tok_rows = tokens.reshape(-1, width)
    grad_rows = upstream.reshape(-1, width)
    moved_rows, moved_grads = shifted((tok_rows, grad_rows), "blk", 1)
    grad_moved, panel_grads = backward_core(
        moved_rows, moved_grads, gate_weight, up_weight, down_weight
    )
    grad_tok = shifted(grad_moved, "blk", -1)
    return (grad_tok.reshape(tokens.shape), panel_grads)


def solution(mesh):
    placed = (
        P("dp", "blk", None, None),
        P("dp", "blk", None, None),
        P(None, "blk"),
        P(None, "blk"),
        P(None, "blk"),
        P("dp", "blk"),
        P("dp", "blk", None),
        P("dp", "blk", None),
    )
    return jax.shard_map(
        shards,
        mesh=mesh,
        in_specs=placed,
        out_specs=(P("dp", "blk", None, None), P(None, "dp", "blk")),
        check_vma=False,
    )
```

profile of v0, /device:TPU:16, one launch (start us, length us, event | category | flops | bytes accessed | tf_op | source)
XLA Modules:
  0.0 287.8 jit_solution(8724467029875597010)
XLA Ops:
  7.2 0.0 copy-start
  7.2 0.0 reduce-scatter.2.cloned.1.call-start
  7.2 2.1 collective-permute-start.1
  9.9 0.8 convert_reduce_fusion
  10.7 0.7 fusion.8
  11.4 0.7 select_reduce_fusion
  12.1 1.5 fusion.4
  13.6 3.5 %collective-permute-start = (bf16[128,4096]{1,0:T(8,128)(2,1)S(1)}, bf16[128,4096]{1,0:T(8,128)(2,1)S(1)}, u32[]{:S(2)}, u32[]{:S(2)}) collective-permute-start(bf16[128,4096]{1,0:T(8,128)(2,1)S(1)} %fusion.4), channel_id=1, source_target_pairs={{47,0},{0,1},{1,2},{2,3},{3,4},{4,5},{5,6},{6,7},{7,8},{8,9},{9,10... | collective-permute-start | bytes 3145736 | tf_op jit(solution)/shard_map/ppermute | solution.py:13
  17.1 17.9 %collective-permute-done.1 = bf16[128,4096]{1,0:T(8,128)(2,1)S(1)} collective-permute-done((bf16[128,4096]{1,0:T(8,128)(2,1)}, bf16[128,4096]{1,0:T(8,128)(2,1)S(1)}, u32[]{:S(2)}, u32[]{:S(2)}) %collective-permute-start.1) | collective-permute-done | bytes 1048608 | tf_op jit(solution)/shard_map/ppermute | solution.py:13
  35.0 2.6 fusion.10
  37.6 0.0 copy-done
  37.6 0.9 fusion.11
  38.6 0.0 copy-start.2
  38.6 7.7 %collective-permute-done = bf16[128,4096]{1,0:T(8,128)(2,1)S(1)} collective-permute-done((bf16[128,4096]{1,0:T(8,128)(2,1)S(1)}, bf16[128,4096]{1,0:T(8,128)(2,1)S(1)}, u32[]{:S(2)}, u32[]{:S(2)}) %collective-permute-start) | collective-permute-done | bytes 1048608 | tf_op jit(solution)/shard_map/ppermute | solution.py:13
  46.2 0.8 fusion.2
  47.1 0.0 copy-done.2
  47.1 0.9 multiply_convert_fusion.2
  48.0 0.8 fusion
  48.8 0.8 fusion.1
  49.7 3.7 %pad_maximum_fusion = bf16[3,4096,308]{1,2,0:T(8,128)(2,1)} fusion(bf16[1,4096,308]{1,2,0:T(8,128)(2,1)S(1)} %fusion.2, bf16[1,4096,308]{1,2,0:T(8,128)(2,1)S(1)} %fusion.1, bf16[1,4096,308]{1,2,0:T(8,128)(2,1)S(1)} %fusion), kind=kLoop, calls=%fused_computation | loop fusion | flops 7569408 | bytes 15138816 | tf_op jit(solution)/shard_map/stack | solution.py:55
  53.3 0.0 reduce-scatter.2.cloned.1.call-update
  53.3 0.0 copy-start.1
  53.4 0.8 fusion.12
  54.1 0.9 copy-done.1
  55.1 0.9 fusion.3
  55.9 1.9 collective-permute-start.2
  57.9 12.3 %collective-permute-done.2 = bf16[128,4096]{1,0:T(8,128)(2,1)} collective-permute-done((bf16[128,4096]{1,0:T(8,128)(2,1)S(1)}, bf16[128,4096]{1,0:T(8,128)(2,1)}, u32[]{:S(2)}, u32[]{:S(2)}) %collective-permute-start.2) | collective-permute-done | bytes 1048608 | tf_op jit(solution)/shard_map/ppermute | solution.py:13
  70.2 206.5 %reduce-scatter.2.cloned.1.call-done = bf16[3,256,308]{1,2,0:T(8,128)(2,1)} async-done(((bf16[3,4096,308]{1,2,0:T(8,128)(2,1)}), bf16[3,256,308]{1,2,0:T(8,128)(2,1)}) %reduce-scatter.2.cloned.1.call-update) | async-done | bytes 473104 | tf_op jit(solution)/shard_map/reduce_scatter | solution.py:54
  276.6 2.0 convert_multiply_fusion
  278.7 2.3 copy.12
  (1 shorter events, 0.0 us)
Async XLA Ops:
  7.2 30.5 %copy-start = (bf16[4096,308]{0,1:T(8,128)(2,1)S(1)}, bf16[4096,308]{0,1:T(8,128)(2,1)}, u32[]{:S(2)}) copy-start(bf16[4096,308]{0,1:T(8,128)(2,1)} %param.10) | copy-start | bytes 7569412
  7.2 269.4 %reduce-scatter.2.cloned.1.call-start = ((), (), s32[]{:S(2)}) async-start(), calls=%async_computation.1 | async-start | bytes 8146944 | tf_op jit(solution)/shard_map/reduce_scatter | solution.py:54
  7.2 27.8 %collective-permute-start.1 = (bf16[128,4096]{1,0:T(8,128)(2,1)}, bf16[128,4096]{1,0:T(8,128)(2,1)S(1)}, u32[]{:S(2)}, u32[]{:S(2)}) collective-permute-start(bf16[128,4096]{1,0:T(8,128)(2,1)} %bitcast.40), channel_id=1, source_target_pairs={{47,0},{0,1},{1,2},{2,3},{3,4},{4,5},{5,6},{6,7},{7,8},{8,9},{9,10... | collective-permute-start | bytes 3145736 | tf_op jit(solution)/shard_map/ppermute | solution.py:13
  13.6 32.6 %collective-permute-start = (bf16[128,4096]{1,0:T(8,128)(2,1)S(1)}, bf16[128,4096]{1,0:T(8,128)(2,1)S(1)}, u32[]{:S(2)}, u32[]{:S(2)}) collective-permute-start(bf16[128,4096]{1,0:T(8,128)(2,1)S(1)} %fusion.4), channel_id=1, source_target_pairs={{47,0},{0,1},{1,2},{2,3},{3,4},{4,5},{5,6},{6,7},{7,8},{8,9},{9,10... | collective-permute-start | bytes 3145736 | tf_op jit(solution)/shard_map/ppermute | solution.py:13
  38.6 8.5 %copy-start.2 = (bf16[4096,308]{0,1:T(8,128)(2,1)S(1)}, bf16[4096,308]{0,1:T(8,128)(2,1)}, u32[]{:S(2)}) copy-start(bf16[4096,308]{0,1:T(8,128)(2,1)} %param.12) | copy-start | bytes 7569412
  53.3 1.7 copy-start.1
  55.9 14.2 %collective-permute-start.2 = (bf16[128,4096]{1,0:T(8,128)(2,1)S(1)}, bf16[128,4096]{1,0:T(8,128)(2,1)}, u32[]{:S(2)}, u32[]{:S(2)}) collective-permute-start(bf16[128,4096]{1,0:T(8,128)(2,1)S(1)} %fusion.3), channel_id=1, source_target_pairs={{1,0},{2,1},{3,2},{4,3},{5,4},{6,5},{7,6},{8,7},{9,8},{10,9},{11,1... | collective-permute-start | bytes 3145736 | tf_op jit(solution)/shard_map/ppermute | solution.py:13
Sparse Core Ops, SparseCore 0:
  53.5 223.1 reduce-scatter.1
where the time goes:
time: 288 us
  waiting for transfers between devices  244 us (85%)
  between operations  14.8 us (5%)
  other arithmetic  9.35 us (3%)
  matrix products  8.59 us (3%)
  starting transfers between devices  7.51 us (3%)
  local copies, waits for them, and re-layouts  3.22 us (1%)
    reduce_scatter x1, waiting for transfers between devices, backward_core(): lax.psum_scatter(jnp.stack([grad_gate, grad_up, grad_down]).astype(jnp.bf...  206 us
    ppermute x3, waiting for transfers between devices, shifted(): return lax.ppermute(block, axis, route)  37.8 us
    ppermute x3, starting transfers between devices, shifted(): return lax.ppermute(block, axis, route)  7.48 us
  transfers between devices with their start and end apart: 4, of which 4 were waited for; matrix products, arithmetic and copies ran while one was open for 3% of the time, Pallas kernels for 0%

commit v1 on v0

--- a/solution.py
+++ b/solution.py
@@ -51,13 +51,39 @@
     grad_gate = contract_rows(tok_rows, d_gate)
     grad_up = contract_rows(tok_rows, d_up)
     grad_down = contract_rows(grad_rows, hidden)
-    summed = lax.psum_scatter(
-        jnp.stack([grad_gate, grad_up, grad_down]).astype(jnp.bfloat16),
-        "dp",
-        scatter_dimension=1,
-        tiled=True,
-    ).astype(jnp.float32)
+    summed = reduce_over_dp(jnp.stack([grad_gate, grad_up, grad_down]))
     return (grad_tok, summed / lax.axis_size("dp"))
+
+
+def reduce_over_dp(parts):
+    n = lax.axis_size("dp")
+    nx = 2
+    ny = n // nx
+    index = lax.axis_index("dp")
+    xh = index // ny
+    y = index % ny
+    three, width, cols = parts.shape
+    half = width // n // 2
+    view = parts.reshape(three, nx, ny, 2, half, cols)
+
+    def chunk(c, h):
+        return lax.dynamic_index_in_dim(view[:, :, :, h], c, axis=2, keepdims=False)
+
+    fwd = [(a * ny + b, a * ny + (b + 1) % ny) for a in range(nx) for b in range(ny)]
+    bwd = [(a * ny + b, a * ny + (b - 1) % ny) for a in range(nx) for b in range(ny)]
+    acc_f = chunk((y + ny - 1) % ny, 0)
+    acc_b = chunk((y + 1) % ny, 1)
+    for s in range(ny - 1):
+        recv_f = lax.ppermute(acc_f.astype(jnp.bfloat16), "dp", fwd)
+        recv_b = lax.ppermute(acc_b.astype(jnp.bfloat16), "dp", bwd)
+        acc_f = recv_f.astype(jnp.float32) + chunk((y + 2 * ny - 2 - s) % ny, 0)
+        acc_b = recv_b.astype(jnp.float32) + chunk((y + 2 + s) % ny, 1)
+    acc = jnp.stack([acc_f, acc_b], axis=2)
+    mine = lax.dynamic_index_in_dim(acc, xh, axis=1, keepdims=False)
+    other = lax.dynamic_index_in_dim(acc, 1 - xh, axis=1, keepdims=False)
+    across = [(a * ny + b, (1 - a) * ny + b) for a in range(nx) for b in range(ny)]
+    got = lax.ppermute(other.astype(jnp.bfloat16), "dp", across)
+    return (mine + got.astype(jnp.float32)).reshape(three, 2 * half, cols)
 
 
 def shards(tokens, cotangent, gate_weight, up_weight, down_weight, counts, seg_ids, pair_side):

time: 288 us -> 254 us (0.88)
  the two profiles are of different devices: /device:TPU:16 before, /device:TPU:194 now
where the time goes in v1:
time: 254 us; the launch traced here: 249 us
  local copies, waits for them, and re-layouts  86 us (34%)
  starting transfers between devices  67.8 us (27%)
  waiting for transfers between devices  56.6 us (22%)
  matrix products  22.6 us (9%)
  other arithmetic  14 us (6%)
    ppermute x7, starting transfers between devices, reduce_over_dp(): recv_b = lax.ppermute(acc_b.astype(jnp.bfloat16), 'dp', bwd)  38.7 us
    ppermute x7, waiting for transfers between devices, reduce_over_dp(): recv_b = lax.ppermute(acc_b.astype(jnp.bfloat16), 'dp', bwd)  35.3 us
    another operation x4, local copies, waits for them, and re-layouts, backward_core(): summed = reduce_over_dp(jnp.stack([grad_gate, grad_up, grad_down]))  29.2 us
    slice x1, local copies, waits for them, and re-layouts, chunk(): return lax.dynamic_index_in_dim(view[:, :, :, h], c, axis=2, keepdims=False)  18.8 us
    unnamed x21, local copies, waits for them, and re-layouts  18.1 us
    ppermute x7, starting transfers between devices, reduce_over_dp(): recv_f = lax.ppermute(acc_f.astype(jnp.bfloat16), 'dp', fwd)  13.6 us
    dot_general x3, matrix products, contract_rows(): lax.dot_general(left, right, (((0,), (0,)), ((), ())), preferred_element_...  12.9 us
    dynamic_slice x1, local copies, waits for them, and re-layouts, chunk(): return lax.dynamic_index_in_dim(view[:, :, :, h], c, axis=2, keepdims=False)  12.1 us
  transfers between devices with their start and end apart: 18, of which 10 were waited for; matrix products, arithmetic and copies ran while one was open for 15% of the time, Pallas kernels for 0%

profile of v1, /device:TPU:194, one launch (start us, length us, event | category | flops | bytes accessed | tf_op | source)
XLA Modules:
  0.0 249.2 jit_solution(1871677162412587020)
XLA Ops:
  5.5 2.5 fusion.1
  8.0 5.6 %collective-permute-start = (bf16[128,4096]{1,0:T(8,128)(2,1)}, bf16[128,4096]{1,0:T(8,128)(2,1)}, u32[]{:S(2)}, u32[]{:S(2)}) collective-permute-start(bf16[128,4096]{1,0:T(8,128)(2,1)} %fusion.1), channel_id=1, source_target_pairs={{47,0},{0,1},{1,2},{2,3},{3,4},{4,5},{5,6},{6,7},{7,8},{8,9},{9,10... | collective-permute-start | bytes 3145736 | tf_op jit(solution)/shard_map/ppermute | solution.py:13
  13.8 3.4 %collective-permute-done.1 = bf16[128,4096]{1,0:T(8,128)(2,1)} collective-permute-done((bf16[128,4096]{1,0:T(8,128)(2,1)}, bf16[128,4096]{1,0:T(8,128)(2,1)}, u32[]{:S(2)}, u32[]{:S(2)}) %collective-permute-start.1) | collective-permute-done | bytes 1048608 | tf_op jit(solution)/shard_map/ppermute | solution.py:13
  17.2 2.9 %fusion.27 = f32[128,308]{0,1:T(8,128)S(1)} fusion(bf16[128,4096]{1,0:T(8,128)(2,1)} %collective-permute-done.1, bf16[4096,308]{0,1:T(8,128)(2,1)} %param.11), kind=kOutput, calls=%fused_computation.80 | convolution fusion | flops 322961408 | bytes 3729408 | tf_op jit(solution)/shard_map/dot_general | solution.py:41
  22.2 6.2 %collective-permute-done = bf16[128,4096]{1,0:T(8,128)(2,1)} collective-permute-done((bf16[128,4096]{1,0:T(8,128)(2,1)}, bf16[128,4096]{1,0:T(8,128)(2,1)}, u32[]{:S(2)}, u32[]{:S(2)}) %collective-permute-start) | collective-permute-done | bytes 1048608 | tf_op jit(solution)/shard_map/ppermute | solution.py:13
  31.2 4.3 %convolution_bitcast_fusion.1 = f32[4096,308]{0,1:T(8,128)} fusion(bf16[128,308]{0,1:T(8,128)(2,1)S(1)} %get-tuple-element.19, bf16[128,4096]{1,0:T(8,128)(2,1)} %collective-permute-done.1), kind=kOutput, calls=%fused_computation.1 | convolution fusion | flops 322961408 | bytes 6173696 | tf_op jit(solution)/shard_map/dot_general | solution.py:28
  35.5 8.2 %stack.21 = f32[1,2,8,2,128,308]{4,3,2,1,5,0:T(2,128)} reshape(f32[4096,308]{0,1:T(8,128)} %convolution_bitcast_fusion.1) | data formatting | bytes 10092544 | tf_op jit(solution)/shard_map/stack | solution.py:54
  43.7 7.0 %constant_dynamic-update-slice_fusion.2 = f32[3,2,8,2,128,308]{4,3,2,1,5,0:T(2,128)} fusion(f32[1,2,8,2,128,308]{4,3,2,1,5,0:T(2,128)} %stack.21), kind=kLoop, calls=%fused_computation.56 | loop fusion | bytes 10092544
  50.7 4.3 %convolution_bitcast_fusion = f32[4096,308]{0,1:T(8,128)} fusion(bf16[128,308]{0,1:T(8,128)(2,1)S(1)} %get-tuple-element.18, bf16[128,4096]{1,0:T(8,128)(2,1)} %collective-permute-done.1), kind=kOutput, calls=%fused_computation | convolution fusion | flops 322961408 | bytes 6173696 | tf_op jit(solution)/shard_map/dot_general | solution.py:28
  55.0 8.0 %stack.22 = f32[1,2,8,2,128,308]{4,3,2,1,5,0:T(2,128)} reshape(f32[4096,308]{0,1:T(8,128)} %convolution_bitcast_fusion) | data formatting | bytes 10092544 | tf_op jit(solution)/shard_map/stack | solution.py:54
  62.9 4.3 %fusion.21 = f32[4096,308]{0,1:T(8,128)} fusion(bf16[128,4096]{1,0:T(8,128)(2,1)} %collective-permute-done, f32[128,308]{0,1:T(8,128)S(1)} %fusion.27, f32[128,308]{0,1:T(8,128)S(1)} %fusion.28), kind=kOutput, calls=%fused_computation.53 | convolution fusion | flops 323197952 | bytes 6410240 | tf_op jit(solution)/shard_map/dot_general | solution.py:28
  67.2 8.4 %stack.23 = f32[1,2,8,2,128,308]{4,3,2,1,5,0:T(2,128)} reshape(f32[4096,308]{0,1:T(8,128)} %fusion.21) | data formatting | bytes 10092544 | tf_op jit(solution)/shard_map/stack | solution.py:54
  75.7 7.3 %constant_dynamic-update-slice_fusion.1 = f32[3,2,8,2,128,308]{4,3,2,1,5,0:T(2,128)} fusion(f32[3,2,8,2,128,308]{4,3,2,1,5,0:T(2,128)} %constant_dynamic-update-slice_fusion.2, f32[1,2,8,2,128,308]{4,3,2,1,5,0:T(2,128)} %stack.22), kind=kLoop, calls=%fused_computation.55 | loop fusion | bytes 10092544
  82.9 4.7 %constant_dynamic-update-slice_fusion = f32[3,2,8,2,128,308]{4,3,2,1,5,0:T(2,128)} fusion(f32[3,2,8,2,128,308]{4,3,2,1,5,0:T(2,128)} %constant_dynamic-update-slice_fusion.1, f32[1,2,8,2,128,308]{4,3,2,1,5,0:T(2,128)S(1)} %copy-done.1), kind=kLoop, calls=%fused_computation.54 | loop fusion | bytes 10092544 | tf_op jit(solution)/shard_map/stack | solution.py:54
  87.6 18.8 %fusion.26 = (f32[3,2,8,1,128,308]{4,3,2,1,5,0:T(1,128)S(1)}, f32[3,2,8,1,128,308]{4,3,2,1,5,0:T(1,128)}) fusion(f32[3,2,8,2,128,308]{4,3,2,1,5,0:T(2,128)} %constant_dynamic-update-slice_fusion), kind=kLoop, calls=%fused_computation.79 | loop fusion | bytes 30277632 | tf_op jit(solution)/shard_map/slice | solution.py:70
  107.2 5.4 %collective-permute-start.10 = (bf16[3,2,128,308]{2,3,1,0:T(8,128)(2,1)S(1)}, bf16[3,2,128,308]{2,3,1,0:T(8,128)(2,1)S(1)}, u32[]{:S(2)}, u32[]{:S(2)}) collective-permute-start(bf16[3,2,128,308]{2,3,1,0:T(8,128)(2,1)S(1)} %bitcast.114), channel_id=1, source_target_pairs={{0,336},{48,0},{96,48},{144,96},{192,144},{240,192},{288,240},{336... | collective-permute-start | bytes 1419272 | tf_op jit(solution)/shard_map/ppermute | solution.py:78
  116.5 12.1 %constant_dynamic-slice_fusion.6 = (f32[3,2,1,1,128,308]{4,3,2,1,5,0:T(1,128)S(1)}, f32[3,2,1,1,128,308]{4,3,2,1,5,0:T(1,128)S(1)}, f32[3,2,1,1,128,308]{4,3,2,1...) fusion(f32[3,2,8,1,128,308]{4,3,2,1,5,0:T(1,128)S(1)} %get-tupl, ...), kind=kLoop, calls=%fused_computation.63 | loop fusion | bytes 26492980 | tf_op jit(solution)/shard_map/jit(dynamic_index_in_dim)/dynamic_slice | solution.py:70
  128.7 5.2 %collective-permute-start.11 = (bf16[3,2,128,308]{2,3,1,0:T(8,128)(2,1)S(1)}, bf16[3,2,128,308]{2,3,1,0:T(8,128)(2,1)S(1)}, u32[]{:S(2)}, u32[]{:S(2)}) collective-permute-start(bf16[3,2,128,308]{2,3,1,0:T(8,128)(2,1)S(1)} %fusion.9), channel_id=1, source_target_pairs={{0,336},{48,0},{96,48},{144,96},{192,144},{240,192},{288,240},{336... | collective-permute-start | bytes 1419272 | tf_op jit(solution)/shard_map/ppermute | solution.py:78
  135.9 8.9 %collective-permute-done.11 = bf16[3,2,128,308]{2,3,1,0:T(8,128)(2,1)S(1)} collective-permute-done((bf16[3,2,128,308]{2,3,1,0:T(8,128)(2,1)S(1)}, bf16[3,2,128,308]{2,3,1,0:T(8,128)(2,1)S(1)}, u32[]{:S(2)}, u32[]{:S(2)}) %collective-permute-start.11) | collective-permute-done | bytes 473120 | tf_op jit(solution)/shard_map/ppermute | solution.py:78
  145.0 5.6 %collective-permute-start.12 = (bf16[3,2,128,308]{2,3,1,0:T(8,128)(2,1)S(1)}, bf16[3,2,128,308]{2,3,1,0:T(8,128)(2,1)S(1)}, u32[]{:S(2)}, u32[]{:S(2)}) collective-permute-start(bf16[3,2,128,308]{2,3,1,0:T(8,128)(2,1)S(1)} %fusion.8), channel_id=1, source_target_pairs={{0,336},{48,0},{96,48},{144,96},{192,144},{240,192},{288,240},{336... | collective-permute-start | bytes 1419272 | tf_op jit(solution)/shard_map/ppermute | solution.py:78
  152.6 8.1 %collective-permute-done.12 = bf16[3,2,128,308]{2,3,1,0:T(8,128)(2,1)S(1)} collective-permute-done((bf16[3,2,128,308]{2,3,1,0:T(8,128)(2,1)S(1)}, bf16[3,2,128,308]{2,3,1,0:T(8,128)(2,1)S(1)}, u32[]{:S(2)}, u32[]{:S(2)}) %collective-permute-start.12) | collective-permute-done | bytes 473120 | tf_op jit(solution)/shard_map/ppermute | solution.py:78
  160.8 5.7 %collective-permute-start.13 = (bf16[3,2,128,308]{2,3,1,0:T(8,128)(2,1)S(1)}, bf16[3,2,128,308]{2,3,1,0:T(8,128)(2,1)S(1)}, u32[]{:S(2)}, u32[]{:S(2)}) collective-permute-start(bf16[3,2,128,308]{2,3,1,0:T(8,128)(2,1)S(1)} %fusion.7), channel_id=1, source_target_pairs={{0,336},{48,0},{96,48},{144,96},{192,144},{240,192},{288,240},{336... | collective-permute-start | bytes 1419272 | tf_op jit(solution)/shard_map/ppermute | solution.py:78
  168.6 7.2 %collective-permute-done.13 = bf16[3,2,128,308]{2,3,1,0:T(8,128)(2,1)S(1)} collective-permute-done((bf16[3,2,128,308]{2,3,1,0:T(8,128)(2,1)S(1)}, bf16[3,2,128,308]{2,3,1,0:T(8,128)(2,1)S(1)}, u32[]{:S(2)}, u32[]{:S(2)}) %collective-permute-start.13) | collective-permute-done | bytes 473120 | tf_op jit(solution)/shard_map/ppermute | solution.py:78
  175.9 5.6 %collective-permute-start.14 = (bf16[3,2,128,308]{2,3,1,0:T(8,128)(2,1)S(1)}, bf16[3,2,128,308]{2,3,1,0:T(8,128)(2,1)S(1)}, u32[]{:S(2)}, u32[]{:S(2)}) collective-permute-start(bf16[3,2,128,308]{2,3,1,0:T(8,128)(2,1)S(1)} %fusion.6), channel_id=1, source_target_pairs={{0,336},{48,0},{96,48},{144,96},{192,144},{240,192},{288,240},{336... | collective-permute-start | bytes 1419272 | tf_op jit(solution)/shard_map/ppermute | solution.py:78
  183.6 6.4 %collective-permute-done.14 = bf16[3,2,128,308]{2,3,1,0:T(8,128)(2,1)S(1)} collective-permute-done((bf16[3,2,128,308]{2,3,1,0:T(8,128)(2,1)S(1)}, bf16[3,2,128,308]{2,3,1,0:T(8,128)(2,1)S(1)}, u32[]{:S(2)}, u32[]{:S(2)}) %collective-permute-start.14) | collective-permute-done | bytes 473120 | tf_op jit(solution)/shard_map/ppermute | solution.py:78
  190.1 5.6 %collective-permute-start.15 = (bf16[3,2,128,308]{2,3,1,0:T(8,128)(2,1)S(1)}, bf16[3,2,128,308]{2,3,1,0:T(8,128)(2,1)S(1)}, u32[]{:S(2)}, u32[]{:S(2)}) collective-permute-start(bf16[3,2,128,308]{2,3,1,0:T(8,128)(2,1)S(1)} %fusion.5), channel_id=1, source_target_pairs={{0,336},{48,0},{96,48},{144,96},{192,144},{240,192},{288,240},{336... | collective-permute-start | bytes 1419272 | tf_op jit(solution)/shard_map/ppermute | solution.py:78
  198.7 4.5 %collective-permute-done.15 = bf16[3,2,128,308]{2,3,1,0:T(8,128)(2,1)S(1)} collective-permute-done((bf16[3,2,128,308]{2,3,1,0:T(8,128)(2,1)S(1)}, bf16[3,2,128,308]{2,3,1,0:T(8,128)(2,1)S(1)}, u32[]{:S(2)}, u32[]{:S(2)}) %collective-permute-start.15) | collective-permute-done | bytes 473120 | tf_op jit(solution)/shard_map/ppermute | solution.py:78
  204.2 5.6 %collective-permute-start.16 = (bf16[3,2,128,308]{2,3,1,0:T(8,128)(2,1)}, bf16[3,2,128,308]{2,3,1,0:T(8,128)(2,1)}, u32[]{:S(2)}, u32[]{:S(2)}) collective-permute-start(bf16[3,2,128,308]{2,3,1,0:T(8,128)(2,1)} %fusion.4), channel_id=1, source_target_pairs={{0,336},{48,0},{96,48},{144,96},{192,144},{240,192},{288,240},{336... | collective-permute-start | bytes 1419272 | tf_op jit(solution)/shard_map/ppermute | solution.py:78
  218.9 4.1 %collective-permute-done.9 = bf16[3,2,128,308]{2,3,1,0:T(8,128)(2,1)} collective-permute-done((bf16[3,2,128,308]{2,3,1,0:T(8,128)(2,1)}, bf16[3,2,128,308]{2,3,1,0:T(8,128)(2,1)}, u32[]{:S(2)}, u32[]{:S(2)}) %collective-permute-start.9) | collective-permute-done | bytes 473120 | tf_op jit(solution)/shard_map/ppermute | solution.py:77
  228.0 5.8 %collective-permute-start.17 = (bf16[3,2,128,308]{2,3,1,0:T(8,128)(2,1)}, bf16[3,2,128,308]{2,3,1,0:T(8,128)(2,1)}, u32[]{:S(2)}, u32[]{:S(2)}) collective-permute-start(bf16[3,2,128,308]{2,3,1,0:T(8,128)(2,1)} %bitcast.109), channel_id=1, source_target_pairs={{0,384},{48,432},{96,480},{144,528},{192,576},{240,624},{288,672},... | collective-permute-start | bytes 1419272 | tf_op jit(solution)/shard_map/ppermute | solution.py:85
  235.7 7.6 %collective-permute-done.17 = bf16[3,2,128,308]{2,3,1,0:T(8,128)(2,1)} collective-permute-done((bf16[3,2,128,308]{2,3,1,0:T(8,128)(2,1)}, bf16[3,2,128,308]{2,3,1,0:T(8,128)(2,1)}, u32[]{:S(2)}, u32[]{:S(2)}) %collective-permute-start.17) | collective-permute-done | bytes 473120 | tf_op jit(solution)/shard_map/ppermute | solution.py:85
  246.6 2.3 copy.99
  (70 shorter events, 45.5 us)
Async XLA Ops:
  0.6 19.5 %copy-start = (bf16[4096,308]{0,1:T(8,128)(2,1)S(1)}, bf16[4096,308]{0,1:T(8,128)(2,1)}, u32[]{:S(2)}) copy-start(bf16[4096,308]{0,1:T(8,128)(2,1)} %param.10) | copy-start | bytes 7569412
  0.6 16.6 %collective-permute-start.1 = (bf16[128,4096]{1,0:T(8,128)(2,1)}, bf16[128,4096]{1,0:T(8,128)(2,1)}, u32[]{:S(2)}, u32[]{:S(2)}) collective-permute-start(bf16[128,4096]{1,0:T(8,128)(2,1)} %bitcast.117), channel_id=1, source_target_pairs={{47,0},{0,1},{1,2},{2,3},{3,4},{4,5},{5,6},{6,7},{7,8},{8,9},{9,10... | collective-permute-start | bytes 3145736 | tf_op jit(solution)/shard_map/ppermute | solution.py:13
  8.0 20.5 %collective-permute-start = (bf16[128,4096]{1,0:T(8,128)(2,1)}, bf16[128,4096]{1,0:T(8,128)(2,1)}, u32[]{:S(2)}, u32[]{:S(2)}) collective-permute-start(bf16[128,4096]{1,0:T(8,128)(2,1)} %fusion.1), channel_id=1, source_target_pairs={{47,0},{0,1},{1,2},{2,3},{3,4},{4,5},{5,6},{6,7},{7,8},{8,9},{9,10... | collective-permute-start | bytes 3145736 | tf_op jit(solution)/shard_map/ppermute | solution.py:13
  13.8 14.6 %copy-start.8 = (bf16[4096,308]{0,1:T(8,128)(2,1)S(1)}, bf16[4096,308]{0,1:T(8,128)(2,1)}, u32[]{:S(2)}) copy-start(bf16[4096,308]{0,1:T(8,128)(2,1)} %param.12) | copy-start | bytes 7569412
  30.6 0.6 copy-start.6
  30.6 20.1 %copy-start.4 = (bf16[128,308]{0,1:T(8,128)(2,1)}, bf16[128,308]{0,1:T(8,128)(2,1)S(1)}, u32[]{:S(2)}) copy-start(bf16[128,308]{0,1:T(8,128)(2,1)S(1)} %get-tuple-element.18) | copy-start | bytes 236548
  75.7 7.3 %copy-start.1 = (f32[1,2,8,2,128,308]{4,3,2,1,5,0:T(2,128)S(1)}, f32[1,2,8,2,128,308]{4,3,2,1,5,0:T(2,128)}, u32[]{:S(2)}) copy-start(f32[1,2,8,2,128,308]{4,3,2,1,5,0:T(2,128)} %stack.23) | copy-start | bytes 15138820
  107.2 21.4 %collective-permute-start.10 = (bf16[3,2,128,308]{2,3,1,0:T(8,128)(2,1)S(1)}, bf16[3,2,128,308]{2,3,1,0:T(8,128)(2,1)S(1)}, u32[]{:S(2)}, u32[]{:S(2)}) collective-permute-start(bf16[3,2,128,308]{2,3,1,0:T(8,128)(2,1)S(1)} %bitcast.114), channel_id=1, source_target_pairs={{0,336},{48,0},{96,48},{144,96},{192,144},{240,192},{288,240},{336... | collective-permute-start | bytes 1419272 | tf_op jit(solution)/shard_map/ppermute | solution.py:78
  114.5 19.3 %collective-permute-start.3 = (bf16[3,2,128,308]{2,3,1,0:T(8,128)(2,1)S(1)}, bf16[3,2,128,308]{2,3,1,0:T(8,128)(2,1)S(1)}, u32[]{:S(2)}, u32[]{:S(2)}) collective-permute-start(bf16[3,2,128,308]{2,3,1,0:T(8,128)(2,1)S(1)} %bitcast.113), channel_id=1, source_target_pairs={{0,48},{48,96},{96,144},{144,192},{192,240},{240,288},{288,336},{3... | collective-permute-start | bytes 1419272 | tf_op jit(solution)/shard_map/ppermute | solution.py:77
  128.7 16.1 %collective-permute-start.11 = (bf16[3,2,128,308]{2,3,1,0:T(8,128)(2,1)S(1)}, bf16[3,2,128,308]{2,3,1,0:T(8,128)(2,1)S(1)}, u32[]{:S(2)}, u32[]{:S(2)}) collective-permute-start(bf16[3,2,128,308]{2,3,1,0:T(8,128)(2,1)S(1)} %fusion.9), channel_id=1, source_target_pairs={{0,336},{48,0},{96,48},{144,96},{192,144},{240,192},{288,240},{336... | collective-permute-start | bytes 1419272 | tf_op jit(solution)/shard_map/ppermute | solution.py:78
  134.0 16.6 %collective-permute-start.4 = (bf16[3,2,128,308]{2,3,1,0:T(8,128)(2,1)S(1)}, bf16[3,2,128,308]{2,3,1,0:T(8,128)(2,1)S(1)}, u32[]{:S(2)}, u32[]{:S(2)}) collective-permute-start(bf16[3,2,128,308]{2,3,1,0:T(8,128)(2,1)S(1)} %fusion.16), channel_id=1, source_target_pairs={{0,48},{48,96},{96,144},{144,192},{192,240},{240,288},{288,336},{3... | collective-permute-start | bytes 1419272 | tf_op jit(solution)/shard_map/ppermute | solution.py:77
  145.0 15.7 %collective-permute-start.12 = (bf16[3,2,128,308]{2,3,1,0:T(8,128)(2,1)S(1)}, bf16[3,2,128,308]{2,3,1,0:T(8,128)(2,1)S(1)}, u32[]{:S(2)}, u32[]{:S(2)}) collective-permute-start(bf16[3,2,128,308]{2,3,1,0:T(8,128)(2,1)S(1)} %fusion.8), channel_id=1, source_target_pairs={{0,336},{48,0},{96,48},{144,96},{192,144},{240,192},{288,240},{336... | collective-permute-start | bytes 1419272 | tf_op jit(solution)/shard_map/ppermute | solution.py:78
  150.7 15.9 %collective-permute-start.5 = (bf16[3,2,128,308]{2,3,1,0:T(8,128)(2,1)S(1)}, bf16[3,2,128,308]{2,3,1,0:T(8,128)(2,1)S(1)}, u32[]{:S(2)}, u32[]{:S(2)}) collective-permute-start(bf16[3,2,128,308]{2,3,1,0:T(8,128)(2,1)S(1)} %fusion.15), channel_id=1, source_target_pairs={{0,48},{48,96},{96,144},{144,192},{192,240},{240,288},{288,336},{3... | collective-permute-start | bytes 1419272 | tf_op jit(solution)/shard_map/ppermute | solution.py:77
  160.8 37.1 %copy-start.7 = (bf16[128,308]{0,1:T(8,128)(2,1)S(1)}, bf16[128,308]{0,1:T(8,128)(2,1)}, u32[]{:S(2)}) copy-start(bf16[128,308]{0,1:T(8,128)(2,1)} %copy-done.6) | copy-start | bytes 236548
  160.8 15.0 %collective-permute-start.13 = (bf16[3,2,128,308]{2,3,1,0:T(8,128)(2,1)S(1)}, bf16[3,2,128,308]{2,3,1,0:T(8,128)(2,1)S(1)}, u32[]{:S(2)}, u32[]{:S(2)}) collective-permute-start(bf16[3,2,128,308]{2,3,1,0:T(8,128)(2,1)S(1)} %fusion.7), channel_id=1, source_target_pairs={{0,336},{48,0},{96,48},{144,96},{192,144},{240,192},{288,240},{336... | collective-permute-start | bytes 1419272 | tf_op jit(solution)/shard_map/ppermute | solution.py:78
  166.7 14.9 %collective-permute-start.6 = (bf16[3,2,128,308]{2,3,1,0:T(8,128)(2,1)S(1)}, bf16[3,2,128,308]{2,3,1,0:T(8,128)(2,1)S(1)}, u32[]{:S(2)}, u32[]{:S(2)}) collective-permute-start(bf16[3,2,128,308]{2,3,1,0:T(8,128)(2,1)S(1)} %fusion.14), channel_id=1, source_target_pairs={{0,48},{48,96},{96,144},{144,192},{192,240},{240,288},{288,336},{3... | collective-permute-start | bytes 1419272 | tf_op jit(solution)/shard_map/ppermute | solution.py:77
  175.9 14.0 %collective-permute-start.14 = (bf16[3,2,128,308]{2,3,1,0:T(8,128)(2,1)S(1)}, bf16[3,2,128,308]{2,3,1,0:T(8,128)(2,1)S(1)}, u32[]{:S(2)}, u32[]{:S(2)}) collective-permute-start(bf16[3,2,128,308]{2,3,1,0:T(8,128)(2,1)S(1)} %fusion.6), channel_id=1, source_target_pairs={{0,336},{48,0},{96,48},{144,96},{192,144},{240,192},{288,240},{336... | collective-permute-start | bytes 1419272 | tf_op jit(solution)/shard_map/ppermute | solution.py:78
  181.7 14.0 %collective-permute-start.7 = (bf16[3,2,128,308]{2,3,1,0:T(8,128)(2,1)S(1)}, bf16[3,2,128,308]{2,3,1,0:T(8,128)(2,1)S(1)}, u32[]{:S(2)}, u32[]{:S(2)}) collective-permute-start(bf16[3,2,128,308]{2,3,1,0:T(8,128)(2,1)S(1)} %fusion.13), channel_id=1, source_target_pairs={{0,48},{48,96},{96,144},{144,192},{192,240},{240,288},{288,336},{3... | collective-permute-start | bytes 1419272 | tf_op jit(solution)/shard_map/ppermute | solution.py:77
  190.1 13.2 %collective-permute-start.15 = (bf16[3,2,128,308]{2,3,1,0:T(8,128)(2,1)S(1)}, bf16[3,2,128,308]{2,3,1,0:T(8,128)(2,1)S(1)}, u32[]{:S(2)}, u32[]{:S(2)}) collective-permute-start(bf16[3,2,128,308]{2,3,1,0:T(8,128)(2,1)S(1)} %fusion.5), channel_id=1, source_target_pairs={{0,336},{48,0},{96,48},{144,96},{192,144},{240,192},{288,240},{336... | collective-permute-start | bytes 1419272 | tf_op jit(solution)/shard_map/ppermute | solution.py:78
  195.7 16.9 %copy-start.2 = (bf16[4096,308]{0,1:T(8,128)(2,1)S(1)}, bf16[4096,308]{0,1:T(8,128)(2,1)}, u32[]{:S(2)}) copy-start(bf16[4096,308]{0,1:T(8,128)(2,1)} %param.11) | copy-start | bytes 7569412
  195.7 16.9 %copy-start.5 = (bf16[128,308]{0,1:T(8,128)(2,1)S(1)}, bf16[128,308]{0,1:T(8,128)(2,1)}, u32[]{:S(2)}) copy-start(bf16[128,308]{0,1:T(8,128)(2,1)} %copy-done.4) | copy-start | bytes 236548
  195.8 13.9 %collective-permute-start.8 = (bf16[3,2,128,308]{2,3,1,0:T(8,128)(2,1)S(1)}, bf16[3,2,128,308]{2,3,1,0:T(8,128)(2,1)S(1)}, u32[]{:S(2)}, u32[]{:S(2)}) collective-permute-start(bf16[3,2,128,308]{2,3,1,0:T(8,128)(2,1)S(1)} %fusion.12), channel_id=1, source_target_pairs={{0,48},{48,96},{96,144},{144,192},{192,240},{240,288},{288,336},{3... | collective-permute-start | bytes 1419272 | tf_op jit(solution)/shard_map/ppermute | solution.py:77
  204.2 12.6 %collective-permute-start.16 = (bf16[3,2,128,308]{2,3,1,0:T(8,128)(2,1)}, bf16[3,2,128,308]{2,3,1,0:T(8,128)(2,1)}, u32[]{:S(2)}, u32[]{:S(2)}) collective-permute-start(bf16[3,2,128,308]{2,3,1,0:T(8,128)(2,1)} %fusion.4), channel_id=1, source_target_pairs={{0,336},{48,0},{96,48},{144,96},{192,144},{240,192},{288,240},{336... | collective-permute-start | bytes 1419272 | tf_op jit(solution)/shard_map/ppermute | solution.py:78
  210.7 12.3 %collective-permute-start.9 = (bf16[3,2,128,308]{2,3,1,0:T(8,128)(2,1)}, bf16[3,2,128,308]{2,3,1,0:T(8,128)(2,1)}, u32[]{:S(2)}, u32[]{:S(2)}) collective-permute-start(bf16[3,2,128,308]{2,3,1,0:T(8,128)(2,1)} %fusion.11), channel_id=1, source_target_pairs={{0,48},{48,96},{96,144},{144,192},{192,240},{240,288},{288,336},{3... | collective-permute-start | bytes 1419272 | tf_op jit(solution)/shard_map/ppermute | solution.py:77
  214.4 19.4 %collective-permute-start.2 = (bf16[128,4096]{1,0:T(8,128)(2,1)}, bf16[128,4096]{1,0:T(8,128)(2,1)}, u32[]{:S(2)}, u32[]{:S(2)}) collective-permute-start(bf16[128,4096]{1,0:T(8,128)(2,1)} %fusion), channel_id=1, source_target_pairs={{1,0},{2,1},{3,2},{4,3},{5,4},{6,5},{7,6},{8,7},{9,8},{10,9},{11,1... | collective-permute-start | bytes 3145736 | tf_op jit(solution)/shard_map/ppermute | solution.py:13
  225.4 0.9 copy-start.3
  228.0 15.3 %collective-permute-start.17 = (bf16[3,2,128,308]{2,3,1,0:T(8,128)(2,1)}, bf16[3,2,128,308]{2,3,1,0:T(8,128)(2,1)}, u32[]{:S(2)}, u32[]{:S(2)}) collective-permute-start(bf16[3,2,128,308]{2,3,1,0:T(8,128)(2,1)} %bitcast.109), channel_id=1, source_target_pairs={{0,384},{48,432},{96,480},{144,528},{192,576},{240,624},{288,672},... | collective-permute-start | bytes 1419272 | tf_op jit(solution)/shard_map/ppermute | solution.py:85

commit v2 on v1

--- a/solution.py
+++ b/solution.py
@@ -48,26 +48,33 @@
     )
     d_up = (d_hidden * gate_act).astype(jnp.bfloat16)
     grad_tok = (contract_cols(d_gate, w_gate) + contract_cols(d_up, w_up)).astype(jnp.bfloat16)
-    grad_gate = contract_rows(tok_rows, d_gate)
-    grad_up = contract_rows(tok_rows, d_up)
-    grad_down = contract_rows(grad_rows, hidden)
-    summed = reduce_over_dp(jnp.stack([grad_gate, grad_up, grad_down]))
+    summed = reduce_over_dp(
+        tok_rows, grad_rows, jnp.concatenate([d_gate, d_up], axis=1), hidden
+    )
     return (grad_tok, summed / lax.axis_size("dp"))
 
 
-def reduce_over_dp(parts):
+def reduce_over_dp(tok_rows, grad_rows, d_both, hidden):
     n = lax.axis_size("dp")
     nx = 2
     ny = n // nx
     index = lax.axis_index("dp")
     xh = index // ny
     y = index % ny
-    three, width, cols = parts.shape
-    half = width // n // 2
-    view = parts.reshape(three, nx, ny, 2, half, cols)
+    rows, width = tok_rows.shape
+    cols = hidden.shape[1]
+    lane = 128
+    blocks = width // lane // nx
+    tok_view = tok_rows.reshape(rows, nx, blocks, lane)
+    grad_view = grad_rows.reshape(rows, nx, blocks, lane)
 
     def chunk(c, h):
-        return lax.dynamic_index_in_dim(view[:, :, :, h], c, axis=2, keepdims=False)
+        b = c * 2 + h
+        tok_part = lax.dynamic_index_in_dim(tok_view, b, axis=2, keepdims=False)
+        grad_part = lax.dynamic_index_in_dim(grad_view, b, axis=2, keepdims=False)
+        first = contract_rows(d_both, tok_part.reshape(rows, nx * lane))
+        second = contract_rows(hidden, grad_part.reshape(rows, nx * lane))
+        return jnp.concatenate([first, second], axis=0)
 
     fwd = [(a * ny + b, a * ny + (b + 1) % ny) for a in range(nx) for b in range(ny)]
     bwd = [(a * ny + b, a * ny + (b - 1) % ny) for a in range(nx) for b in range(ny)]
@@ -78,12 +85,13 @@
         recv_b = lax.ppermute(acc_b.astype(jnp.bfloat16), "dp", bwd)
         acc_f = recv_f.astype(jnp.float32) + chunk((y + 2 * ny - 2 - s) % ny, 0)
         acc_b = recv_b.astype(jnp.float32) + chunk((y + 2 + s) % ny, 1)
-    acc = jnp.stack([acc_f, acc_b], axis=2)
-    mine = lax.dynamic_index_in_dim(acc, xh, axis=1, keepdims=False)
-    other = lax.dynamic_index_in_dim(acc, 1 - xh, axis=1, keepdims=False)
+    acc = jnp.stack([acc_f, acc_b], axis=1).reshape(-1, 2, nx, lane)
+    mine = lax.dynamic_index_in_dim(acc, xh, axis=2, keepdims=False)
+    other = lax.dynamic_index_in_dim(acc, 1 - xh, axis=2, keepdims=False)
     across = [(a * ny + b, (1 - a) * ny + b) for a in range(nx) for b in range(ny)]
     got = lax.ppermute(other.astype(jnp.bfloat16), "dp", across)
-    return (mine + got.astype(jnp.float32)).reshape(three, 2 * half, cols)
+    total = (mine + got.astype(jnp.float32)).reshape(3, cols, 2 * lane)
+    return jnp.transpose(total, (0, 2, 1))
 
 
 def shards(tokens, cotangent, gate_weight, up_weight, down_weight, counts, seg_ids, pair_side):

time: 254 us -> 187 us (0.74)
  the two profiles are of different devices: /device:TPU:194 before, /device:TPU:4 now
where the time goes in v2:
time: 187 us; the launch traced here: 186 us
  waiting for transfers between devices  74.8 us (40%)
  starting transfers between devices  61.9 us (33%)
  local copies, waits for them, and re-layouts  19.1 us (10%)
  matrix products  18.4 us (10%)
  other arithmetic  9.96 us (5%)
  between operations  2.14 us (1%)
    ppermute x7, starting transfers between devices, reduce_over_dp(): recv_b = lax.ppermute(acc_b.astype(jnp.bfloat16), 'dp', bwd)  38.5 us
    ppermute x7, waiting for transfers between devices, reduce_over_dp(): recv_b = lax.ppermute(acc_b.astype(jnp.bfloat16), 'dp', bwd)  36.1 us
    ppermute x3, waiting for transfers between devices, shifted(): return lax.ppermute(block, axis, route)  24.3 us
    ppermute x7, starting transfers between devices, reduce_over_dp(): recv_f = lax.ppermute(acc_f.astype(jnp.bfloat16), 'dp', fwd)  13.6 us
    dot_general x32, matrix products, contract_rows(): lax.dot_general(left, right, (((0,), (0,)), ((), ())), preferred_element_...  9.65 us
    unnamed x12, local copies, waits for them, and re-layouts  9.51 us
    ppermute x1, waiting for transfers between devices, reduce_over_dp(): got = lax.ppermute(other.astype(jnp.bfloat16), 'dp', across)  9.33 us
    ppermute x3, starting transfers between devices, shifted(): return lax.ppermute(block, axis, route)  7.03 us
  transfers between devices with their start and end apart: 18, of which 10 were waited for; matrix products, arithmetic and copies ran while one was open for 15% of the time, Pallas kernels for 0%

profile of v2, /device:TPU:4, one launch (start us, length us, event | category | flops | bytes accessed | tf_op | source)
XLA Modules:
  0.0 186.3 jit_solution(13290890461318131520)
XLA Ops:
  0.6 2.4 %copy.19 = bf16[1,1,128,4096]{2,3,1,0:T(8,128)(2,1)} copy(bf16[1,1,128,4096]{3,2,1,0:T(8,128)(2,1)} %param.8) | data formatting | bytes 2097152 | tf_op args[0]
  7.8 2.3 %copy.18 = bf16[1,1,128,4096]{2,3,1,0:T(8,128)(2,1)} copy(bf16[1,1,128,4096]{3,2,1,0:T(8,128)(2,1)} %param.9) | data formatting | bytes 2097152 | tf_op args[1]
  10.1 2.4 %fusion.1 = bf16[128,4096]{0,1:T(8,128)(2,1)} fusion(bf16[1,1,128,4096]{2,3,1,0:T(8,128)(2,1)} %copy.18, f32[128]{0:T(128)S(1)} %select_reduce_fusion), kind=kLoop, calls=%fused_computation.7 | loop fusion | flops 1572864 | bytes 2097664 | tf_op jit(solution)/shard_map/reshape | solution.py:102
  12.5 3.2 %collective-permute-start = (bf16[128,4096]{0,1:T(8,128)(2,1)}, bf16[128,4096]{0,1:T(8,128)(2,1)}, u32[]{:S(2)}, u32[]{:S(2)}) collective-permute-start(bf16[128,4096]{0,1:T(8,128)(2,1)} %fusion.1), channel_id=1, source_target_pairs={{47,0},{0,1},{1,2},{2,3},{3,4},{4,5},{5,6},{6,7},{7,8},{8,9},{9,10... | collective-permute-start | bytes 3145736 | tf_op jit(solution)/shard_map/ppermute | solution.py:13
  16.0 14.5 %collective-permute-done.1 = bf16[128,4096]{0,1:T(8,128)(2,1)} collective-permute-done((bf16[128,4096]{0,1:T(8,128)(2,1)}, bf16[128,4096]{0,1:T(8,128)(2,1)}, u32[]{:S(2)}, u32[]{:S(2)}) %collective-permute-start.1) | collective-permute-done | bytes 1048608 | tf_op jit(solution)/shard_map/ppermute | solution.py:13
  32.0 9.8 %collective-permute-done = bf16[128,4096]{0,1:T(8,128)(2,1)} collective-permute-done((bf16[128,4096]{0,1:T(8,128)(2,1)}, bf16[128,4096]{0,1:T(8,128)(2,1)}, u32[]{:S(2)}, u32[]{:S(2)}) %collective-permute-start) | collective-permute-done | bytes 1048608 | tf_op jit(solution)/shard_map/ppermute | solution.py:13
  43.3 2.0 %fusion.33 = f32[128,308]{0,1:T(8,128)S(1)} fusion(bf16[128,4096]{0,1:T(8,128)(2,1)} %collective-permute-done, bf16[4096,308]{0,1:T(8,128)(2,1)S(1)} %copy-done.3), kind=kOutput, calls=%fused_computation.101 | convolution fusion | flops 322961408 | bytes 3729408 | tf_op jit(solution)/shard_map/dot_general | solution.py:45
  45.4 2.0 %fusion.34 = f32[128,308]{0,1:T(8,128)S(1)} fusion(bf16[128,4096]{0,1:T(8,128)(2,1)} %collective-permute-done.1, bf16[4096,308]{0,1:T(8,128)(2,1)S(1)} %copy-done.1), kind=kOutput, calls=%fused_computation.102 | convolution fusion | flops 322961408 | bytes 3729408 | tf_op jit(solution)/shard_map/dot_general | solution.py:40
  47.5 2.1 %multiply_convert_fusion.1 = (bf16[128,308]{0,1:T(8,128)(2,1)S(1)}, bf16[128,308]{0,1:T(8,128)(2,1)S(1)}, bf16[128,308]{0,1:T(8,128)(2,1)S(1)}) fusion(f32[128,308]{0,1:T(8,128)S(1)} %fusion.34, f32[128,308]{0,1:T(8,128)S(1)} %fusion.33, bf16[128,4096]{0,1:T(8,128)(2,1)} %collective-permute-done.1, bf16[4096,308]{0,1:T(8,128)(2,1)S(1)} %copy-done), kind=kOutput, calls=%fused_computation.42 | convolution fusion | flops 323552768 | bytes 4123648 | tf_op jit(solution)/shard_map/dot_general | solution.py:41
  51.0 5.4 %collective-permute-start.10 = (bf16[924,256]{1,0:T(8,128)(2,1)S(1)}, bf16[924,256]{1,0:T(8,128)(2,1)S(1)}, u32[]{:S(2)}, u32[]{:S(2)}) collective-permute-start(bf16[924,256]{1,0:T(8,128)(2,1)S(1)} %pad_maximum_fusion.1), channel_id=1, source_target_pairs={{0,336},{48,0},{96,48},{144,96},{192,144},{240,192},{288,240},{336... | collective-permute-start | bytes 1419272 | tf_op jit(solution)/shard_map/ppermute | solution.py:85
  60.1 1.9 %collective-permute-start.3 = (bf16[924,256]{1,0:T(8,128)(2,1)S(1)}, bf16[924,256]{1,0:T(8,128)(2,1)S(1)}, u32[]{:S(2)}, u32[]{:S(2)}) collective-permute-start(bf16[924,256]{1,0:T(8,128)(2,1)S(1)} %pad_maximum_fusion), channel_id=1, source_target_pairs={{0,48},{48,96},{96,144},{144,192},{192,240},{240,288},{288,336},{3... | collective-permute-start | bytes 1419272 | tf_op jit(solution)/shard_map/ppermute | solution.py:84
  66.8 1.9 %collective-permute-start.2 = (bf16[128,4096]{1,0:T(8,128)(2,1)}, bf16[128,4096]{1,0:T(8,128)(2,1)}, u32[]{:S(2)}, u32[]{:S(2)}) collective-permute-start(bf16[128,4096]{1,0:T(8,128)(2,1)} %fusion), channel_id=1, source_target_pairs={{1,0},{2,1},{3,2},{4,3},{5,4},{6,5},{7,6},{8,7},{9,8},{10,9},{11,1... | collective-permute-start | bytes 3145736 | tf_op jit(solution)/shard_map/ppermute | solution.py:13
  69.4 5.1 %collective-permute-start.11 = (bf16[924,256]{1,0:T(8,128)(2,1)S(1)}, bf16[924,256]{1,0:T(8,128)(2,1)S(1)}, u32[]{:S(2)}, u32[]{:S(2)}) collective-permute-start(bf16[924,256]{1,0:T(8,128)(2,1)S(1)} %fusion.8), channel_id=1, source_target_pairs={{0,336},{48,0},{96,48},{144,96},{192,144},{240,192},{288,240},{336... | collective-permute-start | bytes 1419272 | tf_op jit(solution)/shard_map/ppermute | solution.py:85
  74.7 1.9 %collective-permute-start.4 = (bf16[924,256]{1,0:T(8,128)(2,1)S(1)}, bf16[924,256]{1,0:T(8,128)(2,1)S(1)}, u32[]{:S(2)}, u32[]{:S(2)}) collective-permute-start(bf16[924,256]{1,0:T(8,128)(2,1)S(1)} %fusion.2), channel_id=1, source_target_pairs={{0,48},{48,96},{96,144},{144,192},{192,240},{240,288},{288,336},{3... | collective-permute-start | bytes 1419272 | tf_op jit(solution)/shard_map/ppermute | solution.py:84
  76.8 8.5 %collective-permute-done.11 = bf16[924,256]{1,0:T(8,128)(2,1)S(1)} collective-permute-done((bf16[924,256]{1,0:T(8,128)(2,1)S(1)}, bf16[924,256]{1,0:T(8,128)(2,1)S(1)}, u32[]{:S(2)}, u32[]{:S(2)}) %collective-permute-start.11) | collective-permute-done | bytes 473120 | tf_op jit(solution)/shard_map/ppermute | solution.py:85
  85.4 5.6 %collective-permute-start.12 = (bf16[924,256]{1,0:T(8,128)(2,1)S(1)}, bf16[924,256]{1,0:T(8,128)(2,1)S(1)}, u32[]{:S(2)}, u32[]{:S(2)}) collective-permute-start(bf16[924,256]{1,0:T(8,128)(2,1)S(1)} %fusion.9), channel_id=1, source_target_pairs={{0,336},{48,0},{96,48},{144,96},{192,144},{240,192},{288,240},{336... | collective-permute-start | bytes 1419272 | tf_op jit(solution)/shard_map/ppermute | solution.py:85
  93.4 7.6 %collective-permute-done.12 = bf16[924,256]{1,0:T(8,128)(2,1)S(1)} collective-permute-done((bf16[924,256]{1,0:T(8,128)(2,1)S(1)}, bf16[924,256]{1,0:T(8,128)(2,1)S(1)}, u32[]{:S(2)}, u32[]{:S(2)}) %collective-permute-start.12) | collective-permute-done | bytes 473120 | tf_op jit(solution)/shard_map/ppermute | solution.py:85
  101.1 5.6 %collective-permute-start.13 = (bf16[924,256]{1,0:T(8,128)(2,1)S(1)}, bf16[924,256]{1,0:T(8,128)(2,1)S(1)}, u32[]{:S(2)}, u32[]{:S(2)}) collective-permute-start(bf16[924,256]{1,0:T(8,128)(2,1)S(1)} %fusion.10), channel_id=1, source_target_pairs={{0,336},{48,0},{96,48},{144,96},{192,144},{240,192},{288,240},{336... | collective-permute-start | bytes 1419272 | tf_op jit(solution)/shard_map/ppermute | solution.py:85
  106.9 1.9 %collective-permute-start.6 = (bf16[924,256]{1,0:T(8,128)(2,1)S(1)}, bf16[924,256]{1,0:T(8,128)(2,1)S(1)}, u32[]{:S(2)}, u32[]{:S(2)}) collective-permute-start(bf16[924,256]{1,0:T(8,128)(2,1)S(1)} %fusion.4), channel_id=1, source_target_pairs={{0,48},{48,96},{96,144},{144,192},{192,240},{240,288},{288,336},{3... | collective-permute-start | bytes 1419272 | tf_op jit(solution)/shard_map/ppermute | solution.py:84
  109.0 6.7 %collective-permute-done.13 = bf16[924,256]{1,0:T(8,128)(2,1)S(1)} collective-permute-done((bf16[924,256]{1,0:T(8,128)(2,1)S(1)}, bf16[924,256]{1,0:T(8,128)(2,1)S(1)}, u32[]{:S(2)}, u32[]{:S(2)}) %collective-permute-start.13) | collective-permute-done | bytes 473120 | tf_op jit(solution)/shard_map/ppermute | solution.py:85
  115.9 5.6 %collective-permute-start.14 = (bf16[924,256]{1,0:T(8,128)(2,1)S(1)}, bf16[924,256]{1,0:T(8,128)(2,1)S(1)}, u32[]{:S(2)}, u32[]{:S(2)}) collective-permute-start(bf16[924,256]{1,0:T(8,128)(2,1)S(1)} %fusion.11), channel_id=1, source_target_pairs={{0,336},{48,0},{96,48},{144,96},{192,144},{240,192},{288,240},{336... | collective-permute-start | bytes 1419272 | tf_op jit(solution)/shard_map/ppermute | solution.py:85
  123.8 5.9 %collective-permute-done.14 = bf16[924,256]{1,0:T(8,128)(2,1)S(1)} collective-permute-done((bf16[924,256]{1,0:T(8,128)(2,1)S(1)}, bf16[924,256]{1,0:T(8,128)(2,1)S(1)}, u32[]{:S(2)}, u32[]{:S(2)}) %collective-permute-start.14) | collective-permute-done | bytes 473120 | tf_op jit(solution)/shard_map/ppermute | solution.py:85
  129.8 5.6 %collective-permute-start.15 = (bf16[924,256]{1,0:T(8,128)(2,1)S(1)}, bf16[924,256]{1,0:T(8,128)(2,1)S(1)}, u32[]{:S(2)}, u32[]{:S(2)}) collective-permute-start(bf16[924,256]{1,0:T(8,128)(2,1)S(1)} %fusion.12), channel_id=1, source_target_pairs={{0,336},{48,0},{96,48},{144,96},{192,144},{240,192},{288,240},{336... | collective-permute-start | bytes 1419272 | tf_op jit(solution)/shard_map/ppermute | solution.py:85
  135.6 1.9 %collective-permute-start.8 = (bf16[924,256]{1,0:T(8,128)(2,1)S(1)}, bf16[924,256]{1,0:T(8,128)(2,1)S(1)}, u32[]{:S(2)}, u32[]{:S(2)}) collective-permute-start(bf16[924,256]{1,0:T(8,128)(2,1)S(1)} %fusion.6), channel_id=1, source_target_pairs={{0,48},{48,96},{96,144},{144,192},{192,240},{240,288},{288,336},{3... | collective-permute-start | bytes 1419272 | tf_op jit(solution)/shard_map/ppermute | solution.py:84
  137.8 5.0 %collective-permute-done.15 = bf16[924,256]{1,0:T(8,128)(2,1)S(1)} collective-permute-done((bf16[924,256]{1,0:T(8,128)(2,1)S(1)}, bf16[924,256]{1,0:T(8,128)(2,1)S(1)}, u32[]{:S(2)}, u32[]{:S(2)}) %collective-permute-start.15) | collective-permute-done | bytes 473120 | tf_op jit(solution)/shard_map/ppermute | solution.py:85
  142.9 5.6 %collective-permute-start.16 = (bf16[924,256]{1,0:T(8,128)(2,1)S(1)}, bf16[924,256]{1,0:T(8,128)(2,1)S(1)}, u32[]{:S(2)}, u32[]{:S(2)}) collective-permute-start(bf16[924,256]{1,0:T(8,128)(2,1)S(1)} %fusion.13), channel_id=1, source_target_pairs={{0,336},{48,0},{96,48},{144,96},{192,144},{240,192},{288,240},{336... | collective-permute-start | bytes 1419272 | tf_op jit(solution)/shard_map/ppermute | solution.py:85
  149.5 2.1 %collective-permute-start.9 = (bf16[924,256]{1,0:T(8,128)(2,1)}, bf16[924,256]{1,0:T(8,128)(2,1)}, u32[]{:S(2)}, u32[]{:S(2)}) collective-permute-start(bf16[924,256]{1,0:T(8,128)(2,1)} %fusion.7), channel_id=1, source_target_pairs={{0,48},{48,96},{96,144},{144,192},{192,240},{240,288},{288,336},{3... | collective-permute-start | bytes 1419272 | tf_op jit(solution)/shard_map/ppermute | solution.py:84
  152.5 2.5 %collective-permute-done.16 = bf16[924,256]{1,0:T(8,128)(2,1)S(1)} collective-permute-done((bf16[924,256]{1,0:T(8,128)(2,1)S(1)}, bf16[924,256]{1,0:T(8,128)(2,1)S(1)}, u32[]{:S(2)}, u32[]{:S(2)}) %collective-permute-start.16) | collective-permute-done | bytes 473120 | tf_op jit(solution)/shard_map/ppermute | solution.py:85
  156.5 5.1 %collective-permute-done.9 = bf16[924,256]{1,0:T(8,128)(2,1)} collective-permute-done((bf16[924,256]{1,0:T(8,128)(2,1)}, bf16[924,256]{1,0:T(8,128)(2,1)}, u32[]{:S(2)}, u32[]{:S(2)}) %collective-permute-start.9) | collective-permute-done | bytes 473120 | tf_op jit(solution)/shard_map/ppermute | solution.py:84
  168.3 2.7 %collective-permute-start.17 = (bf16[924,2,128]{2,0,1:T(8,128)(2,1)S(1)}, bf16[924,2,128]{2,0,1:T(8,128)(2,1)S(1)}, u32[]{:S(2)}, u32[]{:S(2)}) collective-permute-start(bf16[924,2,128]{2,0,1:T(8,128)(2,1)S(1)} %fusion.15), channel_id=1, source_target_pairs={{0,384},{48,432},{96,480},{144,528},{192,576},{240,624},{288,672},... | collective-permute-start | bytes 1419272 | tf_op jit(solution)/shard_map/ppermute | solution.py:92
  171.0 9.3 %collective-permute-done.17 = bf16[924,2,128]{2,0,1:T(8,128)(2,1)S(1)} collective-permute-done((bf16[924,2,128]{2,0,1:T(8,128)(2,1)S(1)}, bf16[924,2,128]{2,0,1:T(8,128)(2,1)S(1)}, u32[]{:S(2)}, u32[]{:S(2)}) %collective-permute-start.17) | collective-permute-done | bytes 473120 | tf_op jit(solution)/shard_map/ppermute | solution.py:92
  184.1 2.3 %copy.28 = bf16[1,1,128,4096]{3,2,1,0:T(8,128)(2,1)} copy(bf16[1,1,128,4096]{3,2,1,0:T(8,128)(2,1)} %bitcast.6) | data formatting | bytes 2097152
  (83 shorter events, 37.8 us)
Async XLA Ops:
  0.6 46.8 %copy-start = (bf16[4096,308]{0,1:T(8,128)(2,1)S(1)}, bf16[4096,308]{0,1:T(8,128)(2,1)}, u32[]{:S(2)}) copy-start(bf16[4096,308]{0,1:T(8,128)(2,1)} %param.11) | copy-start | bytes 7569412
  3.1 27.4 %collective-permute-start.1 = (bf16[128,4096]{0,1:T(8,128)(2,1)}, bf16[128,4096]{0,1:T(8,128)(2,1)}, u32[]{:S(2)}, u32[]{:S(2)}) collective-permute-start(bf16[128,4096]{0,1:T(8,128)(2,1)} %bitcast.112), channel_id=1, source_target_pairs={{47,0},{0,1},{1,2},{2,3},{3,4},{4,5},{5,6},{6,7},{7,8},{8,9},{9,10... | collective-permute-start | bytes 3145736 | tf_op jit(solution)/shard_map/ppermute | solution.py:13
  12.5 29.3 %collective-permute-start = (bf16[128,4096]{0,1:T(8,128)(2,1)}, bf16[128,4096]{0,1:T(8,128)(2,1)}, u32[]{:S(2)}, u32[]{:S(2)}) collective-permute-start(bf16[128,4096]{0,1:T(8,128)(2,1)} %fusion.1), channel_id=1, source_target_pairs={{47,0},{0,1},{1,2},{2,3},{3,4},{4,5},{5,6},{6,7},{7,8},{8,9},{9,10... | collective-permute-start | bytes 3145736 | tf_op jit(solution)/shard_map/ppermute | solution.py:13
  16.0 27.4 %copy-start.3 = (bf16[4096,308]{0,1:T(8,128)(2,1)S(1)}, bf16[4096,308]{0,1:T(8,128)(2,1)}, u32[]{:S(2)}) copy-start(bf16[4096,308]{0,1:T(8,128)(2,1)} %param.12) | copy-start | bytes 7569412
  41.7 3.7 %copy-start.1 = (bf16[4096,308]{0,1:T(8,128)(2,1)S(1)}, bf16[4096,308]{0,1:T(8,128)(2,1)}, u32[]{:S(2)}) copy-start(bf16[4096,308]{0,1:T(8,128)(2,1)} %param.10) | copy-start | bytes 7569412
  51.0 18.2 %collective-permute-start.10 = (bf16[924,256]{1,0:T(8,128)(2,1)S(1)}, bf16[924,256]{1,0:T(8,128)(2,1)S(1)}, u32[]{:S(2)}, u32[]{:S(2)}) collective-permute-start(bf16[924,256]{1,0:T(8,128)(2,1)S(1)} %pad_maximum_fusion.1), channel_id=1, source_target_pairs={{0,336},{48,0},{96,48},{144,96},{192,144},{240,192},{288,240},{336... | collective-permute-start | bytes 1419272 | tf_op jit(solution)/shard_map/ppermute | solution.py:85
  60.1 14.4 %collective-permute-start.3 = (bf16[924,256]{1,0:T(8,128)(2,1)S(1)}, bf16[924,256]{1,0:T(8,128)(2,1)S(1)}, u32[]{:S(2)}, u32[]{:S(2)}) collective-permute-start(bf16[924,256]{1,0:T(8,128)(2,1)S(1)} %pad_maximum_fusion), channel_id=1, source_target_pairs={{0,48},{48,96},{96,144},{144,192},{192,240},{240,288},{288,336},{3... | collective-permute-start | bytes 1419272 | tf_op jit(solution)/shard_map/ppermute | solution.py:84
  66.8 104.2 %collective-permute-start.2 = (bf16[128,4096]{1,0:T(8,128)(2,1)}, bf16[128,4096]{1,0:T(8,128)(2,1)}, u32[]{:S(2)}, u32[]{:S(2)}) collective-permute-start(bf16[128,4096]{1,0:T(8,128)(2,1)} %fusion), channel_id=1, source_target_pairs={{1,0},{2,1},{3,2},{4,3},{5,4},{6,5},{7,6},{8,7},{9,8},{10,9},{11,1... | collective-permute-start | bytes 3145736 | tf_op jit(solution)/shard_map/ppermute | solution.py:13
  69.4 15.9 %collective-permute-start.11 = (bf16[924,256]{1,0:T(8,128)(2,1)S(1)}, bf16[924,256]{1,0:T(8,128)(2,1)S(1)}, u32[]{:S(2)}, u32[]{:S(2)}) collective-permute-start(bf16[924,256]{1,0:T(8,128)(2,1)S(1)} %fusion.8), channel_id=1, source_target_pairs={{0,336},{48,0},{96,48},{144,96},{192,144},{240,192},{288,240},{336... | collective-permute-start | bytes 1419272 | tf_op jit(solution)/shard_map/ppermute | solution.py:85
  74.7 16.4 %collective-permute-start.4 = (bf16[924,256]{1,0:T(8,128)(2,1)S(1)}, bf16[924,256]{1,0:T(8,128)(2,1)S(1)}, u32[]{:S(2)}, u32[]{:S(2)}) collective-permute-start(bf16[924,256]{1,0:T(8,128)(2,1)S(1)} %fusion.2), channel_id=1, source_target_pairs={{0,48},{48,96},{96,144},{144,192},{192,240},{240,288},{288,336},{3... | collective-permute-start | bytes 1419272 | tf_op jit(solution)/shard_map/ppermute | solution.py:84
  85.4 15.5 %collective-permute-start.12 = (bf16[924,256]{1,0:T(8,128)(2,1)S(1)}, bf16[924,256]{1,0:T(8,128)(2,1)S(1)}, u32[]{:S(2)}, u32[]{:S(2)}) collective-permute-start(bf16[924,256]{1,0:T(8,128)(2,1)S(1)} %fusion.9), channel_id=1, source_target_pairs={{0,336},{48,0},{96,48},{144,96},{192,144},{240,192},{288,240},{336... | collective-permute-start | bytes 1419272 | tf_op jit(solution)/shard_map/ppermute | solution.py:85
  91.2 15.5 %collective-permute-start.5 = (bf16[924,256]{1,0:T(8,128)(2,1)S(1)}, bf16[924,256]{1,0:T(8,128)(2,1)S(1)}, u32[]{:S(2)}, u32[]{:S(2)}) collective-permute-start(bf16[924,256]{1,0:T(8,128)(2,1)S(1)} %fusion.3), channel_id=1, source_target_pairs={{0,48},{48,96},{96,144},{144,192},{192,240},{240,288},{288,336},{3... | collective-permute-start | bytes 1419272 | tf_op jit(solution)/shard_map/ppermute | solution.py:84
  101.1 14.7 %collective-permute-start.13 = (bf16[924,256]{1,0:T(8,128)(2,1)S(1)}, bf16[924,256]{1,0:T(8,128)(2,1)S(1)}, u32[]{:S(2)}, u32[]{:S(2)}) collective-permute-start(bf16[924,256]{1,0:T(8,128)(2,1)S(1)} %fusion.10), channel_id=1, source_target_pairs={{0,336},{48,0},{96,48},{144,96},{192,144},{240,192},{288,240},{336... | collective-permute-start | bytes 1419272 | tf_op jit(solution)/shard_map/ppermute | solution.py:85
  106.9 14.6 %collective-permute-start.6 = (bf16[924,256]{1,0:T(8,128)(2,1)S(1)}, bf16[924,256]{1,0:T(8,128)(2,1)S(1)}, u32[]{:S(2)}, u32[]{:S(2)}) collective-permute-start(bf16[924,256]{1,0:T(8,128)(2,1)S(1)} %fusion.4), channel_id=1, source_target_pairs={{0,48},{48,96},{96,144},{144,192},{192,240},{240,288},{288,336},{3... | collective-permute-start | bytes 1419272 | tf_op jit(solution)/shard_map/ppermute | solution.py:84
  115.9 13.8 %collective-permute-start.14 = (bf16[924,256]{1,0:T(8,128)(2,1)S(1)}, bf16[924,256]{1,0:T(8,128)(2,1)S(1)}, u32[]{:S(2)}, u32[]{:S(2)}) collective-permute-start(bf16[924,256]{1,0:T(8,128)(2,1)S(1)} %fusion.11), channel_id=1, source_target_pairs={{0,336},{48,0},{96,48},{144,96},{192,144},{240,192},{288,240},{336... | collective-permute-start | bytes 1419272 | tf_op jit(solution)/shard_map/ppermute | solution.py:85
  121.6 13.8 %collective-permute-start.7 = (bf16[924,256]{1,0:T(8,128)(2,1)S(1)}, bf16[924,256]{1,0:T(8,128)(2,1)S(1)}, u32[]{:S(2)}, u32[]{:S(2)}) collective-permute-start(bf16[924,256]{1,0:T(8,128)(2,1)S(1)} %fusion.5), channel_id=1, source_target_pairs={{0,48},{48,96},{96,144},{144,192},{192,240},{240,288},{288,336},{3... | collective-permute-start | bytes 1419272 | tf_op jit(solution)/shard_map/ppermute | solution.py:84
  129.8 13.0 %collective-permute-start.15 = (bf16[924,256]{1,0:T(8,128)(2,1)S(1)}, bf16[924,256]{1,0:T(8,128)(2,1)S(1)}, u32[]{:S(2)}, u32[]{:S(2)}) collective-permute-start(bf16[924,256]{1,0:T(8,128)(2,1)S(1)} %fusion.12), channel_id=1, source_target_pairs={{0,336},{48,0},{96,48},{144,96},{192,144},{240,192},{288,240},{336... | collective-permute-start | bytes 1419272 | tf_op jit(solution)/shard_map/ppermute | solution.py:85
  135.6 12.9 %collective-permute-start.8 = (bf16[924,256]{1,0:T(8,128)(2,1)S(1)}, bf16[924,256]{1,0:T(8,128)(2,1)S(1)}, u32[]{:S(2)}, u32[]{:S(2)}) collective-permute-start(bf16[924,256]{1,0:T(8,128)(2,1)S(1)} %fusion.6), channel_id=1, source_target_pairs={{0,48},{48,96},{96,144},{144,192},{192,240},{240,288},{288,336},{3... | collective-permute-start | bytes 1419272 | tf_op jit(solution)/shard_map/ppermute | solution.py:84
  142.9 12.1 %collective-permute-start.16 = (bf16[924,256]{1,0:T(8,128)(2,1)S(1)}, bf16[924,256]{1,0:T(8,128)(2,1)S(1)}, u32[]{:S(2)}, u32[]{:S(2)}) collective-permute-start(bf16[924,256]{1,0:T(8,128)(2,1)S(1)} %fusion.13), channel_id=1, source_target_pairs={{0,336},{48,0},{96,48},{144,96},{192,144},{240,192},{288,240},{336... | collective-permute-start | bytes 1419272 | tf_op jit(solution)/shard_map/ppermute | solution.py:85
  149.5 12.1 %collective-permute-start.9 = (bf16[924,256]{1,0:T(8,128)(2,1)}, bf16[924,256]{1,0:T(8,128)(2,1)}, u32[]{:S(2)}, u32[]{:S(2)}) collective-permute-start(bf16[924,256]{1,0:T(8,128)(2,1)} %fusion.7), channel_id=1, source_target_pairs={{0,48},{48,96},{96,144},{144,192},{192,240},{240,288},{288,336},{3... | collective-permute-start | bytes 1419272 | tf_op jit(solution)/shard_map/ppermute | solution.py:84
  166.9 1.3 copy-start.2
  168.3 12.1 %collective-permute-start.17 = (bf16[924,2,128]{2,0,1:T(8,128)(2,1)S(1)}, bf16[924,2,128]{2,0,1:T(8,128)(2,1)S(1)}, u32[]{:S(2)}, u32[]{:S(2)}) collective-permute-start(bf16[924,2,128]{2,0,1:T(8,128)(2,1)S(1)} %fusion.15), channel_id=1, source_target_pairs={{0,384},{48,432},{96,480},{144,528},{192,576},{240,624},{288,672},... | collective-permute-start | bytes 1419272 | tf_op jit(solution)/shard_map/ppermute | solution.py:92

commit v3 on v1

--- a/solution.py
+++ b/solution.py
@@ -37,6 +37,20 @@
 
 
 def backward_core(tok_rows, grad_rows, w_gate, w_up, w_down):
+    n = lax.axis_size("dp")
+    nx = 2
+    ny = n // nx
+    xh = lax.axis_index("dp") // ny
+    across = [(a * ny + b, (1 - a) * ny + b) for a in range(nx) for b in range(ny)]
+    rows, width = tok_rows.shape
+    tok_halves = tok_rows.reshape(rows, nx, width // nx)
+    grad_halves = grad_rows.reshape(rows, nx, width // nx)
+    tok_mine = lax.dynamic_index_in_dim(tok_halves, xh, axis=1, keepdims=False)
+    grad_mine = lax.dynamic_index_in_dim(grad_halves, xh, axis=1, keepdims=False)
+    tok_other = lax.dynamic_index_in_dim(tok_halves, 1 - xh, axis=1, keepdims=False)
+    grad_other = lax.dynamic_index_in_dim(grad_halves, 1 - xh, axis=1, keepdims=False)
+    tok_peer, grad_peer = lax.ppermute((tok_other, grad_other), "dp", across)
+
     gate_pre = jnp.dot(tok_rows, w_gate, preferred_element_type=jnp.float32)
     up_pre = jnp.dot(tok_rows, w_up, preferred_element_type=jnp.float32)
     sigmoid_gate = jax.nn.sigmoid(gate_pre)
@@ -48,26 +62,34 @@
     )
     d_up = (d_hidden * gate_act).astype(jnp.bfloat16)
     grad_tok = (contract_cols(d_gate, w_gate) + contract_cols(d_up, w_up)).astype(jnp.bfloat16)
-    grad_gate = contract_rows(tok_rows, d_gate)
-    grad_up = contract_rows(tok_rows, d_up)
-    grad_down = contract_rows(grad_rows, hidden)
-    summed = reduce_over_dp(jnp.stack([grad_gate, grad_up, grad_down]))
-    return (grad_tok, summed / lax.axis_size("dp"))
+    mixed = jnp.concatenate([d_gate, d_up, hidden], axis=1)
+    mixed_peer = lax.ppermute(mixed, "dp", across)
+    mixed_all = jnp.concatenate([mixed, mixed_peer], axis=0)
+    tok_all = jnp.concatenate([tok_mine, tok_peer], axis=0)
+    grad_all = jnp.concatenate([grad_mine, grad_peer], axis=0)
+    summed = reduce_over_y(tok_all, grad_all, mixed_all, hidden.shape[1])
+    return (grad_tok, summed / n)
 
 
-def reduce_over_dp(parts):
+def reduce_over_y(tok_all, grad_all, mixed_all, cols):
     n = lax.axis_size("dp")
     nx = 2
     ny = n // nx
-    index = lax.axis_index("dp")
-    xh = index // ny
-    y = index % ny
-    three, width, cols = parts.shape
-    half = width // n // 2
-    view = parts.reshape(three, nx, ny, 2, half, cols)
+    y = lax.axis_index("dp") % ny
+    rows, width = tok_all.shape
+    lane = width // ny // 2
+    tok_view = tok_all.reshape(rows, ny * 2, lane)
+    grad_view = grad_all.reshape(rows, ny * 2, lane)
+    d_both = mixed_all[:, : 2 * cols]
+    hidden = mixed_all[:, 2 * cols :]
 
     def chunk(c, h):
-        return lax.dynamic_index_in_dim(view[:, :, :, h], c, axis=2, keepdims=False)
+        b = c * 2 + h
+        tok_part = lax.dynamic_index_in_dim(tok_view, b, axis=1, keepdims=False)
+        grad_part = lax.dynamic_index_in_dim(grad_view, b, axis=1, keepdims=False)
+        first = contract_rows(d_both, tok_part)
+        second = contract_rows(hidden, grad_part)
+        return jnp.concatenate([first, second], axis=0)
 
     fwd = [(a * ny + b, a * ny + (b + 1) % ny) for a in range(nx) for b in range(ny)]
     bwd = [(a * ny + b, a * ny + (b - 1) % ny) for a in range(nx) for b in range(ny)]
@@ -78,12 +100,8 @@
         recv_b = lax.ppermute(acc_b.astype(jnp.bfloat16), "dp", bwd)
         acc_f = recv_f.astype(jnp.float32) + chunk((y + 2 * ny - 2 - s) % ny, 0)
         acc_b = recv_b.astype(jnp.float32) + chunk((y + 2 + s) % ny, 1)
-    acc = jnp.stack([acc_f, acc_b], axis=2)
-    mine = lax.dynamic_index_in_dim(acc, xh, axis=1, keepdims=False)
-    other = lax.dynamic_index_in_dim(acc, 1 - xh, axis=1, keepdims=False)
-    across = [(a * ny + b, (1 - a) * ny + b) for a in range(nx) for b in range(ny)]
-    got = lax.ppermute(other.astype(jnp.bfloat16), "dp", across)
-    return (mine + got.astype(jnp.float32)).reshape(three, 2 * half, cols)
+    total = jnp.concatenate([acc_f, acc_b], axis=1).reshape(3, cols, 2 * lane)
+    return jnp.transpose(total, (0, 2, 1))
 
 
 def shards(tokens, cotangent, gate_weight, up_weight, down_weight, counts, seg_ids, pair_side):

time: 254 us -> 184 us (0.72)
  the two profiles are of different devices: /device:TPU:194 before, /device:TPU:24 now
where the time goes in v3:
time: 184 us; the launch traced here: 183 us
  starting transfers between devices  71.4 us (39%)
  waiting for transfers between devices  57.6 us (31%)
  matrix products  24.6 us (13%)
  local copies, waits for them, and re-layouts  18.7 us (10%)
  other arithmetic  8.24 us (4%)
  between operations  2.4 us (1%)
    ppermute x7, starting transfers between devices, reduce_over_y(): recv_f = lax.ppermute(acc_f.astype(jnp.bfloat16), 'dp', fwd)  38.3 us
    ppermute x3, waiting for transfers between devices, shifted(): return lax.ppermute(block, axis, route)  31 us
    ppermute x7, waiting for transfers between devices, reduce_over_y(): recv_f = lax.ppermute(acc_f.astype(jnp.bfloat16), 'dp', fwd)  14.4 us
    ppermute x7, starting transfers between devices, reduce_over_y(): recv_b = lax.ppermute(acc_b.astype(jnp.bfloat16), 'dp', bwd)  13.4 us
    dot_general x32, matrix products, contract_rows(): lax.dot_general(left, right, (((0,), (0,)), ((), ())), preferred_element_...  12 us
    ppermute x2, starting transfers between devices, backward_core(): tok_peer, grad_peer = lax.ppermute((tok_other, grad_other), 'dp', across)  9.65 us
    ppermute x3, starting transfers between devices, shifted(): return lax.ppermute(block, axis, route)  7.33 us
    ppermute x7, waiting for transfers between devices, reduce_over_y(): recv_b = lax.ppermute(acc_b.astype(jnp.bfloat16), 'dp', bwd)  6.13 us
  transfers between devices with their start and end apart: 20, of which 12 were waited for; matrix products, arithmetic and copies ran while one was open for 20% of the time, Pallas kernels for 0%

profile of v3, /device:TPU:24, one launch (start us, length us, event | category | flops | bytes accessed | tf_op | source)
XLA Modules:
  0.0 183.0 jit_solution(14717474952415254789)
XLA Ops:
  3.6 2.5 %fusion.1 = bf16[128,4096]{1,0:T(8,128)(2,1)} fusion(bf16[1,1,128,4096]{3,2,1,0:T(8,128)(2,1)} %param.9, f32[128]{0:T(128)S(1)} %select_reduce_fusion), kind=kLoop, calls=%fused_computation.71 | loop fusion | flops 1572864 | bytes 2097664 | tf_op jit(solution)/shard_map/reshape | solution.py:112
  8.0 3.5 %collective-permute-start.1 = (bf16[128,4096]{1,0:T(8,128)(2,1)}, bf16[128,4096]{1,0:T(8,128)(2,1)}, u32[]{:S(2)}, u32[]{:S(2)}) collective-permute-start(bf16[128,4096]{1,0:T(8,128)(2,1)} %bitcast.247), channel_id=1, source_target_pairs={{47,0},{0,1},{1,2},{2,3},{3,4},{4,5},{5,6},{6,7},{7,8},{8,9},{9,10... | collective-permute-start | bytes 3145736 | tf_op jit(solution)/shard_map/ppermute | solution.py:13
  11.8 22.0 %collective-permute-done = bf16[128,4096]{1,0:T(8,128)(2,1)} collective-permute-done((bf16[128,4096]{1,0:T(8,128)(2,1)}, bf16[128,4096]{1,0:T(8,128)(2,1)}, u32[]{:S(2)}, u32[]{:S(2)}) %collective-permute-start) | collective-permute-done | bytes 1048608 | tf_op jit(solution)/shard_map/ppermute | solution.py:13
  33.8 2.3 %copy.52 = bf16[128,4096]{0,1:T(8,128)(2,1)} copy(bf16[128,4096]{1,0:T(8,128)(2,1)} %collective-permute-done) | data formatting | bytes 2097152 | tf_op jit(solution)/shard_map/ppermute | solution.py:13
  36.1 9.0 %collective-permute-done.1 = bf16[128,4096]{1,0:T(8,128)(2,1)} collective-permute-done((bf16[128,4096]{1,0:T(8,128)(2,1)}, bf16[128,4096]{1,0:T(8,128)(2,1)}, u32[]{:S(2)}, u32[]{:S(2)}) %collective-permute-start.1) | collective-permute-done | bytes 1048608 | tf_op jit(solution)/shard_map/ppermute | solution.py:13
  45.1 2.3 %copy.48 = bf16[128,4096]{0,1:T(8,128)(2,1)} copy(bf16[128,4096]{1,0:T(8,128)(2,1)} %collective-permute-done.1) | data formatting | bytes 2097152 | tf_op jit(solution)/shard_map/ppermute | solution.py:13
  47.3 2.7 %constant_dynamic-slice_fusion = (bf16[128,1,2048]{0,2,1:T(8,128)(2,1)}, bf16[128,1,2048]{0,2,1:T(8,128)(2,1)S(1)}, bf16[128,1,2048]{0,2,1:T(8,128)(2,1)}, bf16[128,1,2048]{0,2,1:T(8,128)(2,1)}) fusion(bf16[128,2,2048]{0,2,1:T(8,128)(2,1)} %bitcast.240, s32[]{:T(128)S(6)} %select_n.147, s32[]{:T(128)S(6)} %select_n.146, bf16[128,2,2048]{0,2,1:T(8,128)(2,1)} %bitcast.241), kind=kLoop, calls=%fused_computation.232 | loop fusion | bytes 4194312 | tf_op jit(solution)/shard_map/jit(dynamic_index_in_dim)/dynamic_slice | solution.py:51
  50.0 2.1 %copy.49 = bf16[128,1,2048]{2,0,1:T(8,128)(2,1)} copy(bf16[128,1,2048]{0,2,1:T(8,128)(2,1)} %get-tuple-element.10) | data formatting | bytes 1048576 | tf_op jit(solution)/shard_map/jit(dynamic_index_in_dim)/dynamic_slice | solution.py:50
  52.1 4.9 %collective-permute-start.4 = (bf16[128,2048]{1,0:T(8,128)(2,1)}, bf16[128,2048]{1,0:T(8,128)(2,1)}, u32[]{:S(2)}, u32[]{:S(2)}) collective-permute-start(bf16[128,2048]{1,0:T(8,128)(2,1)} %bitcast.243), channel_id=1, source_target_pairs={{0,384},{48,432},{96,480},{144,528},{192,576},{240,624},{288,672},... | collective-permute-start | bytes 1572872 | tf_op jit(solution)/shard_map/ppermute | solution.py:52
  57.0 2.9 %fusion.221 = f32[128,308]{0,1:T(8,128)S(1)} fusion(bf16[128,4096]{1,0:T(8,128)(2,1)} %collective-permute-done, bf16[4096,308]{0,1:T(8,128)(2,1)} %param.12), kind=kOutput, calls=%fused_computation.292 | convolution fusion | flops 322961408 | bytes 3729408 | tf_op jit(solution)/shard_map/dot_general | solution.py:59
  59.9 2.1 %fusion.222 = f32[128,308]{0,1:T(8,128)S(1)} fusion(bf16[128,4096]{1,0:T(8,128)(2,1)} %collective-permute-done.1, bf16[4096,308]{0,1:T(8,128)(2,1)S(1)} %copy-done.5), kind=kOutput, calls=%fused_computation.293 | convolution fusion | flops 322961408 | bytes 3729408 | tf_op jit(solution)/shard_map/dot_general | solution.py:54
  62.0 2.1 %multiply_convert_fusion.1 = (bf16[128,308]{0,1:T(8,128)(2,1)S(1)}, bf16[128,308]{0,1:T(8,128)(2,1)S(1)}, bf16[128,308]{0,1:T(8,128)(2,1)S(1)}) fusion(f32[128,308]{0,1:T(8,128)S(1)} %fusion.222, f32[128,308]{0,1:T(8,128)S(1)} %fusion.221, bf16[128,4096]{1,0:T(8,128)(2,1)} %collective-permute-done.1, bf16[4096,308]{0,1:T(8,128)(2,1)S(1)} %copy-done), kind=kOutput, calls=%fused_computation.104 | convolution fusion | flops 323552768 | bytes 4123648 | tf_op jit(solution)/shard_map/dot_general | solution.py:55
  64.1 2.1 %fusion.223 = f32[128,4096]{1,0:T(8,128)} fusion(bf16[128,308]{0,1:T(8,128)(2,1)S(1)} %get-tuple-element.7, bf16[4096,308]{0,1:T(8,128)(2,1)S(1)} %copy-done.5), kind=kOutput, calls=%fused_computation.294 | convolution fusion | flops 322961408 | bytes 4699136 | tf_op jit(solution)/shard_map/dot_general | solution.py:34
  66.2 2.7 %collective-permute-start.3 = (bf16[128,924]{0,1:T(8,128)(2,1)S(1)}, bf16[128,924]{0,1:T(8,128)(2,1)}, u32[]{:S(2)}, u32[]{:S(2)}) collective-permute-start(bf16[128,924]{0,1:T(8,128)(2,1)S(1)} %pad_maximum_fusion.1), channel_id=1, source_target_pairs={{0,384},{48,432},{96,480},{144,528},{192,576},{240,624},{288,672},... | collective-permute-start | bytes 709640 | tf_op jit(solution)/shard_map/ppermute | solution.py:66
  69.0 2.0 %copy.53 = bf16[128,1,2048]{2,0,1:T(8,128)(2,1)} copy(bf16[128,1,2048]{0,2,1:T(8,128)(2,1)} %get-tuple-element.4) | data formatting | bytes 1048576 | tf_op jit(solution)/shard_map/jit(dynamic_index_in_dim)/dynamic_slice | solution.py:51
  71.0 4.8 %collective-permute-start.5 = (bf16[128,2048]{1,0:T(8,128)(2,1)}, bf16[128,2048]{1,0:T(8,128)(2,1)}, u32[]{:S(2)}, u32[]{:S(2)}) collective-permute-start(bf16[128,2048]{1,0:T(8,128)(2,1)} %bitcast.244), channel_id=1, source_target_pairs={{0,384},{48,432},{96,480},{144,528},{192,576},{240,624},{288,672},... | collective-permute-start | bytes 1572872 | tf_op jit(solution)/shard_map/ppermute | solution.py:52
  75.8 3.4 %fusion = bf16[128,4096]{1,0:T(8,128)(2,1)} fusion(f32[128,4096]{1,0:T(8,128)} %fusion.223, bf16[128,308]{0,1:T(8,128)(2,1)S(1)} %get-tuple-element.8, bf16[4096,308]{0,1:T(8,128)(2,1)S(1)} %copy-done), kind=kOutput, calls=%fused_computation.1 | convolution fusion | flops 324009984 | bytes 5747712 | tf_op jit(solution)/shard_map/dot_general | solution.py:34
  81.1 6.1 %collective-permute-done.3 = bf16[128,924]{0,1:T(8,128)(2,1)} collective-permute-done((bf16[128,924]{0,1:T(8,128)(2,1)S(1)}, bf16[128,924]{0,1:T(8,128)(2,1)}, u32[]{:S(2)}, u32[]{:S(2)}) %collective-permute-start.3) | collective-permute-done | bytes 236576 | tf_op jit(solution)/shard_map/ppermute | solution.py:66
  89.8 2.1 %copy.50 = bf16[128,2048]{0,1:T(8,128)(2,1)} copy(bf16[128,2048]{1,0:T(8,128)(2,1)} %collective-permute-done.4) | data formatting | bytes 1048576 | tf_op jit(solution)/shard_map/ppermute | solution.py:52
  95.3 2.0 %copy.54 = bf16[128,2048]{0,1:T(8,128)(2,1)} copy(bf16[128,2048]{1,0:T(8,128)(2,1)} %collective-permute-done.5) | data formatting | bytes 1048576 | tf_op jit(solution)/shard_map/ppermute | solution.py:52
  103.5 4.7 %collective-permute-start.6 = (bf16[924,128]{1,0:T(8,128)(2,1)S(1)}, bf16[924,128]{1,0:T(8,128)(2,1)S(1)}, u32[]{:S(2)}, u32[]{:S(2)}) collective-permute-start(bf16[924,128]{1,0:T(8,128)(2,1)S(1)} %pad_maximum_fusion.2), channel_id=1, source_target_pairs={{0,48},{48,96},{96,144},{144,192},{192,240},{240,288},{288,336},{3... | collective-permute-start | bytes 709640 | tf_op jit(solution)/shard_map/ppermute | solution.py:99
  112.6 5.6 %collective-permute-start.7 = (bf16[924,128]{1,0:T(8,128)(2,1)S(1)}, bf16[924,128]{1,0:T(8,128)(2,1)S(1)}, u32[]{:S(2)}, u32[]{:S(2)}) collective-permute-start(bf16[924,128]{1,0:T(8,128)(2,1)S(1)} %fusion.2), channel_id=1, source_target_pairs={{0,48},{48,96},{96,144},{144,192},{192,240},{240,288},{288,336},{3... | collective-permute-start | bytes 709640 | tf_op jit(solution)/shard_map/ppermute | solution.py:99
  120.5 3.3 %collective-permute-done.7 = bf16[924,128]{1,0:T(8,128)(2,1)S(1)} collective-permute-done((bf16[924,128]{1,0:T(8,128)(2,1)S(1)}, bf16[924,128]{1,0:T(8,128)(2,1)S(1)}, u32[]{:S(2)}, u32[]{:S(2)}) %collective-permute-start.7) | collective-permute-done | bytes 236576 | tf_op jit(solution)/shard_map/ppermute | solution.py:99
  123.8 5.6 %collective-permute-start.8 = (bf16[924,128]{1,0:T(8,128)(2,1)S(1)}, bf16[924,128]{1,0:T(8,128)(2,1)S(1)}, u32[]{:S(2)}, u32[]{:S(2)}) collective-permute-start(bf16[924,128]{1,0:T(8,128)(2,1)S(1)} %fusion.3), channel_id=1, source_target_pairs={{0,48},{48,96},{96,144},{144,192},{192,240},{240,288},{288,336},{3... | collective-permute-start | bytes 709640 | tf_op jit(solution)/shard_map/ppermute | solution.py:99
  131.9 3.2 %collective-permute-done.8 = bf16[924,128]{1,0:T(8,128)(2,1)S(1)} collective-permute-done((bf16[924,128]{1,0:T(8,128)(2,1)S(1)}, bf16[924,128]{1,0:T(8,128)(2,1)S(1)}, u32[]{:S(2)}, u32[]{:S(2)}) %collective-permute-start.8) | collective-permute-done | bytes 236576 | tf_op jit(solution)/shard_map/ppermute | solution.py:99
  135.1 5.6 %collective-permute-start.9 = (bf16[924,128]{1,0:T(8,128)(2,1)S(1)}, bf16[924,128]{1,0:T(8,128)(2,1)S(1)}, u32[]{:S(2)}, u32[]{:S(2)}) collective-permute-start(bf16[924,128]{1,0:T(8,128)(2,1)S(1)} %fusion.4), channel_id=1, source_target_pairs={{0,48},{48,96},{96,144},{144,192},{192,240},{240,288},{288,336},{3... | collective-permute-start | bytes 709640 | tf_op jit(solution)/shard_map/ppermute | solution.py:99
  143.0 2.6 %collective-permute-done.9 = bf16[924,128]{1,0:T(8,128)(2,1)S(1)} collective-permute-done((bf16[924,128]{1,0:T(8,128)(2,1)S(1)}, bf16[924,128]{1,0:T(8,128)(2,1)S(1)}, u32[]{:S(2)}, u32[]{:S(2)}) %collective-permute-start.9) | collective-permute-done | bytes 236576 | tf_op jit(solution)/shard_map/ppermute | solution.py:99
  145.6 5.6 %collective-permute-start.10 = (bf16[924,128]{1,0:T(8,128)(2,1)S(1)}, bf16[924,128]{1,0:T(8,128)(2,1)S(1)}, u32[]{:S(2)}, u32[]{:S(2)}) collective-permute-start(bf16[924,128]{1,0:T(8,128)(2,1)S(1)} %fusion.5), channel_id=1, source_target_pairs={{0,48},{48,96},{96,144},{144,192},{192,240},{240,288},{288,336},{3... | collective-permute-start | bytes 709640 | tf_op jit(solution)/shard_map/ppermute | solution.py:99
  155.2 5.6 %collective-permute-start.11 = (bf16[924,128]{1,0:T(8,128)(2,1)S(1)}, bf16[924,128]{1,0:T(8,128)(2,1)S(1)}, u32[]{:S(2)}, u32[]{:S(2)}) collective-permute-start(bf16[924,128]{1,0:T(8,128)(2,1)S(1)} %fusion.6), channel_id=1, source_target_pairs={{0,48},{48,96},{96,144},{144,192},{192,240},{240,288},{288,336},{3... | collective-permute-start | bytes 709640 | tf_op jit(solution)/shard_map/ppermute | solution.py:99
  164.4 5.6 %collective-permute-start.12 = (bf16[924,128]{1,0:T(8,128)(2,1)S(1)}, bf16[924,128]{1,0:T(8,128)(2,1)S(1)}, u32[]{:S(2)}, u32[]{:S(2)}) collective-permute-start(bf16[924,128]{1,0:T(8,128)(2,1)S(1)} %fusion.7), channel_id=1, source_target_pairs={{0,48},{48,96},{96,144},{144,192},{192,240},{240,288},{288,336},{3... | collective-permute-start | bytes 709640 | tf_op jit(solution)/shard_map/ppermute | solution.py:99
  173.7 5.9 %collective-permute-done.19 = bf16[924,128]{1,0:T(8,128)(2,1)S(1)} collective-permute-done((bf16[924,128]{1,0:T(8,128)(2,1)S(1)}, bf16[924,128]{1,0:T(8,128)(2,1)S(1)}, u32[]{:S(2)}, u32[]{:S(2)}) %collective-permute-start.19) | collective-permute-done | bytes 236576 | tf_op jit(solution)/shard_map/ppermute | solution.py:100
  180.7 2.3 %copy.88 = bf16[1,1,128,4096]{3,2,1,0:T(8,128)(2,1)} copy(bf16[1,1,128,4096]{3,2,1,0:T(8,128)(2,1)} %bitcast.6) | data formatting | bytes 2097152
  (105 shorter events, 41.8 us)
Async XLA Ops:
  0.6 61.3 %copy-start = (bf16[4096,308]{0,1:T(8,128)(2,1)S(1)}, bf16[4096,308]{0,1:T(8,128)(2,1)}, u32[]{:S(2)}) copy-start(bf16[4096,308]{0,1:T(8,128)(2,1)} %param.11) | copy-start | bytes 7569412
  6.1 27.7 %collective-permute-start = (bf16[128,4096]{1,0:T(8,128)(2,1)}, bf16[128,4096]{1,0:T(8,128)(2,1)}, u32[]{:S(2)}, u32[]{:S(2)}) collective-permute-start(bf16[128,4096]{1,0:T(8,128)(2,1)} %fusion.1), channel_id=1, source_target_pairs={{47,0},{0,1},{1,2},{2,3},{3,4},{4,5},{5,6},{6,7},{7,8},{8,9},{9,10... | collective-permute-start | bytes 3145736 | tf_op jit(solution)/shard_map/ppermute | solution.py:13
  8.0 37.1 %collective-permute-start.1 = (bf16[128,4096]{1,0:T(8,128)(2,1)}, bf16[128,4096]{1,0:T(8,128)(2,1)}, u32[]{:S(2)}, u32[]{:S(2)}) collective-permute-start(bf16[128,4096]{1,0:T(8,128)(2,1)} %bitcast.247), channel_id=1, source_target_pairs={{47,0},{0,1},{1,2},{2,3},{3,4},{4,5},{5,6},{6,7},{7,8},{8,9},{9,10... | collective-permute-start | bytes 3145736 | tf_op jit(solution)/shard_map/ppermute | solution.py:13
  52.0 7.8 %copy-start.5 = (bf16[4096,308]{0,1:T(8,128)(2,1)S(1)}, bf16[4096,308]{0,1:T(8,128)(2,1)}, u32[]{:S(2)}) copy-start(bf16[4096,308]{0,1:T(8,128)(2,1)} %param.10) | copy-start | bytes 7569412
  52.1 37.7 %collective-permute-start.4 = (bf16[128,2048]{1,0:T(8,128)(2,1)}, bf16[128,2048]{1,0:T(8,128)(2,1)}, u32[]{:S(2)}, u32[]{:S(2)}) collective-permute-start(bf16[128,2048]{1,0:T(8,128)(2,1)} %bitcast.243), channel_id=1, source_target_pairs={{0,384},{48,432},{96,480},{144,528},{192,576},{240,624},{288,672},... | collective-permute-start | bytes 1572872 | tf_op jit(solution)/shard_map/ppermute | solution.py:52
  64.0 2.2 %copy-start.6 = (bf16[128,308]{0,1:T(8,128)(2,1)}, bf16[128,308]{0,1:T(8,128)(2,1)S(1)}, u32[]{:S(2)}) copy-start(bf16[128,308]{0,1:T(8,128)(2,1)S(1)} %get-tuple-element.7) | copy-start | bytes 236548
  64.0 2.2 %copy-start.10 = (bf16[128,308]{0,1:T(8,128)(2,1)}, bf16[128,308]{0,1:T(8,128)(2,1)S(1)}, u32[]{:S(2)}) copy-start(bf16[128,308]{0,1:T(8,128)(2,1)S(1)} %get-tuple-element.6) | copy-start | bytes 236548
  64.0 11.7 %copy-start.8 = (bf16[128,308]{0,1:T(8,128)(2,1)}, bf16[128,308]{0,1:T(8,128)(2,1)S(1)}, u32[]{:S(2)}) copy-start(bf16[128,308]{0,1:T(8,128)(2,1)S(1)} %get-tuple-element.8) | copy-start | bytes 236548
  66.2 20.9 %collective-permute-start.3 = (bf16[128,924]{0,1:T(8,128)(2,1)S(1)}, bf16[128,924]{0,1:T(8,128)(2,1)}, u32[]{:S(2)}, u32[]{:S(2)}) collective-permute-start(bf16[128,924]{0,1:T(8,128)(2,1)S(1)} %pad_maximum_fusion.1), channel_id=1, source_target_pairs={{0,384},{48,432},{96,480},{144,528},{192,576},{240,624},{288,672},... | collective-permute-start | bytes 709640 | tf_op jit(solution)/shard_map/ppermute | solution.py:66
  71.0 16.1 %copy-start.7 = (bf16[128,308]{0,1:T(8,128)(2,1)S(1)}, bf16[128,308]{0,1:T(8,128)(2,1)}, u32[]{:S(2)}) copy-start(bf16[128,308]{0,1:T(8,128)(2,1)} %copy-done.6) | copy-start | bytes 236548
  71.0 16.1 %copy-start.11 = (bf16[128,308]{0,1:T(8,128)(2,1)S(1)}, bf16[128,308]{0,1:T(8,128)(2,1)}, u32[]{:S(2)}) copy-start(bf16[128,308]{0,1:T(8,128)(2,1)} %copy-done.10) | copy-start | bytes 236548
  71.0 24.3 %collective-permute-start.5 = (bf16[128,2048]{1,0:T(8,128)(2,1)}, bf16[128,2048]{1,0:T(8,128)(2,1)}, u32[]{:S(2)}, u32[]{:S(2)}) collective-permute-start(bf16[128,2048]{1,0:T(8,128)(2,1)} %bitcast.244), channel_id=1, source_target_pairs={{0,384},{48,432},{96,480},{144,528},{192,576},{240,624},{288,672},... | collective-permute-start | bytes 1572872 | tf_op jit(solution)/shard_map/ppermute | solution.py:52
  79.1 91.1 %collective-permute-start.2 = (bf16[128,4096]{1,0:T(8,128)(2,1)}, bf16[128,4096]{1,0:T(8,128)(2,1)}, u32[]{:S(2)}, u32[]{:S(2)}) collective-permute-start(bf16[128,4096]{1,0:T(8,128)(2,1)} %fusion), channel_id=1, source_target_pairs={{1,0},{2,1},{3,2},{4,3},{5,4},{6,5},{7,6},{8,7},{9,8},{10,9},{11,1... | collective-permute-start | bytes 3145736 | tf_op jit(solution)/shard_map/ppermute | solution.py:13
  97.3 2.4 %copy-start.2 = (bf16[128,1,2048]{0,2,1:T(8,128)(2,1)S(1)}, bf16[128,1,2048]{0,2,1:T(8,128)(2,1)}, u32[]{:S(2)}) copy-start(bf16[128,1,2048]{0,2,1:T(8,128)(2,1)} %get-tuple-element.9) | copy-start | bytes 1572868
  97.3 2.4 %copy-start.3 = (bf16[128,2048]{0,1:T(8,128)(2,1)S(1)}, bf16[128,2048]{0,1:T(8,128)(2,1)}, u32[]{:S(2)}) copy-start(bf16[128,2048]{0,1:T(8,128)(2,1)} %copy.50) | copy-start | bytes 1572868
  97.4 2.6 %copy-start.1 = (bf16[128,2048]{0,1:T(8,128)(2,1)S(1)}, bf16[128,2048]{0,1:T(8,128)(2,1)}, u32[]{:S(2)}) copy-start(bf16[128,2048]{0,1:T(8,128)(2,1)} %copy.54) | copy-start | bytes 1572868
  97.4 2.7 %copy-start.4 = (bf16[256,308]{0,1:T(8,128)(2,1)S(1)}, bf16[256,308]{0,1:T(8,128)(2,1)}, u32[]{:S(2)}) copy-start(bf16[256,308]{0,1:T(8,128)(2,1)} %pad_maximum_fusion.4) | copy-start | bytes 473092
  103.5 9.1 %collective-permute-start.6 = (bf16[924,128]{1,0:T(8,128)(2,1)S(1)}, bf16[924,128]{1,0:T(8,128)(2,1)S(1)}, u32[]{:S(2)}, u32[]{:S(2)}) collective-permute-start(bf16[924,128]{1,0:T(8,128)(2,1)S(1)} %pad_maximum_fusion.2), channel_id=1, source_target_pairs={{0,48},{48,96},{96,144},{144,192},{192,240},{240,288},{288,336},{3... | collective-permute-start | bytes 709640 | tf_op jit(solution)/shard_map/ppermute | solution.py:99
  108.2 10.2 %collective-permute-start.13 = (bf16[924,128]{1,0:T(8,128)(2,1)S(1)}, bf16[924,128]{1,0:T(8,128)(2,1)S(1)}, u32[]{:S(2)}, u32[]{:S(2)}) collective-permute-start(bf16[924,128]{1,0:T(8,128)(2,1)S(1)} %pad_maximum_fusion.3), channel_id=1, source_target_pairs={{0,336},{48,0},{96,48},{144,96},{192,144},{240,192},{288,240},{336... | collective-permute-start | bytes 709640 | tf_op jit(solution)/shard_map/ppermute | solution.py:100
  110.9 1.7 copy-start.9
  112.6 11.1 %collective-permute-start.7 = (bf16[924,128]{1,0:T(8,128)(2,1)S(1)}, bf16[924,128]{1,0:T(8,128)(2,1)S(1)}, u32[]{:S(2)}, u32[]{:S(2)}) collective-permute-start(bf16[924,128]{1,0:T(8,128)(2,1)S(1)} %fusion.2), channel_id=1, source_target_pairs={{0,48},{48,96},{96,144},{144,192},{192,240},{240,288},{288,336},{3... | collective-permute-start | bytes 709640 | tf_op jit(solution)/shard_map/ppermute | solution.py:99
  118.5 11.4 %collective-permute-start.14 = (bf16[924,128]{1,0:T(8,128)(2,1)S(1)}, bf16[924,128]{1,0:T(8,128)(2,1)S(1)}, u32[]{:S(2)}, u32[]{:S(2)}) collective-permute-start(bf16[924,128]{1,0:T(8,128)(2,1)S(1)} %fusion.8), channel_id=1, source_target_pairs={{0,336},{48,0},{96,48},{144,96},{192,144},{240,192},{288,240},{336... | collective-permute-start | bytes 709640 | tf_op jit(solution)/shard_map/ppermute | solution.py:100
  123.8 11.2 %collective-permute-start.8 = (bf16[924,128]{1,0:T(8,128)(2,1)S(1)}, bf16[924,128]{1,0:T(8,128)(2,1)S(1)}, u32[]{:S(2)}, u32[]{:S(2)}) collective-permute-start(bf16[924,128]{1,0:T(8,128)(2,1)S(1)} %fusion.3), channel_id=1, source_target_pairs={{0,48},{48,96},{96,144},{144,192},{192,240},{240,288},{288,336},{3... | collective-permute-start | bytes 709640 | tf_op jit(solution)/shard_map/ppermute | solution.py:99
  130.0 11.0 %collective-permute-start.15 = (bf16[924,128]{1,0:T(8,128)(2,1)S(1)}, bf16[924,128]{1,0:T(8,128)(2,1)S(1)}, u32[]{:S(2)}, u32[]{:S(2)}) collective-permute-start(bf16[924,128]{1,0:T(8,128)(2,1)S(1)} %fusion.9), channel_id=1, source_target_pairs={{0,336},{48,0},{96,48},{144,96},{192,144},{240,192},{288,240},{336... | collective-permute-start | bytes 709640 | tf_op jit(solution)/shard_map/ppermute | solution.py:100
  135.1 10.4 %collective-permute-start.9 = (bf16[924,128]{1,0:T(8,128)(2,1)S(1)}, bf16[924,128]{1,0:T(8,128)(2,1)S(1)}, u32[]{:S(2)}, u32[]{:S(2)}) collective-permute-start(bf16[924,128]{1,0:T(8,128)(2,1)S(1)} %fusion.4), channel_id=1, source_target_pairs={{0,48},{48,96},{96,144},{144,192},{192,240},{240,288},{288,336},{3... | collective-permute-start | bytes 709640 | tf_op jit(solution)/shard_map/ppermute | solution.py:99
  141.0 10.4 %collective-permute-start.16 = (bf16[924,128]{1,0:T(8,128)(2,1)S(1)}, bf16[924,128]{1,0:T(8,128)(2,1)S(1)}, u32[]{:S(2)}, u32[]{:S(2)}) collective-permute-start(bf16[924,128]{1,0:T(8,128)(2,1)S(1)} %fusion.10), channel_id=1, source_target_pairs={{0,336},{48,0},{96,48},{144,96},{192,144},{240,192},{288,240},{336... | collective-permute-start | bytes 709640 | tf_op jit(solution)/shard_map/ppermute | solution.py:100
  145.6 9.5 %collective-permute-start.10 = (bf16[924,128]{1,0:T(8,128)(2,1)S(1)}, bf16[924,128]{1,0:T(8,128)(2,1)S(1)}, u32[]{:S(2)}, u32[]{:S(2)}) collective-permute-start(bf16[924,128]{1,0:T(8,128)(2,1)S(1)} %fusion.5), channel_id=1, source_target_pairs={{0,48},{48,96},{96,144},{144,192},{192,240},{240,288},{288,336},{3... | collective-permute-start | bytes 709640 | tf_op jit(solution)/shard_map/ppermute | solution.py:99
  151.5 9.5 %collective-permute-start.17 = (bf16[924,128]{1,0:T(8,128)(2,1)S(1)}, bf16[924,128]{1,0:T(8,128)(2,1)S(1)}, u32[]{:S(2)}, u32[]{:S(2)}) collective-permute-start(bf16[924,128]{1,0:T(8,128)(2,1)S(1)} %fusion.11), channel_id=1, source_target_pairs={{0,336},{48,0},{96,48},{144,96},{192,144},{240,192},{288,240},{336... | collective-permute-start | bytes 709640 | tf_op jit(solution)/shard_map/ppermute | solution.py:100
  155.2 9.2 %collective-permute-start.11 = (bf16[924,128]{1,0:T(8,128)(2,1)S(1)}, bf16[924,128]{1,0:T(8,128)(2,1)S(1)}, u32[]{:S(2)}, u32[]{:S(2)}) collective-permute-start(bf16[924,128]{1,0:T(8,128)(2,1)S(1)} %fusion.6), channel_id=1, source_target_pairs={{0,48},{48,96},{96,144},{144,192},{192,240},{240,288},{288,336},{3... | collective-permute-start | bytes 709640 | tf_op jit(solution)/shard_map/ppermute | solution.py:99
  161.1 9.2 %collective-permute-start.18 = (bf16[924,128]{1,0:T(8,128)(2,1)S(1)}, bf16[924,128]{1,0:T(8,128)(2,1)S(1)}, u32[]{:S(2)}, u32[]{:S(2)}) collective-permute-start(bf16[924,128]{1,0:T(8,128)(2,1)S(1)} %fusion.12), channel_id=1, source_target_pairs={{0,336},{48,0},{96,48},{144,96},{192,144},{240,192},{288,240},{336... | collective-permute-start | bytes 709640 | tf_op jit(solution)/shard_map/ppermute | solution.py:100
  164.4 9.2 %collective-permute-start.12 = (bf16[924,128]{1,0:T(8,128)(2,1)S(1)}, bf16[924,128]{1,0:T(8,128)(2,1)S(1)}, u32[]{:S(2)}, u32[]{:S(2)}) collective-permute-start(bf16[924,128]{1,0:T(8,128)(2,1)S(1)} %fusion.7), channel_id=1, source_target_pairs={{0,48},{48,96},{96,144},{144,192},{192,240},{240,288},{288,336},{3... | collective-permute-start | bytes 709640 | tf_op jit(solution)/shard_map/ppermute | solution.py:99
  170.3 9.2 %collective-permute-start.19 = (bf16[924,128]{1,0:T(8,128)(2,1)S(1)}, bf16[924,128]{1,0:T(8,128)(2,1)S(1)}, u32[]{:S(2)}, u32[]{:S(2)}) collective-permute-start(bf16[924,128]{1,0:T(8,128)(2,1)S(1)} %fusion.13), channel_id=1, source_target_pairs={{0,336},{48,0},{96,48},{144,96},{192,144},{240,192},{288,240},{336... | collective-permute-start | bytes 709640 | tf_op jit(solution)/shard_map/ppermute | solution.py:100
  (1 other events, 0.9 us)

commit v4 on v3

--- a/solution.py
+++ b/solution.py
@@ -36,7 +36,7 @@
     )
 
 
-def backward_core(tok_rows, grad_rows, w_gate, w_up, w_down):
+def backward_core(tok_rows, grad_rows, tok_peer, grad_peer, w_gate, w_up, w_down):
     n = lax.axis_size("dp")
     nx = 2
     ny = n // nx
@@ -47,9 +47,6 @@
     grad_halves = grad_rows.reshape(rows, nx, width // nx)
     tok_mine = lax.dynamic_index_in_dim(tok_halves, xh, axis=1, keepdims=False)
     grad_mine = lax.dynamic_index_in_dim(grad_halves, xh, axis=1, keepdims=False)
-    tok_other = lax.dynamic_index_in_dim(tok_halves, 1 - xh, axis=1, keepdims=False)
-    grad_other = lax.dynamic_index_in_dim(grad_halves, 1 - xh, axis=1, keepdims=False)
-    tok_peer, grad_peer = lax.ppermute((tok_other, grad_other), "dp", across)
 
     gate_pre = jnp.dot(tok_rows, w_gate, preferred_element_type=jnp.float32)
     up_pre = jnp.dot(tok_rows, w_up, preferred_element_type=jnp.float32)
@@ -111,8 +108,18 @@
     tok_rows = tokens.reshape(-1, width)
     grad_rows = upstream.reshape(-1, width)
     moved_rows, moved_grads = shifted((tok_rows, grad_rows), "blk", 1)
+    n = lax.axis_size("dp")
+    nb = lax.axis_size("blk")
+    ny = n // 2
+    xh = lax.axis_index("dp") // ny
+    halves = (tok_rows.reshape(tok_rows.shape[0], 2, -1), grad_rows.reshape(grad_rows.shape[0], 2, -1))
+    other = tuple(lax.dynamic_index_in_dim(h, 1 - xh, axis=1, keepdims=False) for h in halves)
+    diagonal = [
+        (d * nb + j, ((d + ny) % n) * nb + (j + 1) % nb) for d in range(n) for j in range(nb)
+    ]
+    tok_peer, grad_peer = lax.ppermute(other, ("dp", "blk"), diagonal)
     grad_moved, panel_grads = backward_core(
-        moved_rows, moved_grads, gate_weight, up_weight, down_weight
+        moved_rows, moved_grads, tok_peer, grad_peer, gate_weight, up_weight, down_weight
     )
     grad_tok = shifted(grad_moved, "blk", -1)
     return (grad_tok.reshape(tokens.shape), panel_grads)

time: 184 us -> 170 us (0.924)
  waiting for transfers between devices: 57.6 us -> 48.1 us
  matrix products: 24.6 us -> 17 us
  starting transfers between devices: 71.4 us -> 77.5 us
  other arithmetic: 8.24 us -> 5.54 us
    ppermute x3, waiting for transfers between devices: 31 us -> 0.01 us  [shifted(): return lax.ppermute(block, axis, route)]
    ppermute x2, waiting for transfers between devices: 0.01 us -> 28.3 us  [shards(): tok_peer, grad_peer = lax.ppermute(other, ('dp', 'blk'), diagonal)]
    ppermute x3, starting transfers between devices: 7.33 us -> 13.5 us  [shifted(): return lax.ppermute(block, axis, route)]
    ppermute x1, waiting for transfers between devices: 6.09 us -> 0.01 us  [backward_core(): mixed_peer = lax.ppermute(mixed, 'dp', across)]
    dot_general x32, matrix products: 12 us -> 7.13 us  [contract_rows(): lax.dot_general(left, right, (((0,), (0,)), ((), ())), preferred_element_...]
    unnamed x27 -> x19, local copies, waits for them, and re-layouts: 2.34 us -> 7 us
    dot_general x2, matrix products: 5.49 us -> 2.64 us  [contract_cols(): lax.dot_general(left, right, (((1,), (1,)), ((), ())), preferred_element_...]
    ppermute x2 -> x1, local copies, waits for them, and re-layouts: 4.52 us -> 2.29 us  [shifted(): return lax.ppermute(block, axis, route)]
  transfers between devices with their start and end apart: 20 -> 20, of which waited for: 12 -> 10; matrix products, arithmetic and copies ran while one was open for 20% -> 16% of each run, Pallas kernels for 0% -> 0%
where the time goes in v4:
time: 170 us; the launch traced here: 169 us
  starting transfers between devices  77.5 us (46%)
  waiting for transfers between devices  48.1 us (28%)
  local copies, waits for them, and re-layouts  19 us (11%)
  matrix products  17 us (10%)
  other arithmetic  5.54 us (3%)
  between operations  2.29 us (1%)
    ppermute x7, starting transfers between devices, reduce_over_y(): recv_f = lax.ppermute(acc_f.astype(jnp.bfloat16), 'dp', fwd)  38.3 us
    ppermute x2, waiting for transfers between devices, shards(): tok_peer, grad_peer = lax.ppermute(other, ('dp', 'blk'), diagonal)  28.3 us
    ppermute x7, waiting for transfers between devices, reduce_over_y(): recv_f = lax.ppermute(acc_f.astype(jnp.bfloat16), 'dp', fwd)  13.9 us
    ppermute x3, starting transfers between devices, shifted(): return lax.ppermute(block, axis, route)  13.5 us
    ppermute x7, starting transfers between devices, reduce_over_y(): recv_b = lax.ppermute(acc_b.astype(jnp.bfloat16), 'dp', bwd)  13.4 us
    ppermute x2, starting transfers between devices, shards(): tok_peer, grad_peer = lax.ppermute(other, ('dp', 'blk'), diagonal)  9.43 us
    dot_general x32, matrix products, contract_rows(): lax.dot_general(left, right, (((0,), (0,)), ((), ())), preferred_element_...  7.13 us
    unnamed x19, local copies, waits for them, and re-layouts  7 us
  transfers between devices with their start and end apart: 20, of which 10 were waited for; matrix products, arithmetic and copies ran while one was open for 16% of the time, Pallas kernels for 0%

profile of v4, /device:TPU:24, one launch (start us, length us, event | category | flops | bytes accessed | tf_op | source)
XLA Modules:
  0.0 169.4 jit_solution(2367667879300022306)
XLA Ops:
  0.7 2.4 %copy.87 = bf16[1,1,128,4096]{2,3,1,0:T(8,128)(2,1)} copy(bf16[1,1,128,4096]{3,2,1,0:T(8,128)(2,1)} %param.8) | data formatting | bytes 2097152 | tf_op args[0]
  5.2 4.4 %collective-permute-start.4 = (bf16[128,2048]{1,0:T(8,128)(2,1)}, bf16[128,2048]{1,0:T(8,128)(2,1)}, u32[]{:S(2)}, u32[]{:S(2)}) collective-permute-start(bf16[128,2048]{1,0:T(8,128)(2,1)} %bitcast.247), channel_id=1, source_target_pairs={{0,385},{1,386},{2,387},{3,388},{4,389},{5,390},{6,391},{7,392},{8... | collective-permute-start | bytes 1572872 | tf_op jit(solution)/shard_map/ppermute | solution.py:120
  9.5 2.3 %collective-permute-start.1 = (bf16[128,4096]{1,0:T(8,128)(2,1)}, bf16[128,4096]{1,0:T(8,128)(2,1)}, u32[]{:S(2)}, u32[]{:S(2)}) collective-permute-start(bf16[128,4096]{1,0:T(8,128)(2,1)} %bitcast.245), channel_id=1, source_target_pairs={{47,0},{0,1},{1,2},{2,3},{3,4},{4,5},{5,6},{6,7},{7,8},{8,9},{9,10... | collective-permute-start | bytes 3145736 | tf_op jit(solution)/shard_map/ppermute | solution.py:13
  12.8 2.3 %copy.85 = bf16[1,1,128,4096]{2,3,1,0:T(8,128)(2,1)} copy(bf16[1,1,128,4096]{3,2,1,0:T(8,128)(2,1)} %param.9) | data formatting | bytes 2097152 | tf_op args[1]
  15.0 2.5 %fusion.249 = bf16[128,4096]{0,1:T(8,128)(2,1)} fusion(f32[128]{0:T(128)S(1)} %select_reduce_fusion, bf16[1,1,128,4096]{2,3,1,0:T(8,128)(2,1)} %copy.85), kind=kLoop, calls=%fused_computation.294 | loop fusion | flops 1572864 | bytes 2097664 | tf_op jit(solution)/shard_map/reshape | solution.py:109
  17.5 2.2 %collective-permute-start = (bf16[128,4096]{0,1:T(8,128)(2,1)}, bf16[128,4096]{0,1:T(8,128)(2,1)}, u32[]{:S(2)}, u32[]{:S(2)}) collective-permute-start(bf16[128,4096]{0,1:T(8,128)(2,1)} %fusion.249), channel_id=1, source_target_pairs={{47,0},{0,1},{1,2},{2,3},{3,4},{4,5},{5,6},{6,7},{7,8},{8,9},{9,10... | collective-permute-start | bytes 3145736 | tf_op jit(solution)/shard_map/ppermute | solution.py:13
  21.0 5.1 %collective-permute-start.5 = (bf16[128,2048]{1,0:T(8,128)(2,1)}, bf16[128,2048]{1,0:T(8,128)(2,1)}, u32[]{:S(2)}, u32[]{:S(2)}) collective-permute-start(bf16[128,2048]{1,0:T(8,128)(2,1)} %bitcast.248), channel_id=1, source_target_pairs={{0,385},{1,386},{2,387},{3,388},{4,389},{5,390},{6,391},{7,392},{8... | collective-permute-start | bytes 1572872 | tf_op jit(solution)/shard_map/ppermute | solution.py:120
  26.4 2.2 %collective-permute-done.4 = bf16[128,2048]{1,0:T(8,128)(2,1)} collective-permute-done((bf16[128,2048]{1,0:T(8,128)(2,1)}, bf16[128,2048]{1,0:T(8,128)(2,1)}, u32[]{:S(2)}, u32[]{:S(2)}) %collective-permute-start.4) | collective-permute-done | bytes 524320 | tf_op jit(solution)/shard_map/ppermute | solution.py:120
  28.6 2.0 %copy.89 = bf16[128,2048]{0,1:T(8,128)(2,1)} copy(bf16[128,2048]{1,0:T(8,128)(2,1)} %collective-permute-done.4) | data formatting | bytes 1048576 | tf_op jit(solution)/shard_map/ppermute | solution.py:120
  30.6 26.1 %collective-permute-done.5 = bf16[128,2048]{1,0:T(8,128)(2,1)} collective-permute-done((bf16[128,2048]{1,0:T(8,128)(2,1)}, bf16[128,2048]{1,0:T(8,128)(2,1)}, u32[]{:S(2)}, u32[]{:S(2)}) %collective-permute-start.5) | collective-permute-done | bytes 524320 | tf_op jit(solution)/shard_map/ppermute | solution.py:120
  58.0 3.0 %fusion.220 = f32[128,308]{0,1:T(8,128)S(1)} fusion(bf16[128,4096]{0,1:T(8,128)(2,1)} %collective-permute-done, bf16[4096,308]{0,1:T(8,128)(2,1)} %param.12), kind=kOutput, calls=%fused_computation.291 | convolution fusion | flops 322961408 | bytes 3729408 | tf_op jit(solution)/shard_map/dot_general | solution.py:56
  61.1 2.1 %fusion.221 = f32[128,308]{0,1:T(8,128)S(1)} fusion(bf16[128,4096]{1,0:T(8,128)(2,1)} %collective-permute-done.1, bf16[4096,308]{0,1:T(8,128)(2,1)S(1)} %copy-done.2), kind=kOutput, calls=%fused_computation.292 | convolution fusion | flops 322961408 | bytes 3729408 | tf_op jit(solution)/shard_map/dot_general | solution.py:51
  63.2 2.1 %multiply_convert_fusion.1 = (bf16[128,308]{0,1:T(8,128)(2,1)S(1)}, bf16[128,308]{0,1:T(8,128)(2,1)S(1)}, bf16[128,308]{0,1:T(8,128)(2,1)S(1)}) fusion(f32[128,308]{0,1:T(8,128)S(1)} %fusion.221, f32[128,308]{0,1:T(8,128)S(1)} %fusion.220, bf16[128,4096]{1,0:T(8,128)(2,1)} %collective-permute-done.1, bf16[4096,308]{0,1:T(8,128)(2,1)S(1)} %copy-done), kind=kOutput, calls=%fused_computation.103 | convolution fusion | flops 323552768 | bytes 4123648 | tf_op jit(solution)/shard_map/dot_general | solution.py:52
  66.9 2.9 %collective-permute-start.3 = (bf16[128,924]{0,1:T(8,128)(2,1)}, bf16[128,924]{0,1:T(8,128)(2,1)S(1)}, u32[]{:S(2)}, u32[]{:S(2)}) collective-permute-start(bf16[128,924]{0,1:T(8,128)(2,1)} %pad_maximum_fusion.1), channel_id=1, source_target_pairs={{0,384},{48,432},{96,480},{144,528},{192,576},{240,624},{288,672},... | collective-permute-start | bytes 709640 | tf_op jit(solution)/shard_map/ppermute | solution.py:63
  71.5 8.9 %collective-permute-start.2 = (bf16[128,4096]{1,0:T(8,128)(2,1)}, bf16[128,4096]{1,0:T(8,128)(2,1)}, u32[]{:S(2)}, u32[]{:S(2)}) collective-permute-start(bf16[128,4096]{1,0:T(8,128)(2,1)} %fusion), channel_id=1, source_target_pairs={{1,0},{2,1},{3,2},{4,3},{5,4},{6,5},{7,6},{8,7},{9,8},{10,9},{11,1... | collective-permute-start | bytes 3145736 | tf_op jit(solution)/shard_map/ppermute | solution.py:13
  80.5 2.3 %copy.86 = bf16[128,4096]{0,1:T(8,128)(2,1)} copy(bf16[128,4096]{1,0:T(8,128)(2,1)} %collective-permute-done.1) | data formatting | bytes 2097152 | tf_op jit(solution)/shard_map/ppermute | solution.py:13
  90.7 4.7 %collective-permute-start.6 = (bf16[924,128]{1,0:T(8,128)(2,1)S(1)}, bf16[924,128]{1,0:T(8,128)(2,1)S(1)}, u32[]{:S(2)}, u32[]{:S(2)}) collective-permute-start(bf16[924,128]{1,0:T(8,128)(2,1)S(1)} %pad_maximum_fusion.2), channel_id=1, source_target_pairs={{0,48},{48,96},{96,144},{144,192},{192,240},{240,288},{288,336},{3... | collective-permute-start | bytes 709640 | tf_op jit(solution)/shard_map/ppermute | solution.py:96
  95.4 1.9 %collective-permute-start.13 = (bf16[924,128]{1,0:T(8,128)(2,1)S(1)}, bf16[924,128]{1,0:T(8,128)(2,1)S(1)}, u32[]{:S(2)}, u32[]{:S(2)}) collective-permute-start(bf16[924,128]{1,0:T(8,128)(2,1)S(1)} %pad_maximum_fusion.3), channel_id=1, source_target_pairs={{0,336},{48,0},{96,48},{144,96},{192,144},{240,192},{288,240},{336... | collective-permute-start | bytes 709640 | tf_op jit(solution)/shard_map/ppermute | solution.py:97
  98.9 2.1 %collective-permute-done.6 = bf16[924,128]{1,0:T(8,128)(2,1)S(1)} collective-permute-done((bf16[924,128]{1,0:T(8,128)(2,1)S(1)}, bf16[924,128]{1,0:T(8,128)(2,1)S(1)}, u32[]{:S(2)}, u32[]{:S(2)}) %collective-permute-start.6) | collective-permute-done | bytes 236576 | tf_op jit(solution)/shard_map/ppermute | solution.py:96
  101.0 5.6 %collective-permute-start.7 = (bf16[924,128]{1,0:T(8,128)(2,1)S(1)}, bf16[924,128]{1,0:T(8,128)(2,1)S(1)}, u32[]{:S(2)}, u32[]{:S(2)}) collective-permute-start(bf16[924,128]{1,0:T(8,128)(2,1)S(1)} %fusion.1), channel_id=1, source_target_pairs={{0,48},{48,96},{96,144},{144,192},{192,240},{240,288},{288,336},{3... | collective-permute-start | bytes 709640 | tf_op jit(solution)/shard_map/ppermute | solution.py:96
  106.9 1.9 %collective-permute-start.14 = (bf16[924,128]{1,0:T(8,128)(2,1)S(1)}, bf16[924,128]{1,0:T(8,128)(2,1)S(1)}, u32[]{:S(2)}, u32[]{:S(2)}) collective-permute-start(bf16[924,128]{1,0:T(8,128)(2,1)S(1)} %fusion.7), channel_id=1, source_target_pairs={{0,336},{48,0},{96,48},{144,96},{192,144},{240,192},{288,240},{336... | collective-permute-start | bytes 709640 | tf_op jit(solution)/shard_map/ppermute | solution.py:97
  108.8 3.4 %collective-permute-done.7 = bf16[924,128]{1,0:T(8,128)(2,1)S(1)} collective-permute-done((bf16[924,128]{1,0:T(8,128)(2,1)S(1)}, bf16[924,128]{1,0:T(8,128)(2,1)S(1)}, u32[]{:S(2)}, u32[]{:S(2)}) %collective-permute-start.7) | collective-permute-done | bytes 236576 | tf_op jit(solution)/shard_map/ppermute | solution.py:96
  112.3 5.6 %collective-permute-start.8 = (bf16[924,128]{1,0:T(8,128)(2,1)S(1)}, bf16[924,128]{1,0:T(8,128)(2,1)S(1)}, u32[]{:S(2)}, u32[]{:S(2)}) collective-permute-start(bf16[924,128]{1,0:T(8,128)(2,1)S(1)} %fusion.2), channel_id=1, source_target_pairs={{0,48},{48,96},{96,144},{144,192},{192,240},{240,288},{288,336},{3... | collective-permute-start | bytes 709640 | tf_op jit(solution)/shard_map/ppermute | solution.py:96
  120.1 2.6 %collective-permute-done.8 = bf16[924,128]{1,0:T(8,128)(2,1)S(1)} collective-permute-done((bf16[924,128]{1,0:T(8,128)(2,1)S(1)}, bf16[924,128]{1,0:T(8,128)(2,1)S(1)}, u32[]{:S(2)}, u32[]{:S(2)}) %collective-permute-start.8) | collective-permute-done | bytes 236576 | tf_op jit(solution)/shard_map/ppermute | solution.py:96
  122.7 5.6 %collective-permute-start.9 = (bf16[924,128]{1,0:T(8,128)(2,1)S(1)}, bf16[924,128]{1,0:T(8,128)(2,1)S(1)}, u32[]{:S(2)}, u32[]{:S(2)}) collective-permute-start(bf16[924,128]{1,0:T(8,128)(2,1)S(1)} %fusion.3), channel_id=1, source_target_pairs={{0,48},{48,96},{96,144},{144,192},{192,240},{240,288},{288,336},{3... | collective-permute-start | bytes 709640 | tf_op jit(solution)/shard_map/ppermute | solution.py:96
  132.3 5.6 %collective-permute-start.10 = (bf16[924,128]{1,0:T(8,128)(2,1)S(1)}, bf16[924,128]{1,0:T(8,128)(2,1)S(1)}, u32[]{:S(2)}, u32[]{:S(2)}) collective-permute-start(bf16[924,128]{1,0:T(8,128)(2,1)S(1)} %fusion.4), channel_id=1, source_target_pairs={{0,48},{48,96},{96,144},{144,192},{192,240},{240,288},{288,336},{3... | collective-permute-start | bytes 709640 | tf_op jit(solution)/shard_map/ppermute | solution.py:96
  138.2 1.9 %collective-permute-start.17 = (bf16[924,128]{1,0:T(8,128)(2,1)S(1)}, bf16[924,128]{1,0:T(8,128)(2,1)S(1)}, u32[]{:S(2)}, u32[]{:S(2)}) collective-permute-start(bf16[924,128]{1,0:T(8,128)(2,1)S(1)} %fusion.10), channel_id=1, source_target_pairs={{0,336},{48,0},{96,48},{144,96},{192,144},{240,192},{288,240},{336... | collective-permute-start | bytes 709640 | tf_op jit(solution)/shard_map/ppermute | solution.py:97
  141.6 5.6 %collective-permute-start.11 = (bf16[924,128]{1,0:T(8,128)(2,1)S(1)}, bf16[924,128]{1,0:T(8,128)(2,1)S(1)}, u32[]{:S(2)}, u32[]{:S(2)}) collective-permute-start(bf16[924,128]{1,0:T(8,128)(2,1)S(1)} %fusion.5), channel_id=1, source_target_pairs={{0,48},{48,96},{96,144},{144,192},{192,240},{240,288},{288,336},{3... | collective-permute-start | bytes 709640 | tf_op jit(solution)/shard_map/ppermute | solution.py:96
  147.5 1.9 %collective-permute-start.18 = (bf16[924,128]{1,0:T(8,128)(2,1)S(1)}, bf16[924,128]{1,0:T(8,128)(2,1)S(1)}, u32[]{:S(2)}, u32[]{:S(2)}) collective-permute-start(bf16[924,128]{1,0:T(8,128)(2,1)S(1)} %fusion.11), channel_id=1, source_target_pairs={{0,336},{48,0},{96,48},{144,96},{192,144},{240,192},{288,240},{336... | collective-permute-start | bytes 709640 | tf_op jit(solution)/shard_map/ppermute | solution.py:97
  150.9 5.6 %collective-permute-start.12 = (bf16[924,128]{1,0:T(8,128)(2,1)S(1)}, bf16[924,128]{1,0:T(8,128)(2,1)S(1)}, u32[]{:S(2)}, u32[]{:S(2)}) collective-permute-start(bf16[924,128]{1,0:T(8,128)(2,1)S(1)} %fusion.6), channel_id=1, source_target_pairs={{0,48},{48,96},{96,144},{144,192},{192,240},{240,288},{288,336},{3... | collective-permute-start | bytes 709640 | tf_op jit(solution)/shard_map/ppermute | solution.py:96
  160.1 5.8 %collective-permute-done.19 = bf16[924,128]{1,0:T(8,128)(2,1)S(1)} collective-permute-done((bf16[924,128]{1,0:T(8,128)(2,1)S(1)}, bf16[924,128]{1,0:T(8,128)(2,1)S(1)}, u32[]{:S(2)}, u32[]{:S(2)}) %collective-permute-start.19) | collective-permute-done | bytes 236576 | tf_op jit(solution)/shard_map/ppermute | solution.py:97
  167.1 2.3 %copy.126 = bf16[1,1,128,4096]{3,2,1,0:T(8,128)(2,1)} copy(bf16[1,1,128,4096]{3,2,1,0:T(8,128)(2,1)} %bitcast.6) | data formatting | bytes 2097152
  (100 shorter events, 32.2 us)
Async XLA Ops:
  0.6 62.6 %copy-start = (bf16[4096,308]{0,1:T(8,128)(2,1)S(1)}, bf16[4096,308]{0,1:T(8,128)(2,1)}, u32[]{:S(2)}) copy-start(bf16[4096,308]{0,1:T(8,128)(2,1)} %param.11) | copy-start | bytes 7569412
  0.6 11.9 %copy-start.6 = (s32[1,1,128]{2,1,0:T(1,128)S(1)}, s32[1,1,128]{2,1,0:T(1,128)}, u32[]{:S(2)}) copy-start(s32[1,1,128]{2,1,0:T(1,128)} %param.14) | copy-start | bytes 1540
  0.7 12.0 %copy-start.7 = (s32[1,1,4]{2,1,0:T(1,128)S(1)}, s32[1,1,4]{2,1,0:T(1,128)}, u32[]{:S(2)}) copy-start(s32[1,1,4]{2,1,0:T(1,128)} %param.15) | copy-start | bytes 52
  5.2 23.4 %collective-permute-start.4 = (bf16[128,2048]{1,0:T(8,128)(2,1)}, bf16[128,2048]{1,0:T(8,128)(2,1)}, u32[]{:S(2)}, u32[]{:S(2)}) collective-permute-start(bf16[128,2048]{1,0:T(8,128)(2,1)} %bitcast.247), channel_id=1, source_target_pairs={{0,385},{1,386},{2,387},{3,388},{4,389},{5,390},{6,391},{7,392},{8... | collective-permute-start | bytes 1572872 | tf_op jit(solution)/shard_map/ppermute | solution.py:120
  9.5 51.5 %collective-permute-start.1 = (bf16[128,4096]{1,0:T(8,128)(2,1)}, bf16[128,4096]{1,0:T(8,128)(2,1)}, u32[]{:S(2)}, u32[]{:S(2)}) collective-permute-start(bf16[128,4096]{1,0:T(8,128)(2,1)} %bitcast.245), channel_id=1, source_target_pairs={{47,0},{0,1},{1,2},{2,3},{3,4},{4,5},{5,6},{6,7},{7,8},{8,9},{9,10... | collective-permute-start | bytes 3145736 | tf_op jit(solution)/shard_map/ppermute | solution.py:13
  15.0 4.7 %copy-start.3 = (bf16[1,1,128,4096]{2,3,1,0:T(8,128)(2,1)S(1)}, bf16[1,1,128,4096]{2,3,1,0:T(8,128)(2,1)}, u32[]{:S(2)}) copy-start(bf16[1,1,128,4096]{2,3,1,0:T(8,128)(2,1)} %copy.85) | copy-start | bytes 3145732
  17.5 40.5 %collective-permute-start = (bf16[128,4096]{0,1:T(8,128)(2,1)}, bf16[128,4096]{0,1:T(8,128)(2,1)}, u32[]{:S(2)}, u32[]{:S(2)}) collective-permute-start(bf16[128,4096]{0,1:T(8,128)(2,1)} %fusion.249), channel_id=1, source_target_pairs={{47,0},{0,1},{1,2},{2,3},{3,4},{4,5},{5,6},{6,7},{7,8},{8,9},{9,10... | collective-permute-start | bytes 3145736 | tf_op jit(solution)/shard_map/ppermute | solution.py:13
  21.0 35.7 %collective-permute-start.5 = (bf16[128,2048]{1,0:T(8,128)(2,1)}, bf16[128,2048]{1,0:T(8,128)(2,1)}, u32[]{:S(2)}, u32[]{:S(2)}) collective-permute-start(bf16[128,2048]{1,0:T(8,128)(2,1)} %bitcast.248), channel_id=1, source_target_pairs={{0,385},{1,386},{2,387},{3,388},{4,389},{5,390},{6,391},{7,392},{8... | collective-permute-start | bytes 1572872 | tf_op jit(solution)/shard_map/ppermute | solution.py:120
  58.0 3.1 %copy-start.2 = (bf16[4096,308]{0,1:T(8,128)(2,1)S(1)}, bf16[4096,308]{0,1:T(8,128)(2,1)}, u32[]{:S(2)}) copy-start(bf16[4096,308]{0,1:T(8,128)(2,1)} %param.10) | copy-start | bytes 7569412
  65.3 1.6 copy-start.4
  66.9 18.1 %collective-permute-start.3 = (bf16[128,924]{0,1:T(8,128)(2,1)}, bf16[128,924]{0,1:T(8,128)(2,1)S(1)}, u32[]{:S(2)}, u32[]{:S(2)}) collective-permute-start(bf16[128,924]{0,1:T(8,128)(2,1)} %pad_maximum_fusion.1), channel_id=1, source_target_pairs={{0,384},{48,432},{96,480},{144,528},{192,576},{240,624},{288,672},... | collective-permute-start | bytes 709640 | tf_op jit(solution)/shard_map/ppermute | solution.py:63
  71.5 85.1 %collective-permute-start.2 = (bf16[128,4096]{1,0:T(8,128)(2,1)}, bf16[128,4096]{1,0:T(8,128)(2,1)}, u32[]{:S(2)}, u32[]{:S(2)}) collective-permute-start(bf16[128,4096]{1,0:T(8,128)(2,1)} %fusion), channel_id=1, source_target_pairs={{1,0},{2,1},{3,2},{4,3},{5,4},{6,5},{7,6},{8,7},{9,8},{10,9},{11,1... | collective-permute-start | bytes 3145736 | tf_op jit(solution)/shard_map/ppermute | solution.py:13
  82.8 3.2 %copy-start.1 = (bf16[128,2048]{0,1:T(8,128)(2,1)S(1)}, bf16[128,2048]{0,1:T(8,128)(2,1)}, u32[]{:S(2)}) copy-start(bf16[128,2048]{0,1:T(8,128)(2,1)} %copy.89) | copy-start | bytes 1572868
  83.9 2.6 %copy-start.5 = (bf16[128,308]{0,1:T(8,128)(2,1)S(1)}, bf16[128,308]{0,1:T(8,128)(2,1)}, u32[]{:S(2)}) copy-start(bf16[128,308]{0,1:T(8,128)(2,1)} %copy-done.4) | copy-start | bytes 236548
  90.7 10.2 %collective-permute-start.6 = (bf16[924,128]{1,0:T(8,128)(2,1)S(1)}, bf16[924,128]{1,0:T(8,128)(2,1)S(1)}, u32[]{:S(2)}, u32[]{:S(2)}) collective-permute-start(bf16[924,128]{1,0:T(8,128)(2,1)S(1)} %pad_maximum_fusion.2), channel_id=1, source_target_pairs={{0,48},{48,96},{96,144},{144,192},{192,240},{240,288},{288,336},{3... | collective-permute-start | bytes 709640 | tf_op jit(solution)/shard_map/ppermute | solution.py:96
  95.4 11.4 %collective-permute-start.13 = (bf16[924,128]{1,0:T(8,128)(2,1)S(1)}, bf16[924,128]{1,0:T(8,128)(2,1)S(1)}, u32[]{:S(2)}, u32[]{:S(2)}) collective-permute-start(bf16[924,128]{1,0:T(8,128)(2,1)S(1)} %pad_maximum_fusion.3), channel_id=1, source_target_pairs={{0,336},{48,0},{96,48},{144,96},{192,144},{240,192},{288,240},{336... | collective-permute-start | bytes 709640 | tf_op jit(solution)/shard_map/ppermute | solution.py:97
  101.0 11.2 %collective-permute-start.7 = (bf16[924,128]{1,0:T(8,128)(2,1)S(1)}, bf16[924,128]{1,0:T(8,128)(2,1)S(1)}, u32[]{:S(2)}, u32[]{:S(2)}) collective-permute-start(bf16[924,128]{1,0:T(8,128)(2,1)S(1)} %fusion.1), channel_id=1, source_target_pairs={{0,48},{48,96},{96,144},{144,192},{192,240},{240,288},{288,336},{3... | collective-permute-start | bytes 709640 | tf_op jit(solution)/shard_map/ppermute | solution.py:96
  106.9 11.2 %collective-permute-start.14 = (bf16[924,128]{1,0:T(8,128)(2,1)S(1)}, bf16[924,128]{1,0:T(8,128)(2,1)S(1)}, u32[]{:S(2)}, u32[]{:S(2)}) collective-permute-start(bf16[924,128]{1,0:T(8,128)(2,1)S(1)} %fusion.7), channel_id=1, source_target_pairs={{0,336},{48,0},{96,48},{144,96},{192,144},{240,192},{288,240},{336... | collective-permute-start | bytes 709640 | tf_op jit(solution)/shard_map/ppermute | solution.py:97
  112.3 10.4 %collective-permute-start.8 = (bf16[924,128]{1,0:T(8,128)(2,1)S(1)}, bf16[924,128]{1,0:T(8,128)(2,1)S(1)}, u32[]{:S(2)}, u32[]{:S(2)}) collective-permute-start(bf16[924,128]{1,0:T(8,128)(2,1)S(1)} %fusion.2), channel_id=1, source_target_pairs={{0,48},{48,96},{96,144},{144,192},{192,240},{240,288},{288,336},{3... | collective-permute-start | bytes 709640 | tf_op jit(solution)/shard_map/ppermute | solution.py:96
  118.2 10.4 %collective-permute-start.15 = (bf16[924,128]{1,0:T(8,128)(2,1)S(1)}, bf16[924,128]{1,0:T(8,128)(2,1)S(1)}, u32[]{:S(2)}, u32[]{:S(2)}) collective-permute-start(bf16[924,128]{1,0:T(8,128)(2,1)S(1)} %fusion.8), channel_id=1, source_target_pairs={{0,336},{48,0},{96,48},{144,96},{192,144},{240,192},{288,240},{336... | collective-permute-start | bytes 709640 | tf_op jit(solution)/shard_map/ppermute | solution.py:97
  122.7 9.5 %collective-permute-start.9 = (bf16[924,128]{1,0:T(8,128)(2,1)S(1)}, bf16[924,128]{1,0:T(8,128)(2,1)S(1)}, u32[]{:S(2)}, u32[]{:S(2)}) collective-permute-start(bf16[924,128]{1,0:T(8,128)(2,1)S(1)} %fusion.3), channel_id=1, source_target_pairs={{0,48},{48,96},{96,144},{144,192},{192,240},{240,288},{288,336},{3... | collective-permute-start | bytes 709640 | tf_op jit(solution)/shard_map/ppermute | solution.py:96
  128.6 9.5 %collective-permute-start.16 = (bf16[924,128]{1,0:T(8,128)(2,1)S(1)}, bf16[924,128]{1,0:T(8,128)(2,1)S(1)}, u32[]{:S(2)}, u32[]{:S(2)}) collective-permute-start(bf16[924,128]{1,0:T(8,128)(2,1)S(1)} %fusion.9), channel_id=1, source_target_pairs={{0,336},{48,0},{96,48},{144,96},{192,144},{240,192},{288,240},{336... | collective-permute-start | bytes 709640 | tf_op jit(solution)/shard_map/ppermute | solution.py:97
  132.3 9.2 %collective-permute-start.10 = (bf16[924,128]{1,0:T(8,128)(2,1)S(1)}, bf16[924,128]{1,0:T(8,128)(2,1)S(1)}, u32[]{:S(2)}, u32[]{:S(2)}) collective-permute-start(bf16[924,128]{1,0:T(8,128)(2,1)S(1)} %fusion.4), channel_id=1, source_target_pairs={{0,48},{48,96},{96,144},{144,192},{192,240},{240,288},{288,336},{3... | collective-permute-start | bytes 709640 | tf_op jit(solution)/shard_map/ppermute | solution.py:96
  138.2 9.2 %collective-permute-start.17 = (bf16[924,128]{1,0:T(8,128)(2,1)S(1)}, bf16[924,128]{1,0:T(8,128)(2,1)S(1)}, u32[]{:S(2)}, u32[]{:S(2)}) collective-permute-start(bf16[924,128]{1,0:T(8,128)(2,1)S(1)} %fusion.10), channel_id=1, source_target_pairs={{0,336},{48,0},{96,48},{144,96},{192,144},{240,192},{288,240},{336... | collective-permute-start | bytes 709640 | tf_op jit(solution)/shard_map/ppermute | solution.py:97
  141.6 9.2 %collective-permute-start.11 = (bf16[924,128]{1,0:T(8,128)(2,1)S(1)}, bf16[924,128]{1,0:T(8,128)(2,1)S(1)}, u32[]{:S(2)}, u32[]{:S(2)}) collective-permute-start(bf16[924,128]{1,0:T(8,128)(2,1)S(1)} %fusion.5), channel_id=1, source_target_pairs={{0,48},{48,96},{96,144},{144,192},{192,240},{240,288},{288,336},{3... | collective-permute-start | bytes 709640 | tf_op jit(solution)/shard_map/ppermute | solution.py:96
  147.5 9.2 %collective-permute-start.18 = (bf16[924,128]{1,0:T(8,128)(2,1)S(1)}, bf16[924,128]{1,0:T(8,128)(2,1)S(1)}, u32[]{:S(2)}, u32[]{:S(2)}) collective-permute-start(bf16[924,128]{1,0:T(8,128)(2,1)S(1)} %fusion.11), channel_id=1, source_target_pairs={{0,336},{48,0},{96,48},{144,96},{192,144},{240,192},{288,240},{336... | collective-permute-start | bytes 709640 | tf_op jit(solution)/shard_map/ppermute | solution.py:97
  150.9 9.2 %collective-permute-start.12 = (bf16[924,128]{1,0:T(8,128)(2,1)S(1)}, bf16[924,128]{1,0:T(8,128)(2,1)S(1)}, u32[]{:S(2)}, u32[]{:S(2)}) collective-permute-start(bf16[924,128]{1,0:T(8,128)(2,1)S(1)} %fusion.6), channel_id=1, source_target_pairs={{0,48},{48,96},{96,144},{144,192},{192,240},{240,288},{288,336},{3... | collective-permute-start | bytes 709640 | tf_op jit(solution)/shard_map/ppermute | solution.py:96
  156.7 9.2 %collective-permute-start.19 = (bf16[924,128]{1,0:T(8,128)(2,1)S(1)}, bf16[924,128]{1,0:T(8,128)(2,1)S(1)}, u32[]{:S(2)}, u32[]{:S(2)}) collective-permute-start(bf16[924,128]{1,0:T(8,128)(2,1)S(1)} %fusion.12), channel_id=1, source_target_pairs={{0,336},{48,0},{96,48},{144,96},{192,144},{240,192},{288,240},{336... | collective-permute-start | bytes 709640 | tf_op jit(solution)/shard_map/ppermute | solution.py:97

commit v5 on v4

--- a/solution.py
+++ b/solution.py
@@ -58,17 +58,21 @@
         jnp.bfloat16
     )
     d_up = (d_hidden * gate_act).astype(jnp.bfloat16)
-    grad_tok = (contract_cols(d_gate, w_gate) + contract_cols(d_up, w_up)).astype(jnp.bfloat16)
     mixed = jnp.concatenate([d_gate, d_up, hidden], axis=1)
     mixed_peer = lax.ppermute(mixed, "dp", across)
     mixed_all = jnp.concatenate([mixed, mixed_peer], axis=0)
     tok_all = jnp.concatenate([tok_mine, tok_peer], axis=0)
     grad_all = jnp.concatenate([grad_mine, grad_peer], axis=0)
-    summed = reduce_over_y(tok_all, grad_all, mixed_all, hidden.shape[1])
+    def late(d_gate, d_up):
+        return (contract_cols(d_gate, w_gate) + contract_cols(d_up, w_up)).astype(jnp.bfloat16)
+
+    summed, grad_tok = reduce_over_y(
+        tok_all, grad_all, mixed_all, hidden.shape[1], late, (d_gate, d_up)
+    )
     return (grad_tok, summed / n)
 
 
-def reduce_over_y(tok_all, grad_all, mixed_all, cols):
+def reduce_over_y(tok_all, grad_all, mixed_all, cols, late, late_args):
     n = lax.axis_size("dp")
     nx = 2
     ny = n // nx
@@ -95,10 +99,13 @@
     for s in range(ny - 1):
         recv_f = lax.ppermute(acc_f.astype(jnp.bfloat16), "dp", fwd)
         recv_b = lax.ppermute(acc_b.astype(jnp.bfloat16), "dp", bwd)
+        if s == 0:
+            recv_f, recv_b, late_args = lax.optimization_barrier((recv_f, recv_b, late_args))
+            late_out = late(*late_args)
         acc_f = recv_f.astype(jnp.float32) + chunk((y + 2 * ny - 2 - s) % ny, 0)
         acc_b = recv_b.astype(jnp.float32) + chunk((y + 2 + s) % ny, 1)
     total = jnp.concatenate([acc_f, acc_b], axis=1).reshape(3, cols, 2 * lane)
-    return jnp.transpose(total, (0, 2, 1))
+    return jnp.transpose(total, (0, 2, 1)), late_out
 
 
 def shards(tokens, cotangent, gate_weight, up_weight, down_weight, counts, seg_ids, pair_side):

time: 170 us -> 169 us (level)
  starting transfers between devices: 77.5 us -> 71.7 us
  waiting for transfers between devices: 48.1 us -> 53 us
    ppermute x7, waiting for transfers between devices: 5.88 us -> 15 us  [reduce_over_y(): recv_b = lax.ppermute(acc_b.astype(jnp.bfloat16), 'dp', bwd)]
    ppermute x7, waiting for transfers between devices: 13.9 us -> 7.45 us  [reduce_over_y(): recv_f = lax.ppermute(acc_f.astype(jnp.bfloat16), 'dp', fwd)]
    ppermute x3, starting transfers between devices: 13.5 us -> 7.98 us  [shifted(): return lax.ppermute(block, axis, route)]
    ppermute x1, waiting for transfers between devices: 0.01 us -> 2.3 us  [backward_core(): mixed_peer = lax.ppermute(mixed, 'dp', across)]
    unnamed x19 -> x23, local copies, waits for them, and re-layouts: 7 us -> 7.64 us
  transfers between devices with their start and end apart: 20 -> 20, of which waited for: 10 -> 12; matrix products, arithmetic and copies ran while one was open for 16% -> 13% of each run, Pallas kernels for 0% -> 0%
where the time goes in v5:
time: 169 us; the launch traced here: 168 us
  starting transfers between devices  71.7 us (42%)
  waiting for transfers between devices  53 us (31%)
  local copies, waits for them, and re-layouts  19.6 us (12%)
  matrix products  16 us (9%)
  other arithmetic  5.55 us (3%)
  between operations  2.34 us (1%)
    ppermute x7, starting transfers between devices, reduce_over_y(): recv_f = lax.ppermute(acc_f.astype(jnp.bfloat16), 'dp', fwd)  37.4 us
    ppermute x2, waiting for transfers between devices, shards(): tok_peer, grad_peer = lax.ppermute(other, ('dp', 'blk'), diagonal)  28.3 us
    ppermute x7, waiting for transfers between devices, reduce_over_y(): recv_b = lax.ppermute(acc_b.astype(jnp.bfloat16), 'dp', bwd)  15 us
    ppermute x7, starting transfers between devices, reduce_over_y(): recv_b = lax.ppermute(acc_b.astype(jnp.bfloat16), 'dp', bwd)  14 us
    ppermute x2, starting transfers between devices, shards(): tok_peer, grad_peer = lax.ppermute(other, ('dp', 'blk'), diagonal)  9.43 us
    ppermute x3, starting transfers between devices, shifted(): return lax.ppermute(block, axis, route)  7.98 us
    unnamed x23, local copies, waits for them, and re-layouts  7.64 us
    ppermute x7, waiting for transfers between devices, reduce_over_y(): recv_f = lax.ppermute(acc_f.astype(jnp.bfloat16), 'dp', fwd)  7.45 us
  transfers between devices with their start and end apart: 20, of which 12 were waited for; matrix products, arithmetic and copies ran while one was open for 13% of the time, Pallas kernels for 0%

profile of v5, /device:TPU:24, one launch (start us, length us, event | category | flops | bytes accessed | tf_op | source)
XLA Modules:
  0.0 168.2 jit_solution(7195844446570524410)
XLA Ops:
  0.7 2.4 %copy.87 = bf16[1,1,128,4096]{2,3,1,0:T(8,128)(2,1)} copy(bf16[1,1,128,4096]{3,2,1,0:T(8,128)(2,1)} %param.8) | data formatting | bytes 2097152 | tf_op args[0]
  5.2 4.4 %collective-permute-start.3 = (bf16[128,2048]{1,0:T(8,128)(2,1)}, bf16[128,2048]{1,0:T(8,128)(2,1)}, u32[]{:S(2)}, u32[]{:S(2)}) collective-permute-start(bf16[128,2048]{1,0:T(8,128)(2,1)} %bitcast.248), channel_id=1, source_target_pairs={{0,385},{1,386},{2,387},{3,388},{4,389},{5,390},{6,391},{7,392},{8... | collective-permute-start | bytes 1572872 | tf_op jit(solution)/shard_map/ppermute | solution.py:127
  9.5 2.3 %collective-permute-start.1 = (bf16[128,4096]{1,0:T(8,128)(2,1)}, bf16[128,4096]{1,0:T(8,128)(2,1)}, u32[]{:S(2)}, u32[]{:S(2)}) collective-permute-start(bf16[128,4096]{1,0:T(8,128)(2,1)} %bitcast.245), channel_id=1, source_target_pairs={{47,0},{0,1},{1,2},{2,3},{3,4},{4,5},{5,6},{6,7},{7,8},{8,9},{9,10... | collective-permute-start | bytes 3145736 | tf_op jit(solution)/shard_map/ppermute | solution.py:13
  12.8 2.3 %copy.85 = bf16[1,1,128,4096]{2,3,1,0:T(8,128)(2,1)} copy(bf16[1,1,128,4096]{3,2,1,0:T(8,128)(2,1)} %param.9) | data formatting | bytes 2097152 | tf_op args[1]
  15.0 2.5 %fusion.249 = bf16[128,4096]{0,1:T(8,128)(2,1)} fusion(f32[128]{0:T(128)S(1)} %select_reduce_fusion, bf16[1,1,128,4096]{2,3,1,0:T(8,128)(2,1)} %copy.85), kind=kLoop, calls=%fused_computation.294 | loop fusion | flops 1572864 | bytes 2097664 | tf_op jit(solution)/shard_map/reshape | solution.py:116
  17.5 2.2 %collective-permute-start = (bf16[128,4096]{0,1:T(8,128)(2,1)}, bf16[128,4096]{0,1:T(8,128)(2,1)}, u32[]{:S(2)}, u32[]{:S(2)}) collective-permute-start(bf16[128,4096]{0,1:T(8,128)(2,1)} %fusion.249), channel_id=1, source_target_pairs={{47,0},{0,1},{1,2},{2,3},{3,4},{4,5},{5,6},{6,7},{7,8},{8,9},{9,10... | collective-permute-start | bytes 3145736 | tf_op jit(solution)/shard_map/ppermute | solution.py:13
  21.0 5.1 %collective-permute-start.4 = (bf16[128,2048]{1,0:T(8,128)(2,1)}, bf16[128,2048]{1,0:T(8,128)(2,1)}, u32[]{:S(2)}, u32[]{:S(2)}) collective-permute-start(bf16[128,2048]{1,0:T(8,128)(2,1)} %bitcast.249), channel_id=1, source_target_pairs={{0,385},{1,386},{2,387},{3,388},{4,389},{5,390},{6,391},{7,392},{8... | collective-permute-start | bytes 1572872 | tf_op jit(solution)/shard_map/ppermute | solution.py:127
  26.4 2.2 %collective-permute-done.3 = bf16[128,2048]{1,0:T(8,128)(2,1)} collective-permute-done((bf16[128,2048]{1,0:T(8,128)(2,1)}, bf16[128,2048]{1,0:T(8,128)(2,1)}, u32[]{:S(2)}, u32[]{:S(2)}) %collective-permute-start.3) | collective-permute-done | bytes 524320 | tf_op jit(solution)/shard_map/ppermute | solution.py:127
  28.6 2.0 %copy.89 = bf16[128,2048]{0,1:T(8,128)(2,1)} copy(bf16[128,2048]{1,0:T(8,128)(2,1)} %collective-permute-done.3) | data formatting | bytes 1048576 | tf_op jit(solution)/shard_map/ppermute | solution.py:127
  30.6 26.1 %collective-permute-done.4 = bf16[128,2048]{1,0:T(8,128)(2,1)} collective-permute-done((bf16[128,2048]{1,0:T(8,128)(2,1)}, bf16[128,2048]{1,0:T(8,128)(2,1)}, u32[]{:S(2)}, u32[]{:S(2)}) %collective-permute-start.4) | collective-permute-done | bytes 524320 | tf_op jit(solution)/shard_map/ppermute | solution.py:127
  58.0 3.0 %fusion.220 = f32[128,308]{0,1:T(8,128)S(1)} fusion(bf16[128,4096]{0,1:T(8,128)(2,1)} %collective-permute-done, bf16[4096,308]{0,1:T(8,128)(2,1)} %param.12), kind=kOutput, calls=%fused_computation.291 | convolution fusion | flops 322961408 | bytes 3729408 | tf_op jit(solution)/shard_map/dot_general | solution.py:56
  61.1 2.1 %fusion.221 = f32[128,308]{0,1:T(8,128)S(1)} fusion(bf16[128,4096]{1,0:T(8,128)(2,1)} %collective-permute-done.1, bf16[4096,308]{0,1:T(8,128)(2,1)S(1)} %copy-done.2), kind=kOutput, calls=%fused_computation.292 | convolution fusion | flops 322961408 | bytes 3729408 | tf_op jit(solution)/shard_map/dot_general | solution.py:52
  63.2 2.1 %multiply_convert_fusion.3 = (bf16[128,308]{0,1:T(8,128)(2,1)S(1)}, bf16[128,308]{0,1:T(8,128)(2,1)S(1)}, bf16[128,308]{0,1:T(8,128)(2,1)S(1)}) fusion(f32[128,308]{0,1:T(8,128)S(1)} %fusion.220, f32[128,308]{0,1:T(8,128)S(1)} %fusion.221, bf16[128,4096]{1,0:T(8,128)(2,1)} %collective-permute-done.1, bf16[4096,308]{0,1:T(8,128)(2,1)S(1)} %copy-done), kind=kOutput, calls=%fused_computation.105 | convolution fusion | flops 323552768 | bytes 4123648 | tf_op jit(solution)/shard_map/dot_general | solution.py:51
  66.7 2.9 %collective-permute-start.2 = (bf16[128,924]{0,1:T(8,128)(2,1)}, bf16[128,924]{0,1:T(8,128)(2,1)S(1)}, u32[]{:S(2)}, u32[]{:S(2)}) collective-permute-start(bf16[128,924]{0,1:T(8,128)(2,1)} %pad_maximum_fusion.1), channel_id=1, source_target_pairs={{0,384},{48,432},{96,480},{144,528},{192,576},{240,624},{288,672},... | collective-permute-start | bytes 709640 | tf_op jit(solution)/shard_map/ppermute | solution.py:62
  69.6 2.3 %copy.86 = bf16[128,4096]{0,1:T(8,128)(2,1)} copy(bf16[128,4096]{1,0:T(8,128)(2,1)} %collective-permute-done.1) | data formatting | bytes 2097152 | tf_op jit(solution)/shard_map/ppermute | solution.py:13
  74.1 2.3 %collective-permute-done.2 = bf16[128,924]{0,1:T(8,128)(2,1)S(1)} collective-permute-done((bf16[128,924]{0,1:T(8,128)(2,1)}, bf16[128,924]{0,1:T(8,128)(2,1)S(1)}, u32[]{:S(2)}, u32[]{:S(2)}) %collective-permute-start.2) | collective-permute-done | bytes 236576 | tf_op jit(solution)/shard_map/ppermute | solution.py:62
  83.0 2.4 %collective-permute-start.6 = (bf16[924,128]{1,0:T(8,128)(2,1)S(1)}, bf16[924,128]{1,0:T(8,128)(2,1)S(1)}, u32[]{:S(2)}, u32[]{:S(2)}) collective-permute-start(bf16[924,128]{1,0:T(8,128)(2,1)S(1)} %pad_maximum_fusion.3), channel_id=1, source_target_pairs={{0,336},{48,0},{96,48},{144,96},{192,144},{240,192},{288,240},{336... | collective-permute-start | bytes 709640 | tf_op jit(solution)/shard_map/ppermute | solution.py:101
  85.4 4.7 %collective-permute-start.5 = (bf16[924,128]{1,0:T(8,128)(2,1)S(1)}, bf16[924,128]{1,0:T(8,128)(2,1)S(1)}, u32[]{:S(2)}, u32[]{:S(2)}) collective-permute-start(bf16[924,128]{1,0:T(8,128)(2,1)S(1)} %pad_maximum_fusion.2), channel_id=1, source_target_pairs={{0,48},{48,96},{96,144},{144,192},{192,240},{240,288},{288,336},{3... | collective-permute-start | bytes 709640 | tf_op jit(solution)/shard_map/ppermute | solution.py:100
  91.1 3.2 %collective-permute-done.6 = bf16[924,128]{1,0:T(8,128)(2,1)S(1)} collective-permute-done((bf16[924,128]{1,0:T(8,128)(2,1)S(1)}, bf16[924,128]{1,0:T(8,128)(2,1)S(1)}, u32[]{:S(2)}, u32[]{:S(2)}) %collective-permute-start.6) | collective-permute-done | bytes 236576 | tf_op jit(solution)/shard_map/ppermute | solution.py:101
  95.8 5.6 %collective-permute-start.8 = (bf16[924,128]{1,0:T(8,128)(2,1)S(1)}, bf16[924,128]{1,0:T(8,128)(2,1)S(1)}, u32[]{:S(2)}, u32[]{:S(2)}) collective-permute-start(bf16[924,128]{1,0:T(8,128)(2,1)S(1)} %fusion.1), channel_id=1, source_target_pairs={{0,48},{48,96},{96,144},{144,192},{192,240},{240,288},{288,336},{3... | collective-permute-start | bytes 709640 | tf_op jit(solution)/shard_map/ppermute | solution.py:100
  101.7 2.1 %collective-permute-start.14 = (bf16[924,128]{1,0:T(8,128)(2,1)S(1)}, bf16[924,128]{1,0:T(8,128)(2,1)S(1)}, u32[]{:S(2)}, u32[]{:S(2)}) collective-permute-start(bf16[924,128]{1,0:T(8,128)(2,1)S(1)} %fusion.7), channel_id=1, source_target_pairs={{0,336},{48,0},{96,48},{144,96},{192,144},{240,192},{288,240},{336... | collective-permute-start | bytes 709640 | tf_op jit(solution)/shard_map/ppermute | solution.py:101
  103.8 3.1 %collective-permute-done.8 = bf16[924,128]{1,0:T(8,128)(2,1)S(1)} collective-permute-done((bf16[924,128]{1,0:T(8,128)(2,1)S(1)}, bf16[924,128]{1,0:T(8,128)(2,1)S(1)}, u32[]{:S(2)}, u32[]{:S(2)}) %collective-permute-start.8) | collective-permute-done | bytes 236576 | tf_op jit(solution)/shard_map/ppermute | solution.py:100
  106.9 5.6 %collective-permute-start.9 = (bf16[924,128]{1,0:T(8,128)(2,1)S(1)}, bf16[924,128]{1,0:T(8,128)(2,1)S(1)}, u32[]{:S(2)}, u32[]{:S(2)}) collective-permute-start(bf16[924,128]{1,0:T(8,128)(2,1)S(1)} %fusion.2), channel_id=1, source_target_pairs={{0,48},{48,96},{96,144},{144,192},{192,240},{240,288},{288,336},{3... | collective-permute-start | bytes 709640 | tf_op jit(solution)/shard_map/ppermute | solution.py:100
  115.1 2.0 %collective-permute-done.9 = bf16[924,128]{1,0:T(8,128)(2,1)S(1)} collective-permute-done((bf16[924,128]{1,0:T(8,128)(2,1)S(1)}, bf16[924,128]{1,0:T(8,128)(2,1)S(1)}, u32[]{:S(2)}, u32[]{:S(2)}) %collective-permute-start.9) | collective-permute-done | bytes 236576 | tf_op jit(solution)/shard_map/ppermute | solution.py:100
  117.2 5.6 %collective-permute-start.10 = (bf16[924,128]{1,0:T(8,128)(2,1)S(1)}, bf16[924,128]{1,0:T(8,128)(2,1)S(1)}, u32[]{:S(2)}, u32[]{:S(2)}) collective-permute-start(bf16[924,128]{1,0:T(8,128)(2,1)S(1)} %fusion.3), channel_id=1, source_target_pairs={{0,48},{48,96},{96,144},{144,192},{192,240},{240,288},{288,336},{3... | collective-permute-start | bytes 709640 | tf_op jit(solution)/shard_map/ppermute | solution.py:100
  126.5 5.6 %collective-permute-start.11 = (bf16[924,128]{1,0:T(8,128)(2,1)S(1)}, bf16[924,128]{1,0:T(8,128)(2,1)S(1)}, u32[]{:S(2)}, u32[]{:S(2)}) collective-permute-start(bf16[924,128]{1,0:T(8,128)(2,1)S(1)} %fusion.4), channel_id=1, source_target_pairs={{0,48},{48,96},{96,144},{144,192},{192,240},{240,288},{288,336},{3... | collective-permute-start | bytes 709640 | tf_op jit(solution)/shard_map/ppermute | solution.py:100
  132.9 3.5 %collective-permute-start.7 = (bf16[128,4096]{1,0:T(8,128)(2,1)S(1)}, bf16[128,4096]{1,0:T(8,128)(2,1)S(1)}, u32[]{:S(2)}, u32[]{:S(2)}) collective-permute-start(bf16[128,4096]{1,0:T(8,128)(2,1)S(1)} %fusion), channel_id=1, source_target_pairs={{1,0},{2,1},{3,2},{4,3},{5,4},{6,5},{7,6},{8,7},{9,8},{10,9},{11,1... | collective-permute-start | bytes 3145736 | tf_op jit(solution)/shard_map/ppermute | solution.py:13
  138.4 5.1 %collective-permute-start.12 = (bf16[924,128]{1,0:T(8,128)(2,1)S(1)}, bf16[924,128]{1,0:T(8,128)(2,1)S(1)}, u32[]{:S(2)}, u32[]{:S(2)}) collective-permute-start(bf16[924,128]{1,0:T(8,128)(2,1)S(1)} %fusion.5), channel_id=1, source_target_pairs={{0,48},{48,96},{96,144},{144,192},{192,240},{240,288},{288,336},{3... | collective-permute-start | bytes 709640 | tf_op jit(solution)/shard_map/ppermute | solution.py:100
  143.8 2.4 %collective-permute-done.17 = bf16[924,128]{1,0:T(8,128)(2,1)S(1)} collective-permute-done((bf16[924,128]{1,0:T(8,128)(2,1)S(1)}, bf16[924,128]{1,0:T(8,128)(2,1)S(1)}, u32[]{:S(2)}, u32[]{:S(2)}) %collective-permute-start.17) | collective-permute-done | bytes 236576 | tf_op jit(solution)/shard_map/ppermute | solution.py:101
  148.2 5.1 %collective-permute-start.13 = (bf16[924,128]{1,0:T(8,128)(2,1)S(1)}, bf16[924,128]{1,0:T(8,128)(2,1)S(1)}, u32[]{:S(2)}, u32[]{:S(2)}) collective-permute-start(bf16[924,128]{1,0:T(8,128)(2,1)S(1)} %fusion.6), channel_id=1, source_target_pairs={{0,48},{48,96},{96,144},{144,192},{192,240},{240,288},{288,336},{3... | collective-permute-start | bytes 709640 | tf_op jit(solution)/shard_map/ppermute | solution.py:100
  157.5 7.2 %collective-permute-done.19 = bf16[924,128]{1,0:T(8,128)(2,1)S(1)} collective-permute-done((bf16[924,128]{1,0:T(8,128)(2,1)S(1)}, bf16[924,128]{1,0:T(8,128)(2,1)S(1)}, u32[]{:S(2)}, u32[]{:S(2)}) %collective-permute-start.19) | collective-permute-done | bytes 236576 | tf_op jit(solution)/shard_map/ppermute | solution.py:101
  165.9 2.3 %copy.126 = bf16[1,1,128,4096]{3,2,1,0:T(8,128)(2,1)} copy(bf16[1,1,128,4096]{3,2,1,0:T(8,128)(2,1)} %bitcast.246) | data formatting | bytes 2097152
  (104 shorter events, 34.3 us)
Async XLA Ops:
  0.6 62.6 %copy-start = (bf16[4096,308]{0,1:T(8,128)(2,1)S(1)}, bf16[4096,308]{0,1:T(8,128)(2,1)}, u32[]{:S(2)}) copy-start(bf16[4096,308]{0,1:T(8,128)(2,1)} %param.10) | copy-start | bytes 7569412
  0.6 11.9 %copy-start.8 = (s32[1,1,128]{2,1,0:T(1,128)S(1)}, s32[1,1,128]{2,1,0:T(1,128)}, u32[]{:S(2)}) copy-start(s32[1,1,128]{2,1,0:T(1,128)} %param.14) | copy-start | bytes 1540
  0.7 12.0 %copy-start.9 = (s32[1,1,4]{2,1,0:T(1,128)S(1)}, s32[1,1,4]{2,1,0:T(1,128)}, u32[]{:S(2)}) copy-start(s32[1,1,4]{2,1,0:T(1,128)} %param.15) | copy-start | bytes 52
  5.2 23.4 %collective-permute-start.3 = (bf16[128,2048]{1,0:T(8,128)(2,1)}, bf16[128,2048]{1,0:T(8,128)(2,1)}, u32[]{:S(2)}, u32[]{:S(2)}) collective-permute-start(bf16[128,2048]{1,0:T(8,128)(2,1)} %bitcast.248), channel_id=1, source_target_pairs={{0,385},{1,386},{2,387},{3,388},{4,389},{5,390},{6,391},{7,392},{8... | collective-permute-start | bytes 1572872 | tf_op jit(solution)/shard_map/ppermute | solution.py:127
  9.5 51.5 %collective-permute-start.1 = (bf16[128,4096]{1,0:T(8,128)(2,1)}, bf16[128,4096]{1,0:T(8,128)(2,1)}, u32[]{:S(2)}, u32[]{:S(2)}) collective-permute-start(bf16[128,4096]{1,0:T(8,128)(2,1)} %bitcast.245), channel_id=1, source_target_pairs={{47,0},{0,1},{1,2},{2,3},{3,4},{4,5},{5,6},{6,7},{7,8},{8,9},{9,10... | collective-permute-start | bytes 3145736 | tf_op jit(solution)/shard_map/ppermute | solution.py:13
  15.0 4.7 %copy-start.4 = (bf16[1,1,128,4096]{2,3,1,0:T(8,128)(2,1)S(1)}, bf16[1,1,128,4096]{2,3,1,0:T(8,128)(2,1)}, u32[]{:S(2)}) copy-start(bf16[1,1,128,4096]{2,3,1,0:T(8,128)(2,1)} %copy.85) | copy-start | bytes 3145732
  17.5 40.5 %collective-permute-start = (bf16[128,4096]{0,1:T(8,128)(2,1)}, bf16[128,4096]{0,1:T(8,128)(2,1)}, u32[]{:S(2)}, u32[]{:S(2)}) collective-permute-start(bf16[128,4096]{0,1:T(8,128)(2,1)} %fusion.249), channel_id=1, source_target_pairs={{47,0},{0,1},{1,2},{2,3},{3,4},{4,5},{5,6},{6,7},{7,8},{8,9},{9,10... | collective-permute-start | bytes 3145736 | tf_op jit(solution)/shard_map/ppermute | solution.py:13
  21.0 35.7 %collective-permute-start.4 = (bf16[128,2048]{1,0:T(8,128)(2,1)}, bf16[128,2048]{1,0:T(8,128)(2,1)}, u32[]{:S(2)}, u32[]{:S(2)}) collective-permute-start(bf16[128,2048]{1,0:T(8,128)(2,1)} %bitcast.249), channel_id=1, source_target_pairs={{0,385},{1,386},{2,387},{3,388},{4,389},{5,390},{6,391},{7,392},{8... | collective-permute-start | bytes 1572872 | tf_op jit(solution)/shard_map/ppermute | solution.py:127
  58.0 3.1 %copy-start.2 = (bf16[4096,308]{0,1:T(8,128)(2,1)S(1)}, bf16[4096,308]{0,1:T(8,128)(2,1)}, u32[]{:S(2)}) copy-start(bf16[4096,308]{0,1:T(8,128)(2,1)} %param.11) | copy-start | bytes 7569412
  65.3 0.6 copy-start.6
  66.7 9.7 %collective-permute-start.2 = (bf16[128,924]{0,1:T(8,128)(2,1)}, bf16[128,924]{0,1:T(8,128)(2,1)S(1)}, u32[]{:S(2)}, u32[]{:S(2)}) collective-permute-start(bf16[128,924]{0,1:T(8,128)(2,1)} %pad_maximum_fusion.1), channel_id=1, source_target_pairs={{0,384},{48,432},{96,480},{144,528},{192,576},{240,624},{288,672},... | collective-permute-start | bytes 709640 | tf_op jit(solution)/shard_map/ppermute | solution.py:62
  71.8 5.5 %copy-start.1 = (bf16[128,2048]{0,1:T(8,128)(2,1)S(1)}, bf16[128,2048]{0,1:T(8,128)(2,1)}, u32[]{:S(2)}) copy-start(bf16[128,2048]{0,1:T(8,128)(2,1)} %copy.89) | copy-start | bytes 1572868
  73.0 4.9 %copy-start.7 = (bf16[128,308]{0,1:T(8,128)(2,1)S(1)}, bf16[128,308]{0,1:T(8,128)(2,1)}, u32[]{:S(2)}) copy-start(bf16[128,308]{0,1:T(8,128)(2,1)} %copy-done.6) | copy-start | bytes 236548
  83.0 11.3 %collective-permute-start.6 = (bf16[924,128]{1,0:T(8,128)(2,1)S(1)}, bf16[924,128]{1,0:T(8,128)(2,1)S(1)}, u32[]{:S(2)}, u32[]{:S(2)}) collective-permute-start(bf16[924,128]{1,0:T(8,128)(2,1)S(1)} %pad_maximum_fusion.3), channel_id=1, source_target_pairs={{0,336},{48,0},{96,48},{144,96},{192,144},{240,192},{288,240},{336... | collective-permute-start | bytes 709640 | tf_op jit(solution)/shard_map/ppermute | solution.py:101
  85.4 10.4 %collective-permute-start.5 = (bf16[924,128]{1,0:T(8,128)(2,1)S(1)}, bf16[924,128]{1,0:T(8,128)(2,1)S(1)}, u32[]{:S(2)}, u32[]{:S(2)}) collective-permute-start(bf16[924,128]{1,0:T(8,128)(2,1)S(1)} %pad_maximum_fusion.2), channel_id=1, source_target_pairs={{0,48},{48,96},{96,144},{144,192},{192,240},{240,288},{288,336},{3... | collective-permute-start | bytes 709640 | tf_op jit(solution)/shard_map/ppermute | solution.py:100
  95.8 11.0 %collective-permute-start.8 = (bf16[924,128]{1,0:T(8,128)(2,1)S(1)}, bf16[924,128]{1,0:T(8,128)(2,1)S(1)}, u32[]{:S(2)}, u32[]{:S(2)}) collective-permute-start(bf16[924,128]{1,0:T(8,128)(2,1)S(1)} %fusion.1), channel_id=1, source_target_pairs={{0,48},{48,96},{96,144},{144,192},{192,240},{240,288},{288,336},{3... | collective-permute-start | bytes 709640 | tf_op jit(solution)/shard_map/ppermute | solution.py:100
  101.7 21.1 %copy-start.3 = (bf16[4096,308]{0,1:T(8,128)(2,1)S(1)}, bf16[4096,308]{0,1:T(8,128)(2,1)}, u32[]{:S(2)}) copy-start(bf16[4096,308]{0,1:T(8,128)(2,1)} %param.11) | copy-start | bytes 7569412
  101.7 11.4 %collective-permute-start.14 = (bf16[924,128]{1,0:T(8,128)(2,1)S(1)}, bf16[924,128]{1,0:T(8,128)(2,1)S(1)}, u32[]{:S(2)}, u32[]{:S(2)}) collective-permute-start(bf16[924,128]{1,0:T(8,128)(2,1)S(1)} %fusion.7), channel_id=1, source_target_pairs={{0,336},{48,0},{96,48},{144,96},{192,144},{240,192},{288,240},{336... | collective-permute-start | bytes 709640 | tf_op jit(solution)/shard_map/ppermute | solution.py:101
  106.9 10.2 %collective-permute-start.9 = (bf16[924,128]{1,0:T(8,128)(2,1)S(1)}, bf16[924,128]{1,0:T(8,128)(2,1)S(1)}, u32[]{:S(2)}, u32[]{:S(2)}) collective-permute-start(bf16[924,128]{1,0:T(8,128)(2,1)S(1)} %fusion.2), channel_id=1, source_target_pairs={{0,48},{48,96},{96,144},{144,192},{192,240},{240,288},{288,336},{3... | collective-permute-start | bytes 709640 | tf_op jit(solution)/shard_map/ppermute | solution.py:100
  113.2 10.4 %collective-permute-start.15 = (bf16[924,128]{1,0:T(8,128)(2,1)S(1)}, bf16[924,128]{1,0:T(8,128)(2,1)S(1)}, u32[]{:S(2)}, u32[]{:S(2)}) collective-permute-start(bf16[924,128]{1,0:T(8,128)(2,1)S(1)} %fusion.8), channel_id=1, source_target_pairs={{0,336},{48,0},{96,48},{144,96},{192,144},{240,192},{288,240},{336... | collective-permute-start | bytes 709640 | tf_op jit(solution)/shard_map/ppermute | solution.py:101
  117.2 9.2 %collective-permute-start.10 = (bf16[924,128]{1,0:T(8,128)(2,1)S(1)}, bf16[924,128]{1,0:T(8,128)(2,1)S(1)}, u32[]{:S(2)}, u32[]{:S(2)}) collective-permute-start(bf16[924,128]{1,0:T(8,128)(2,1)S(1)} %fusion.3), channel_id=1, source_target_pairs={{0,48},{48,96},{96,144},{144,192},{192,240},{240,288},{288,336},{3... | collective-permute-start | bytes 709640 | tf_op jit(solution)/shard_map/ppermute | solution.py:100
  123.7 12.7 %collective-permute-start.16 = (bf16[924,128]{1,0:T(8,128)(2,1)S(1)}, bf16[924,128]{1,0:T(8,128)(2,1)S(1)}, u32[]{:S(2)}, u32[]{:S(2)}) collective-permute-start(bf16[924,128]{1,0:T(8,128)(2,1)S(1)} %fusion.9), channel_id=1, source_target_pairs={{0,336},{48,0},{96,48},{144,96},{192,144},{240,192},{288,240},{336... | collective-permute-start | bytes 709640 | tf_op jit(solution)/shard_map/ppermute | solution.py:101
  126.5 11.9 %collective-permute-start.11 = (bf16[924,128]{1,0:T(8,128)(2,1)S(1)}, bf16[924,128]{1,0:T(8,128)(2,1)S(1)}, u32[]{:S(2)}, u32[]{:S(2)}) collective-permute-start(bf16[924,128]{1,0:T(8,128)(2,1)S(1)} %fusion.4), channel_id=1, source_target_pairs={{0,48},{48,96},{96,144},{144,192},{192,240},{240,288},{288,336},{3... | collective-permute-start | bytes 709640 | tf_op jit(solution)/shard_map/ppermute | solution.py:100
  132.9 20.7 %collective-permute-start.7 = (bf16[128,4096]{1,0:T(8,128)(2,1)S(1)}, bf16[128,4096]{1,0:T(8,128)(2,1)S(1)}, u32[]{:S(2)}, u32[]{:S(2)}) collective-permute-start(bf16[128,4096]{1,0:T(8,128)(2,1)S(1)} %fusion), channel_id=1, source_target_pairs={{1,0},{2,1},{3,2},{4,3},{5,4},{6,5},{7,6},{8,7},{9,8},{10,9},{11,1... | collective-permute-start | bytes 3145736 | tf_op jit(solution)/shard_map/ppermute | solution.py:13
  136.4 9.7 %collective-permute-start.17 = (bf16[924,128]{1,0:T(8,128)(2,1)S(1)}, bf16[924,128]{1,0:T(8,128)(2,1)S(1)}, u32[]{:S(2)}, u32[]{:S(2)}) collective-permute-start(bf16[924,128]{1,0:T(8,128)(2,1)S(1)} %fusion.10), channel_id=1, source_target_pairs={{0,336},{48,0},{96,48},{144,96},{192,144},{240,192},{288,240},{336... | collective-permute-start | bytes 709640 | tf_op jit(solution)/shard_map/ppermute | solution.py:101
  138.4 9.7 %collective-permute-start.12 = (bf16[924,128]{1,0:T(8,128)(2,1)S(1)}, bf16[924,128]{1,0:T(8,128)(2,1)S(1)}, u32[]{:S(2)}, u32[]{:S(2)}) collective-permute-start(bf16[924,128]{1,0:T(8,128)(2,1)S(1)} %fusion.5), channel_id=1, source_target_pairs={{0,48},{48,96},{96,144},{144,192},{192,240},{240,288},{288,336},{3... | collective-permute-start | bytes 709640 | tf_op jit(solution)/shard_map/ppermute | solution.py:100
  146.2 9.2 %collective-permute-start.18 = (bf16[924,128]{1,0:T(8,128)(2,1)S(1)}, bf16[924,128]{1,0:T(8,128)(2,1)S(1)}, u32[]{:S(2)}, u32[]{:S(2)}) collective-permute-start(bf16[924,128]{1,0:T(8,128)(2,1)S(1)} %fusion.11), channel_id=1, source_target_pairs={{0,336},{48,0},{96,48},{144,96},{192,144},{240,192},{288,240},{336... | collective-permute-start | bytes 709640 | tf_op jit(solution)/shard_map/ppermute | solution.py:101
  148.2 9.2 %collective-permute-start.13 = (bf16[924,128]{1,0:T(8,128)(2,1)S(1)}, bf16[924,128]{1,0:T(8,128)(2,1)S(1)}, u32[]{:S(2)}, u32[]{:S(2)}) collective-permute-start(bf16[924,128]{1,0:T(8,128)(2,1)S(1)} %fusion.6), channel_id=1, source_target_pairs={{0,48},{48,96},{96,144},{144,192},{192,240},{240,288},{288,336},{3... | collective-permute-start | bytes 709640 | tf_op jit(solution)/shard_map/ppermute | solution.py:100
  153.6 11.2 %copy-start.5 = (bf16[128,4096]{1,0:T(8,128)(2,1)}, bf16[128,4096]{1,0:T(8,128)(2,1)S(1)}, u32[]{:S(2)}) copy-start(bf16[128,4096]{1,0:T(8,128)(2,1)S(1)} %collective-permute-done.7) | copy-start | bytes 3145732
  155.5 9.2 %collective-permute-start.19 = (bf16[924,128]{1,0:T(8,128)(2,1)S(1)}, bf16[924,128]{1,0:T(8,128)(2,1)S(1)}, u32[]{:S(2)}, u32[]{:S(2)}) collective-permute-start(bf16[924,128]{1,0:T(8,128)(2,1)S(1)} %fusion.12), channel_id=1, source_target_pairs={{0,336},{48,0},{96,48},{144,96},{192,144},{240,192},{288,240},{336... | collective-permute-start | bytes 709640 | tf_op jit(solution)/shard_map/ppermute | solution.py:101

commit v6 on v5

--- a/solution.py
+++ b/solution.py
@@ -63,6 +63,7 @@
     mixed_all = jnp.concatenate([mixed, mixed_peer], axis=0)
     tok_all = jnp.concatenate([tok_mine, tok_peer], axis=0)
     grad_all = jnp.concatenate([grad_mine, grad_peer], axis=0)
+
     def late(d_gate, d_up):
         return (contract_cols(d_gate, w_gate) + contract_cols(d_up, w_up)).astype(jnp.bfloat16)
 
@@ -108,7 +109,7 @@
     return jnp.transpose(total, (0, 2, 1)), late_out
 
 
-def shards(tokens, cotangent, gate_weight, up_weight, down_weight, counts, seg_ids, pair_side):
+def shards_body(tokens, cotangent, gate_weight, up_weight, down_weight, counts, seg_ids, pair_side):
     weights = token_weights(counts, seg_ids, pair_side)
     upstream = (cotangent.astype(jnp.float32) * weights[..., None]).astype(jnp.bfloat16)
     width = tokens.shape[-1]
@@ -124,6 +125,7 @@
     diagonal = [
         (d * nb + j, ((d + ny) % n) * nb + (j + 1) % nb) for d in range(n) for j in range(nb)
     ]
+    other, moved_rows, moved_grads = lax.optimization_barrier((other, moved_rows, moved_grads))
     tok_peer, grad_peer = lax.ppermute(other, ("dp", "blk"), diagonal)
     grad_moved, panel_grads = backward_core(
         moved_rows, moved_grads, tok_peer, grad_peer, gate_weight, up_weight, down_weight
@@ -144,7 +146,7 @@
         P("dp", "blk", None),
     )
     return jax.shard_map(
-        shards,
+        shards_body,
         mesh=mesh,
         in_specs=placed,
         out_specs=(P("dp", "blk", None, None), P(None, "dp", "blk")),

time: 169 us -> 184 us (1.089)
  the two profiles are of different devices: /device:TPU:24 before, /device:TPU:28 now
where the time goes in v6:
time: 184 us; the launch traced here: 183 us
  waiting for transfers between devices  67.1 us (36%)
  starting transfers between devices  65.1 us (35%)
  matrix products  20.9 us (11%)
  local copies, waits for them, and re-layouts  19.6 us (11%)
  other arithmetic  7.71 us (4%)
  between operations  2.22 us (1%)
    ppermute x7, starting transfers between devices, reduce_over_y(): recv_f = lax.ppermute(acc_f.astype(jnp.bfloat16), 'dp', fwd)  37.5 us
    ppermute x3, waiting for transfers between devices, shifted(): return lax.ppermute(block, axis, route)  26.7 us
    ppermute x7, waiting for transfers between devices, reduce_over_y(): recv_b = lax.ppermute(acc_b.astype(jnp.bfloat16), 'dp', bwd)  16.5 us
    ppermute x7, starting transfers between devices, reduce_over_y(): recv_b = lax.ppermute(acc_b.astype(jnp.bfloat16), 'dp', bwd)  14 us
    ppermute x2, waiting for transfers between devices, shards_body(): tok_peer, grad_peer = lax.ppermute(other, ('dp', 'blk'), diagonal)  13 us
    dot_general x32, matrix products, contract_rows(): lax.dot_general(left, right, (((0,), (0,)), ((), ())), preferred_element_...  12 us
    ppermute x7, waiting for transfers between devices, reduce_over_y(): recv_f = lax.ppermute(acc_f.astype(jnp.bfloat16), 'dp', fwd)  10 us
    unnamed x35, local copies, waits for them, and re-layouts  7.12 us
  transfers between devices with their start and end apart: 20, of which 14 were waited for; matrix products, arithmetic and copies ran while one was open for 10% of the time, Pallas kernels for 0%

profile of v6, /device:TPU:28, one launch (start us, length us, event | category | flops | bytes accessed | tf_op | source)
XLA Modules:
  0.0 182.6 jit_solution(16757917240833066006)
XLA Ops:
  3.6 2.3 %copy.87 = bf16[1,1,128,4096]{2,3,1,0:T(8,128)(2,1)} copy(bf16[1,1,128,4096]{3,2,1,0:T(8,128)(2,1)} %param.9) | data formatting | bytes 2097152 | tf_op args[1]
  5.9 2.4 %fusion.249 = bf16[128,4096]{0,1:T(8,128)(2,1)} fusion(f32[128]{0:T(128)S(1)} %select_reduce_fusion, bf16[1,1,128,4096]{2,3,1,0:T(8,128)(2,1)} %copy.87), kind=kLoop, calls=%fused_computation.294 | loop fusion | flops 1572864 | bytes 2097664 | tf_op jit(solution)/shard_map/reshape | solution.py:117
  10.2 3.2 %collective-permute-start = (bf16[128,4096]{1,0:T(8,128)(2,1)}, bf16[128,4096]{1,0:T(8,128)(2,1)}, u32[]{:S(2)}, u32[]{:S(2)}) collective-permute-start(bf16[128,4096]{1,0:T(8,128)(2,1)} %bitcast.245), channel_id=1, source_target_pairs={{47,0},{0,1},{1,2},{2,3},{3,4},{4,5},{5,6},{6,7},{7,8},{8,9},{9,10... | collective-permute-start | bytes 3145736 | tf_op jit(solution)/shard_map/ppermute | solution.py:13
  13.4 2.3 %copy.85 = bf16[1,1,128,4096]{2,3,1,0:T(8,128)(2,1)} copy(bf16[1,1,128,4096]{3,2,1,0:T(8,128)(2,1)} %param.8) | data formatting | bytes 2097152 | tf_op args[0]
  20.3 15.4 %collective-permute-done.1 = bf16[128,4096]{0,1:T(8,128)(2,1)} collective-permute-done((bf16[128,4096]{0,1:T(8,128)(2,1)}, bf16[128,4096]{0,1:T(8,128)(2,1)}, u32[]{:S(2)}, u32[]{:S(2)}) %collective-permute-start.1) | collective-permute-done | bytes 1048608 | tf_op jit(solution)/shard_map/ppermute | solution.py:13
  35.7 11.2 %collective-permute-done = bf16[128,4096]{1,0:T(8,128)(2,1)} collective-permute-done((bf16[128,4096]{1,0:T(8,128)(2,1)}, bf16[128,4096]{1,0:T(8,128)(2,1)}, u32[]{:S(2)}, u32[]{:S(2)}) %collective-permute-start) | collective-permute-done | bytes 1048608 | tf_op jit(solution)/shard_map/ppermute | solution.py:13
  47.0 2.3 %copy.89 = bf16[128,4096]{0,1:T(8,128)(2,1)} copy(bf16[128,4096]{1,0:T(8,128)(2,1)} %collective-permute-done) | data formatting | bytes 2097152 | tf_op jit(solution)/shard_map/optimization_barrier | solution.py:128
  49.2 3.0 %fusion.221 = f32[128,308]{0,1:T(8,128)S(1)} fusion(bf16[128,4096]{1,0:T(8,128)(2,1)} %collective-permute-done, bf16[4096,308]{0,1:T(8,128)(2,1)} %param.11), kind=kOutput, calls=%fused_computation.292 | convolution fusion | flops 322961408 | bytes 3729408 | tf_op jit(solution)/shard_map/dot_general | solution.py:52
  52.3 2.0 %fusion.220 = f32[128,308]{0,1:T(8,128)S(1)} fusion(bf16[128,4096]{0,1:T(8,128)(2,1)} %collective-permute-done.1, bf16[4096,308]{0,1:T(8,128)(2,1)S(1)} %copy-done.6), kind=kOutput, calls=%fused_computation.291 | convolution fusion | flops 322961408 | bytes 3729408 | tf_op jit(solution)/shard_map/dot_general | solution.py:56
  54.3 2.2 %multiply_convert_fusion.3 = (bf16[128,308]{0,1:T(8,128)(2,1)S(1)}, bf16[128,308]{0,1:T(8,128)(2,1)S(1)}, bf16[128,308]{0,1:T(8,128)(2,1)S(1)}) fusion(f32[128,308]{0,1:T(8,128)S(1)} %fusion.220, f32[128,308]{0,1:T(8,128)S(1)} %fusion.221, bf16[128,4096]{1,0:T(8,128)(2,1)} %collective-permute-done, bf16[4096,308]{0,1:T(8,128)(2,1)S(1)} %copy-done), kind=kOutput, calls=%fused_computation.105 | convolution fusion | flops 323552768 | bytes 4123648 | tf_op jit(solution)/shard_map/dot_general | solution.py:51
  56.6 2.7 %collective-permute-start.2 = (bf16[128,924]{0,1:T(8,128)(2,1)S(1)}, bf16[128,924]{0,1:T(8,128)(2,1)S(1)}, u32[]{:S(2)}, u32[]{:S(2)}) collective-permute-start(bf16[128,924]{0,1:T(8,128)(2,1)S(1)} %pad_maximum_fusion.1), channel_id=1, source_target_pairs={{0,384},{48,432},{96,480},{144,528},{192,576},{240,624},{288,672},... | collective-permute-start | bytes 709640 | tf_op jit(solution)/shard_map/ppermute | solution.py:62
  61.3 1.9 %collective-permute-start.4 = (bf16[128,2048]{1,0:T(8,128)(2,1)}, bf16[128,2048]{1,0:T(8,128)(2,1)}, u32[]{:S(2)}, u32[]{:S(2)}) collective-permute-start(bf16[128,2048]{1,0:T(8,128)(2,1)} %bitcast.7), channel_id=1, source_target_pairs={{0,385},{1,386},{2,387},{3,388},{4,389},{5,390},{6,391},{7,392},{8... | collective-permute-start | bytes 1572872 | tf_op jit(solution)/shard_map/ppermute | solution.py:129
  66.9 9.1 %collective-permute-done.3 = bf16[128,2048]{1,0:T(8,128)(2,1)} collective-permute-done((bf16[128,2048]{1,0:T(8,128)(2,1)S(1)}, bf16[128,2048]{1,0:T(8,128)(2,1)}, u32[]{:S(2)}, u32[]{:S(2)}) %collective-permute-start.3) | collective-permute-done | bytes 524320 | tf_op jit(solution)/shard_map/ppermute | solution.py:129
  76.0 2.1 %copy.124 = bf16[128,2048]{0,1:T(8,128)(2,1)} copy(bf16[128,2048]{1,0:T(8,128)(2,1)} %collective-permute-done.3) | data formatting | bytes 1048576 | tf_op jit(solution)/shard_map/concatenate | solution.py:64
  81.5 3.9 %collective-permute-done.4 = bf16[128,2048]{1,0:T(8,128)(2,1)} collective-permute-done((bf16[128,2048]{1,0:T(8,128)(2,1)}, bf16[128,2048]{1,0:T(8,128)(2,1)}, u32[]{:S(2)}, u32[]{:S(2)}) %collective-permute-start.4) | collective-permute-done | bytes 524320 | tf_op jit(solution)/shard_map/ppermute | solution.py:129
  85.4 2.0 %copy.125 = bf16[128,2048]{0,1:T(8,128)(2,1)} copy(bf16[128,2048]{1,0:T(8,128)(2,1)} %collective-permute-done.4) | data formatting | bytes 1048576 | tf_op jit(solution)/shard_map/concatenate | solution.py:65
  94.7 2.3 %collective-permute-start.6 = (bf16[924,128]{1,0:T(8,128)(2,1)S(1)}, bf16[924,128]{1,0:T(8,128)(2,1)S(1)}, u32[]{:S(2)}, u32[]{:S(2)}) collective-permute-start(bf16[924,128]{1,0:T(8,128)(2,1)S(1)} %pad_maximum_fusion.3), channel_id=1, source_target_pairs={{0,336},{48,0},{96,48},{144,96},{192,144},{240,192},{288,240},{336... | collective-permute-start | bytes 709640 | tf_op jit(solution)/shard_map/ppermute | solution.py:102
  97.1 4.7 %collective-permute-start.5 = (bf16[924,128]{1,0:T(8,128)(2,1)S(1)}, bf16[924,128]{1,0:T(8,128)(2,1)S(1)}, u32[]{:S(2)}, u32[]{:S(2)}) collective-permute-start(bf16[924,128]{1,0:T(8,128)(2,1)S(1)} %pad_maximum_fusion.2), channel_id=1, source_target_pairs={{0,48},{48,96},{96,144},{144,192},{192,240},{240,288},{288,336},{3... | collective-permute-start | bytes 709640 | tf_op jit(solution)/shard_map/ppermute | solution.py:101
  106.2 5.6 %collective-permute-start.8 = (bf16[924,128]{1,0:T(8,128)(2,1)S(1)}, bf16[924,128]{1,0:T(8,128)(2,1)S(1)}, u32[]{:S(2)}, u32[]{:S(2)}) collective-permute-start(bf16[924,128]{1,0:T(8,128)(2,1)S(1)} %fusion.1), channel_id=1, source_target_pairs={{0,48},{48,96},{96,144},{144,192},{192,240},{240,288},{288,336},{3... | collective-permute-start | bytes 709640 | tf_op jit(solution)/shard_map/ppermute | solution.py:101
  112.1 2.1 %collective-permute-start.14 = (bf16[924,128]{1,0:T(8,128)(2,1)S(1)}, bf16[924,128]{1,0:T(8,128)(2,1)S(1)}, u32[]{:S(2)}, u32[]{:S(2)}) collective-permute-start(bf16[924,128]{1,0:T(8,128)(2,1)S(1)} %fusion.7), channel_id=1, source_target_pairs={{0,336},{48,0},{96,48},{144,96},{192,144},{240,192},{288,240},{336... | collective-permute-start | bytes 709640 | tf_op jit(solution)/shard_map/ppermute | solution.py:102
  114.1 3.0 %collective-permute-done.8 = bf16[924,128]{1,0:T(8,128)(2,1)S(1)} collective-permute-done((bf16[924,128]{1,0:T(8,128)(2,1)S(1)}, bf16[924,128]{1,0:T(8,128)(2,1)S(1)}, u32[]{:S(2)}, u32[]{:S(2)}) %collective-permute-start.8) | collective-permute-done | bytes 236576 | tf_op jit(solution)/shard_map/ppermute | solution.py:101
  117.2 5.6 %collective-permute-start.9 = (bf16[924,128]{1,0:T(8,128)(2,1)S(1)}, bf16[924,128]{1,0:T(8,128)(2,1)S(1)}, u32[]{:S(2)}, u32[]{:S(2)}) collective-permute-start(bf16[924,128]{1,0:T(8,128)(2,1)S(1)} %fusion.2), channel_id=1, source_target_pairs={{0,48},{48,96},{96,144},{144,192},{192,240},{240,288},{288,336},{3... | collective-permute-start | bytes 709640 | tf_op jit(solution)/shard_map/ppermute | solution.py:101
  125.5 3.1 %collective-permute-done.9 = bf16[924,128]{1,0:T(8,128)(2,1)S(1)} collective-permute-done((bf16[924,128]{1,0:T(8,128)(2,1)S(1)}, bf16[924,128]{1,0:T(8,128)(2,1)S(1)}, u32[]{:S(2)}, u32[]{:S(2)}) %collective-permute-start.9) | collective-permute-done | bytes 236576 | tf_op jit(solution)/shard_map/ppermute | solution.py:101
  128.7 5.7 %collective-permute-start.10 = (bf16[924,128]{1,0:T(8,128)(2,1)S(1)}, bf16[924,128]{1,0:T(8,128)(2,1)S(1)}, u32[]{:S(2)}, u32[]{:S(2)}) collective-permute-start(bf16[924,128]{1,0:T(8,128)(2,1)S(1)} %fusion.3), channel_id=1, source_target_pairs={{0,48},{48,96},{96,144},{144,192},{192,240},{240,288},{288,336},{3... | collective-permute-start | bytes 709640 | tf_op jit(solution)/shard_map/ppermute | solution.py:101
  137.2 2.1 %collective-permute-done.10 = bf16[924,128]{1,0:T(8,128)(2,1)S(1)} collective-permute-done((bf16[924,128]{1,0:T(8,128)(2,1)S(1)}, bf16[924,128]{1,0:T(8,128)(2,1)S(1)}, u32[]{:S(2)}, u32[]{:S(2)}) %collective-permute-start.10) | collective-permute-done | bytes 236576 | tf_op jit(solution)/shard_map/ppermute | solution.py:101
  139.4 5.6 %collective-permute-start.11 = (bf16[924,128]{1,0:T(8,128)(2,1)S(1)}, bf16[924,128]{1,0:T(8,128)(2,1)S(1)}, u32[]{:S(2)}, u32[]{:S(2)}) collective-permute-start(bf16[924,128]{1,0:T(8,128)(2,1)S(1)} %fusion.4), channel_id=1, source_target_pairs={{0,48},{48,96},{96,144},{144,192},{192,240},{240,288},{288,336},{3... | collective-permute-start | bytes 709640 | tf_op jit(solution)/shard_map/ppermute | solution.py:101
  149.8 5.1 %collective-permute-start.12 = (bf16[924,128]{1,0:T(8,128)(2,1)S(1)}, bf16[924,128]{1,0:T(8,128)(2,1)S(1)}, u32[]{:S(2)}, u32[]{:S(2)}) collective-permute-start(bf16[924,128]{1,0:T(8,128)(2,1)S(1)} %fusion.5), channel_id=1, source_target_pairs={{0,48},{48,96},{96,144},{144,192},{192,240},{240,288},{288,336},{3... | collective-permute-start | bytes 709640 | tf_op jit(solution)/shard_map/ppermute | solution.py:101
  155.1 3.9 %collective-permute-done.17 = bf16[924,128]{1,0:T(8,128)(2,1)S(1)} collective-permute-done((bf16[924,128]{1,0:T(8,128)(2,1)S(1)}, bf16[924,128]{1,0:T(8,128)(2,1)S(1)}, u32[]{:S(2)}, u32[]{:S(2)}) %collective-permute-start.17) | collective-permute-done | bytes 236576 | tf_op jit(solution)/shard_map/ppermute | solution.py:102
  161.1 5.1 %collective-permute-start.13 = (bf16[924,128]{1,0:T(8,128)(2,1)S(1)}, bf16[924,128]{1,0:T(8,128)(2,1)S(1)}, u32[]{:S(2)}, u32[]{:S(2)}) collective-permute-start(bf16[924,128]{1,0:T(8,128)(2,1)S(1)} %fusion.6), channel_id=1, source_target_pairs={{0,48},{48,96},{96,144},{144,192},{192,240},{240,288},{288,336},{3... | collective-permute-start | bytes 709640 | tf_op jit(solution)/shard_map/ppermute | solution.py:101
  166.5 3.1 %collective-permute-done.18 = bf16[924,128]{1,0:T(8,128)(2,1)S(1)} collective-permute-done((bf16[924,128]{1,0:T(8,128)(2,1)S(1)}, bf16[924,128]{1,0:T(8,128)(2,1)S(1)}, u32[]{:S(2)}, u32[]{:S(2)}) %collective-permute-start.18) | collective-permute-done | bytes 236576 | tf_op jit(solution)/shard_map/ppermute | solution.py:102
  171.6 7.6 %collective-permute-done.19 = bf16[924,128]{1,0:T(8,128)(2,1)S(1)} collective-permute-done((bf16[924,128]{1,0:T(8,128)(2,1)S(1)}, bf16[924,128]{1,0:T(8,128)(2,1)S(1)}, u32[]{:S(2)}, u32[]{:S(2)}) %collective-permute-start.19) | collective-permute-done | bytes 236576 | tf_op jit(solution)/shard_map/ppermute | solution.py:102
  180.4 2.3 %copy.128 = bf16[1,1,128,4096]{3,2,1,0:T(8,128)(2,1)} copy(bf16[1,1,128,4096]{3,2,1,0:T(8,128)(2,1)} %bitcast.246) | data formatting | bytes 2097152
  (116 shorter events, 45.4 us)
Async XLA Ops:
  0.6 53.7 %copy-start = (bf16[4096,308]{0,1:T(8,128)(2,1)S(1)}, bf16[4096,308]{0,1:T(8,128)(2,1)}, u32[]{:S(2)}) copy-start(bf16[4096,308]{0,1:T(8,128)(2,1)} %param.10) | copy-start | bytes 7569412
  8.3 27.4 %collective-permute-start.1 = (bf16[128,4096]{0,1:T(8,128)(2,1)}, bf16[128,4096]{0,1:T(8,128)(2,1)}, u32[]{:S(2)}, u32[]{:S(2)}) collective-permute-start(bf16[128,4096]{0,1:T(8,128)(2,1)} %fusion.249), channel_id=1, source_target_pairs={{47,0},{0,1},{1,2},{2,3},{3,4},{4,5},{5,6},{6,7},{7,8},{8,9},{9,10... | collective-permute-start | bytes 3145736 | tf_op jit(solution)/shard_map/ppermute | solution.py:13
  10.2 36.8 %collective-permute-start = (bf16[128,4096]{1,0:T(8,128)(2,1)}, bf16[128,4096]{1,0:T(8,128)(2,1)}, u32[]{:S(2)}, u32[]{:S(2)}) collective-permute-start(bf16[128,4096]{1,0:T(8,128)(2,1)} %bitcast.245), channel_id=1, source_target_pairs={{47,0},{0,1},{1,2},{2,3},{3,4},{4,5},{5,6},{6,7},{7,8},{8,9},{9,10... | collective-permute-start | bytes 3145736 | tf_op jit(solution)/shard_map/ppermute | solution.py:13
  49.2 3.0 %copy-start.6 = (bf16[4096,308]{0,1:T(8,128)(2,1)S(1)}, bf16[4096,308]{0,1:T(8,128)(2,1)}, u32[]{:S(2)}) copy-start(bf16[4096,308]{0,1:T(8,128)(2,1)} %param.12) | copy-start | bytes 7569412
  54.3 5.0 %copy-start.15 = (bf16[128,1,2048]{2,0,1:T(8,128)(2,1)S(1)}, bf16[128,1,2048]{2,0,1:T(8,128)(2,1)}, u32[]{:S(2)}) copy-start(bf16[128,1,2048]{2,0,1:T(8,128)(2,1)} %copy.86) | copy-start | bytes 1572868
  54.3 8.9 %copy-start.7 = (bf16[128,4096]{0,1:T(8,128)(2,1)S(1)}, bf16[128,4096]{0,1:T(8,128)(2,1)}, u32[]{:S(2)}) copy-start(bf16[128,4096]{0,1:T(8,128)(2,1)} %copy.89) | copy-start | bytes 3145732
  56.6 9.6 %copy-start.8 = (bf16[128,308]{0,1:T(8,128)(2,1)}, bf16[128,308]{0,1:T(8,128)(2,1)S(1)}, u32[]{:S(2)}) copy-start(bf16[128,308]{0,1:T(8,128)(2,1)S(1)} %get-tuple-element.14) | copy-start | bytes 236548
  56.6 10.3 %copy-start.10 = (bf16[128,308]{0,1:T(8,128)(2,1)}, bf16[128,308]{0,1:T(8,128)(2,1)S(1)}, u32[]{:S(2)}) copy-start(bf16[128,308]{0,1:T(8,128)(2,1)S(1)} %get-tuple-element.15) | copy-start | bytes 236548
  56.6 9.5 %collective-permute-start.2 = (bf16[128,924]{0,1:T(8,128)(2,1)S(1)}, bf16[128,924]{0,1:T(8,128)(2,1)S(1)}, u32[]{:S(2)}, u32[]{:S(2)}) collective-permute-start(bf16[128,924]{0,1:T(8,128)(2,1)S(1)} %pad_maximum_fusion.1), channel_id=1, source_target_pairs={{0,384},{48,432},{96,480},{144,528},{192,576},{240,624},{288,672},... | collective-permute-start | bytes 709640 | tf_op jit(solution)/shard_map/ppermute | solution.py:62
  59.3 16.7 %collective-permute-start.3 = (bf16[128,2048]{1,0:T(8,128)(2,1)S(1)}, bf16[128,2048]{1,0:T(8,128)(2,1)}, u32[]{:S(2)}, u32[]{:S(2)}) collective-permute-start(bf16[128,2048]{1,0:T(8,128)(2,1)S(1)} %bitcast.248), channel_id=1, source_target_pairs={{0,385},{1,386},{2,387},{3,388},{4,389},{5,390},{6,391},{7,392},{8... | collective-permute-start | bytes 1572872 | tf_op jit(solution)/shard_map/ppermute | solution.py:129
  61.3 24.1 %collective-permute-start.4 = (bf16[128,2048]{1,0:T(8,128)(2,1)}, bf16[128,2048]{1,0:T(8,128)(2,1)}, u32[]{:S(2)}, u32[]{:S(2)}) collective-permute-start(bf16[128,2048]{1,0:T(8,128)(2,1)} %bitcast.7), channel_id=1, source_target_pairs={{0,385},{1,386},{2,387},{3,388},{4,389},{5,390},{6,391},{7,392},{8... | collective-permute-start | bytes 1572872 | tf_op jit(solution)/shard_map/ppermute | solution.py:129
  87.4 2.7 %copy-start.4 = (bf16[256,308]{0,1:T(8,128)(2,1)S(1)}, bf16[256,308]{0,1:T(8,128)(2,1)}, u32[]{:S(2)}) copy-start(bf16[256,308]{0,1:T(8,128)(2,1)} %pad_maximum_fusion.4) | copy-start | bytes 473092
  94.7 9.6 %collective-permute-start.6 = (bf16[924,128]{1,0:T(8,128)(2,1)S(1)}, bf16[924,128]{1,0:T(8,128)(2,1)S(1)}, u32[]{:S(2)}, u32[]{:S(2)}) collective-permute-start(bf16[924,128]{1,0:T(8,128)(2,1)S(1)} %pad_maximum_fusion.3), channel_id=1, source_target_pairs={{0,336},{48,0},{96,48},{144,96},{192,144},{240,192},{288,240},{336... | collective-permute-start | bytes 709640 | tf_op jit(solution)/shard_map/ppermute | solution.py:102
  97.1 9.0 %collective-permute-start.5 = (bf16[924,128]{1,0:T(8,128)(2,1)S(1)}, bf16[924,128]{1,0:T(8,128)(2,1)S(1)}, u32[]{:S(2)}, u32[]{:S(2)}) collective-permute-start(bf16[924,128]{1,0:T(8,128)(2,1)S(1)} %pad_maximum_fusion.2), channel_id=1, source_target_pairs={{0,48},{48,96},{96,144},{144,192},{192,240},{240,288},{288,336},{3... | collective-permute-start | bytes 709640 | tf_op jit(solution)/shard_map/ppermute | solution.py:101
  102.1 4.0 %copy-start.12 = (f32[616,128]{1,0:T(8,128)S(1)}, f32[616,128]{1,0:T(8,128)}, u32[]{:S(2)}) copy-start(f32[616,128]{1,0:T(8,128)} %fusion.100) | copy-start | bytes 946180
  106.2 11.0 %collective-permute-start.8 = (bf16[924,128]{1,0:T(8,128)(2,1)S(1)}, bf16[924,128]{1,0:T(8,128)(2,1)S(1)}, u32[]{:S(2)}, u32[]{:S(2)}) collective-permute-start(bf16[924,128]{1,0:T(8,128)(2,1)S(1)} %fusion.1), channel_id=1, source_target_pairs={{0,48},{48,96},{96,144},{144,192},{192,240},{240,288},{288,336},{3... | collective-permute-start | bytes 709640 | tf_op jit(solution)/shard_map/ppermute | solution.py:101
  112.0 22.4 %copy-start.5 = (bf16[4096,308]{0,1:T(8,128)(2,1)S(1)}, bf16[4096,308]{0,1:T(8,128)(2,1)}, u32[]{:S(2)}) copy-start(bf16[4096,308]{0,1:T(8,128)(2,1)} %param.11) | copy-start | bytes 7569412
  112.0 22.4 %copy-start.11 = (bf16[128,308]{0,1:T(8,128)(2,1)S(1)}, bf16[128,308]{0,1:T(8,128)(2,1)}, u32[]{:S(2)}) copy-start(bf16[128,308]{0,1:T(8,128)(2,1)} %copy-done.10) | copy-start | bytes 236548
  112.1 11.4 %collective-permute-start.14 = (bf16[924,128]{1,0:T(8,128)(2,1)S(1)}, bf16[924,128]{1,0:T(8,128)(2,1)S(1)}, u32[]{:S(2)}, u32[]{:S(2)}) collective-permute-start(bf16[924,128]{1,0:T(8,128)(2,1)S(1)} %fusion.7), channel_id=1, source_target_pairs={{0,336},{48,0},{96,48},{144,96},{192,144},{240,192},{288,240},{336... | collective-permute-start | bytes 709640 | tf_op jit(solution)/shard_map/ppermute | solution.py:102
  117.2 11.4 %collective-permute-start.9 = (bf16[924,128]{1,0:T(8,128)(2,1)S(1)}, bf16[924,128]{1,0:T(8,128)(2,1)S(1)}, u32[]{:S(2)}, u32[]{:S(2)}) collective-permute-start(bf16[924,128]{1,0:T(8,128)(2,1)S(1)} %fusion.2), channel_id=1, source_target_pairs={{0,48},{48,96},{96,144},{144,192},{192,240},{240,288},{288,336},{3... | collective-permute-start | bytes 709640 | tf_op jit(solution)/shard_map/ppermute | solution.py:101
  123.5 11.7 %collective-permute-start.15 = (bf16[924,128]{1,0:T(8,128)(2,1)S(1)}, bf16[924,128]{1,0:T(8,128)(2,1)S(1)}, u32[]{:S(2)}, u32[]{:S(2)}) collective-permute-start(bf16[924,128]{1,0:T(8,128)(2,1)S(1)} %fusion.8), channel_id=1, source_target_pairs={{0,336},{48,0},{96,48},{144,96},{192,144},{240,192},{288,240},{336... | collective-permute-start | bytes 709640 | tf_op jit(solution)/shard_map/ppermute | solution.py:102
  128.7 16.3 %copy-start.9 = (bf16[128,308]{0,1:T(8,128)(2,1)S(1)}, bf16[128,308]{0,1:T(8,128)(2,1)}, u32[]{:S(2)}) copy-start(bf16[128,308]{0,1:T(8,128)(2,1)} %copy-done.8) | copy-start | bytes 236548
  128.7 10.6 %collective-permute-start.10 = (bf16[924,128]{1,0:T(8,128)(2,1)S(1)}, bf16[924,128]{1,0:T(8,128)(2,1)S(1)}, u32[]{:S(2)}, u32[]{:S(2)}) collective-permute-start(bf16[924,128]{1,0:T(8,128)(2,1)S(1)} %fusion.3), channel_id=1, source_target_pairs={{0,48},{48,96},{96,144},{144,192},{192,240},{240,288},{288,336},{3... | collective-permute-start | bytes 709640 | tf_op jit(solution)/shard_map/ppermute | solution.py:101
  135.3 12.4 %collective-permute-start.16 = (bf16[924,128]{1,0:T(8,128)(2,1)S(1)}, bf16[924,128]{1,0:T(8,128)(2,1)S(1)}, u32[]{:S(2)}, u32[]{:S(2)}) collective-permute-start(bf16[924,128]{1,0:T(8,128)(2,1)S(1)} %fusion.9), channel_id=1, source_target_pairs={{0,336},{48,0},{96,48},{144,96},{192,144},{240,192},{288,240},{336... | collective-permute-start | bytes 709640 | tf_op jit(solution)/shard_map/ppermute | solution.py:102
  139.4 10.4 %collective-permute-start.11 = (bf16[924,128]{1,0:T(8,128)(2,1)S(1)}, bf16[924,128]{1,0:T(8,128)(2,1)S(1)}, u32[]{:S(2)}, u32[]{:S(2)}) collective-permute-start(bf16[924,128]{1,0:T(8,128)(2,1)S(1)} %fusion.4), channel_id=1, source_target_pairs={{0,48},{48,96},{96,144},{144,192},{192,240},{240,288},{288,336},{3... | collective-permute-start | bytes 709640 | tf_op jit(solution)/shard_map/ppermute | solution.py:101
  145.8 20.7 %collective-permute-start.7 = (bf16[128,4096]{1,0:T(8,128)(2,1)S(1)}, bf16[128,4096]{1,0:T(8,128)(2,1)S(1)}, u32[]{:S(2)}, u32[]{:S(2)}) collective-permute-start(bf16[128,4096]{1,0:T(8,128)(2,1)S(1)} %fusion), channel_id=1, source_target_pairs={{1,0},{2,1},{3,2},{4,3},{5,4},{6,5},{7,6},{8,7},{9,8},{10,9},{11,1... | collective-permute-start | bytes 3145736 | tf_op jit(solution)/shard_map/ppermute | solution.py:13
  147.8 11.3 %collective-permute-start.17 = (bf16[924,128]{1,0:T(8,128)(2,1)S(1)}, bf16[924,128]{1,0:T(8,128)(2,1)S(1)}, u32[]{:S(2)}, u32[]{:S(2)}) collective-permute-start(bf16[924,128]{1,0:T(8,128)(2,1)S(1)} %fusion.10), channel_id=1, source_target_pairs={{0,336},{48,0},{96,48},{144,96},{192,144},{240,192},{288,240},{336... | collective-permute-start | bytes 709640 | tf_op jit(solution)/shard_map/ppermute | solution.py:102
  149.8 11.3 %collective-permute-start.12 = (bf16[924,128]{1,0:T(8,128)(2,1)S(1)}, bf16[924,128]{1,0:T(8,128)(2,1)S(1)}, u32[]{:S(2)}, u32[]{:S(2)}) collective-permute-start(bf16[924,128]{1,0:T(8,128)(2,1)S(1)} %fusion.5), channel_id=1, source_target_pairs={{0,48},{48,96},{96,144},{144,192},{192,240},{240,288},{288,336},{3... | collective-permute-start | bytes 709640 | tf_op jit(solution)/shard_map/ppermute | solution.py:101
  159.1 10.4 %collective-permute-start.18 = (bf16[924,128]{1,0:T(8,128)(2,1)S(1)}, bf16[924,128]{1,0:T(8,128)(2,1)S(1)}, u32[]{:S(2)}, u32[]{:S(2)}) collective-permute-start(bf16[924,128]{1,0:T(8,128)(2,1)S(1)} %fusion.11), channel_id=1, source_target_pairs={{0,336},{48,0},{96,48},{144,96},{192,144},{240,192},{288,240},{336... | collective-permute-start | bytes 709640 | tf_op jit(solution)/shard_map/ppermute | solution.py:102
  161.1 10.4 %collective-permute-start.13 = (bf16[924,128]{1,0:T(8,128)(2,1)S(1)}, bf16[924,128]{1,0:T(8,128)(2,1)S(1)}, u32[]{:S(2)}, u32[]{:S(2)}) collective-permute-start(bf16[924,128]{1,0:T(8,128)(2,1)S(1)} %fusion.6), channel_id=1, source_target_pairs={{0,48},{48,96},{96,144},{144,192},{192,240},{240,288},{288,336},{3... | collective-permute-start | bytes 709640 | tf_op jit(solution)/shard_map/ppermute | solution.py:101
  166.5 12.8 %copy-start.13 = (bf16[128,4096]{1,0:T(8,128)(2,1)}, bf16[128,4096]{1,0:T(8,128)(2,1)S(1)}, u32[]{:S(2)}) copy-start(bf16[128,4096]{1,0:T(8,128)(2,1)S(1)} %collective-permute-done.7) | copy-start | bytes 3145732
  169.6 9.6 %collective-permute-start.19 = (bf16[924,128]{1,0:T(8,128)(2,1)S(1)}, bf16[924,128]{1,0:T(8,128)(2,1)S(1)}, u32[]{:S(2)}, u32[]{:S(2)}) collective-permute-start(bf16[924,128]{1,0:T(8,128)(2,1)S(1)} %fusion.12), channel_id=1, source_target_pairs={{0,336},{48,0},{96,48},{144,96},{192,144},{240,192},{288,240},{336... | collective-permute-start | bytes 709640 | tf_op jit(solution)/shard_map/ppermute | solution.py:102
  (4 other events, 8.4 us)

commit v7 on v5

--- a/solution.py
+++ b/solution.py
@@ -114,7 +114,7 @@
     width = tokens.shape[-1]
     tok_rows = tokens.reshape(-1, width)
     grad_rows = upstream.reshape(-1, width)
-    moved_rows, moved_grads = shifted((tok_rows, grad_rows), "blk", 1)
+    moved_rows, moved_grads = shifted(jnp.stack([tok_rows, grad_rows]), "blk", 1)
     n = lax.axis_size("dp")
     nb = lax.axis_size("blk")
     ny = n // 2
@@ -124,7 +124,7 @@
     diagonal = [
         (d * nb + j, ((d + ny) % n) * nb + (j + 1) % nb) for d in range(n) for j in range(nb)
     ]
-    tok_peer, grad_peer = lax.ppermute(other, ("dp", "blk"), diagonal)
+    tok_peer, grad_peer = lax.ppermute(jnp.stack(other), ("dp", "blk"), diagonal)
     grad_moved, panel_grads = backward_core(
         moved_rows, moved_grads, tok_peer, grad_peer, gate_weight, up_weight, down_weight
     )

time: 169 us -> 176 us (1.041)
  the two profiles are of different devices: /device:TPU:24 before, /device:TPU:26 now
where the time goes in v7:
time: 176 us; the launch traced here: 175 us
  waiting for transfers between devices  66.5 us (38%)
  starting transfers between devices  61 us (35%)
  local copies, waits for them, and re-layouts  19.1 us (11%)
  matrix products  15.9 us (9%)
  other arithmetic  9.73 us (6%)
  between operations  2.39 us (1%)
    ppermute x1, waiting for transfers between devices, shards(): lax.ppermute(jnp.stack(other), ('dp', 'blk'), diagonal)  31.1 us
    ppermute x7, starting transfers between devices, reduce_over_y(): recv_f = lax.ppermute(acc_f.astype(jnp.bfloat16), 'dp', fwd)  30.8 us
    ppermute x7, waiting for transfers between devices, reduce_over_y(): recv_b = lax.ppermute(acc_b.astype(jnp.bfloat16), 'dp', bwd)  20.5 us
    ppermute x7, starting transfers between devices, reduce_over_y(): recv_b = lax.ppermute(acc_b.astype(jnp.bfloat16), 'dp', bwd)  16 us
    ppermute x7, waiting for transfers between devices, reduce_over_y(): recv_f = lax.ppermute(acc_f.astype(jnp.bfloat16), 'dp', fwd)  10.2 us
    dot_general x32, matrix products, contract_rows(): lax.dot_general(left, right, (((0,), (0,)), ((), ())), preferred_element_...  7.13 us
    unnamed x15, local copies, waits for them, and re-layouts  6.84 us
    ppermute x1, starting transfers between devices, shards(): lax.ppermute(jnp.stack(other), ('dp', 'blk'), diagonal)  6.37 us
  transfers between devices with their start and end apart: 18, of which 10 were waited for; matrix products, arithmetic and copies ran while one was open for 11% of the time, Pallas kernels for 0%

profile of v7, /device:TPU:26, one launch (start us, length us, event | category | flops | bytes accessed | tf_op | source)
XLA Modules:
  0.0 174.7 jit_solution(16043063427892873623)
XLA Ops:
  3.6 2.2 %copy.85 = bf16[1,1,128,4096]{2,3,1,0:T(8,128)(2,1)} copy(bf16[1,1,128,4096]{3,2,1,0:T(8,128)(2,1)} %param.8) | data formatting | bytes 2097152 | tf_op args[0]
  5.9 2.3 %copy.86 = bf16[1,1,128,4096]{2,3,1,0:T(8,128)(2,1)} copy(bf16[1,1,128,4096]{3,2,1,0:T(8,128)(2,1)} %param.9) | data formatting | bytes 2097152 | tf_op args[1]
  14.3 2.1 %constant_dynamic-slice_fusion.1 = (bf16[128,1,2048]{0,2,1:T(8,128)(2,1)}, bf16[128,1,2048]{0,2,1:T(8,128)(2,1)S(1)}) fusion(bf16[128,2,2048]{0,2,1:T(8,128)(2,1)} %bitcast.251, s32[]{:T(128)S(6)} %select_n.148, bf16[128,2,2048]{0,2,1:T(8,128)(2,1)} %bitcast.249), kind=kLoop, calls=%fused_computation.241 | loop fusion | bytes 2097156 | tf_op jit(solution)/shard_map/jit(dynamic_index_in_dim)/dynamic_slice | solution.py:123
  16.4 2.1 %copy.89 = bf16[128,1,2048]{2,0,1:T(8,128)(2,1)} copy(bf16[128,1,2048]{0,2,1:T(8,128)(2,1)} %get-tuple-element.19) | data formatting | bytes 1048576 | tf_op jit(solution)/shard_map/jit(dynamic_index_in_dim)/dynamic_slice | solution.py:123
  19.4 2.3 %pad_maximum_fusion.1 = bf16[2,128,2048]{2,1,0:T(8,128)(2,1)} fusion(bf16[1,128,2048]{2,1,0:T(8,128)(2,1)} %bitcast.254, bf16[1,128,2048]{2,1,0:T(8,128)(2,1)} %bitcast.255), kind=kLoop, calls=%fused_computation.72 | loop fusion | flops 524288 | bytes 2097152 | tf_op jit(solution)/shard_map/stack | solution.py:127
  21.7 6.4 %collective-permute-start.2 = (bf16[2,128,2048]{2,1,0:T(8,128)(2,1)}, bf16[2,128,2048]{2,1,0:T(8,128)(2,1)}, u32[]{:S(2)}, u32[]{:S(2)}) collective-permute-start(bf16[2,128,2048]{2,1,0:T(8,128)(2,1)} %pad_maximum_fusion.1), channel_id=1, source_target_pairs={{0,385},{1,386},{2,387},{3,388},{4,389},{5,390},{6,391},{7,392},{8... | collective-permute-start | bytes 3145736 | tf_op jit(solution)/shard_map/ppermute | solution.py:127
  28.3 31.1 %collective-permute-done.2 = bf16[2,128,2048]{2,1,0:T(8,128)(2,1)} collective-permute-done((bf16[2,128,2048]{2,1,0:T(8,128)(2,1)}, bf16[2,128,2048]{2,1,0:T(8,128)(2,1)}, u32[]{:S(2)}, u32[]{:S(2)}) %collective-permute-start.2) | collective-permute-done | bytes 1048608 | tf_op jit(solution)/shard_map/ppermute | solution.py:127
  59.5 2.1 %fusion.230 = (bf16[1,128,2048]{2,1,0:T(8,128)(2,1)S(1)}, bf16[1,128,2048]{2,1,0:T(8,128)(2,1)}) fusion(bf16[2,128,2048]{2,1,0:T(8,128)(2,1)} %collective-permute-done.2), kind=kLoop, calls=%fused_computation.303 | loop fusion | bytes 2097152 | tf_op jit(solution)/shard_map/unstack | solution.py:127
  63.9 3.0 %fusion.5 = f32[128,308]{0,1:T(8,128)S(1)} fusion(bf16[4096,308]{0,1:T(8,128)(2,1)} %param.12, bf16[2,128,4096]{1,2,0:T(8,128)(2,1)} %collective-permute-done), kind=kOutput, calls=%fused_computation.77 | convolution fusion | flops 322961408 | bytes 3762176 | tf_op jit(solution)/shard_map/dot_general | solution.py:56
  66.9 2.1 %fusion.3 = f32[128,308]{0,1:T(8,128)S(1)} fusion(bf16[4096,308]{0,1:T(8,128)(2,1)S(1)} %copy-done.2, bf16[2,128,4096]{1,2,0:T(8,128)(2,1)} %collective-permute-done), kind=kOutput, calls=%fused_computation.75 | convolution fusion | flops 322961408 | bytes 3729408 | tf_op jit(solution)/shard_map/dot_general | solution.py:52
  69.0 2.1 %multiply_convert_fusion.3 = (bf16[128,308]{0,1:T(8,128)(2,1)S(1)}, bf16[128,308]{0,1:T(8,128)(2,1)S(1)}, bf16[128,308]{0,1:T(8,128)(2,1)S(1)}) fusion(f32[128,308]{0,1:T(8,128)S(1)} %fusion.5, f32[128,308]{0,1:T(8,128)S(1)} %fusion.3, bf16[4096,308]{0,1:T(8,128)(2,1)S(1)} %copy-done, bf16[2,128,4096]{1,2,0:T(8,128)(2,1)} %collective-permute-done), kind=kOutput, calls=%fused_computation.113 | convolution fusion | flops 323552768 | bytes 4123648 | tf_op jit(solution)/shard_map/dot_general | solution.py:51
  71.1 4.0 %collective-permute-start.1 = (bf16[128,924]{0,1:T(8,128)(2,1)S(1)}, bf16[128,924]{0,1:T(8,128)(2,1)S(1)}, u32[]{:S(2)}, u32[]{:S(2)}) collective-permute-start(bf16[128,924]{0,1:T(8,128)(2,1)S(1)} %pad_maximum_fusion.3), channel_id=1, source_target_pairs={{0,384},{48,432},{96,480},{144,528},{192,576},{240,624},{288,672},... | collective-permute-start | bytes 709640 | tf_op jit(solution)/shard_map/ppermute | solution.py:62
  76.9 4.8 %collective-permute-done.1 = bf16[128,924]{0,1:T(8,128)(2,1)S(1)} collective-permute-done((bf16[128,924]{0,1:T(8,128)(2,1)S(1)}, bf16[128,924]{0,1:T(8,128)(2,1)S(1)}, u32[]{:S(2)}, u32[]{:S(2)}) %collective-permute-start.1) | collective-permute-done | bytes 236576 | tf_op jit(solution)/shard_map/ppermute | solution.py:62
  87.4 4.7 %collective-permute-start.3 = (bf16[924,128]{1,0:T(8,128)(2,1)S(1)}, bf16[924,128]{1,0:T(8,128)(2,1)S(1)}, u32[]{:S(2)}, u32[]{:S(2)}) collective-permute-start(bf16[924,128]{1,0:T(8,128)(2,1)S(1)} %pad_maximum_fusion.4), channel_id=1, source_target_pairs={{0,48},{48,96},{96,144},{144,192},{192,240},{240,288},{288,336},{3... | collective-permute-start | bytes 709640 | tf_op jit(solution)/shard_map/ppermute | solution.py:100
  92.1 1.9 %collective-permute-start.4 = (bf16[924,128]{1,0:T(8,128)(2,1)S(1)}, bf16[924,128]{1,0:T(8,128)(2,1)S(1)}, u32[]{:S(2)}, u32[]{:S(2)}) collective-permute-start(bf16[924,128]{1,0:T(8,128)(2,1)S(1)} %pad_maximum_fusion.5), channel_id=1, source_target_pairs={{0,336},{48,0},{96,48},{144,96},{192,144},{240,192},{288,240},{336... | collective-permute-start | bytes 709640 | tf_op jit(solution)/shard_map/ppermute | solution.py:101
  95.1 2.9 %collective-permute-done.3 = bf16[924,128]{1,0:T(8,128)(2,1)S(1)} collective-permute-done((bf16[924,128]{1,0:T(8,128)(2,1)S(1)}, bf16[924,128]{1,0:T(8,128)(2,1)S(1)}, u32[]{:S(2)}, u32[]{:S(2)}) %collective-permute-start.3) | collective-permute-done | bytes 236576 | tf_op jit(solution)/shard_map/ppermute | solution.py:100
  98.0 5.9 %collective-permute-done.4 = bf16[924,128]{1,0:T(8,128)(2,1)S(1)} collective-permute-done((bf16[924,128]{1,0:T(8,128)(2,1)S(1)}, bf16[924,128]{1,0:T(8,128)(2,1)S(1)}, u32[]{:S(2)}, u32[]{:S(2)}) %collective-permute-start.4) | collective-permute-done | bytes 236576 | tf_op jit(solution)/shard_map/ppermute | solution.py:101
  104.0 1.9 %collective-permute-start.6 = (bf16[924,128]{1,0:T(8,128)(2,1)S(1)}, bf16[924,128]{1,0:T(8,128)(2,1)S(1)}, u32[]{:S(2)}, u32[]{:S(2)}) collective-permute-start(bf16[924,128]{1,0:T(8,128)(2,1)S(1)} %fusion.7), channel_id=1, source_target_pairs={{0,48},{48,96},{96,144},{144,192},{192,240},{240,288},{288,336},{3... | collective-permute-start | bytes 709640 | tf_op jit(solution)/shard_map/ppermute | solution.py:100
  106.2 3.9 %collective-permute-start.12 = (bf16[924,128]{1,0:T(8,128)(2,1)S(1)}, bf16[924,128]{1,0:T(8,128)(2,1)S(1)}, u32[]{:S(2)}, u32[]{:S(2)}) collective-permute-start(bf16[924,128]{1,0:T(8,128)(2,1)S(1)} %fusion.13), channel_id=1, source_target_pairs={{0,336},{48,0},{96,48},{144,96},{192,144},{240,192},{288,240},{336... | collective-permute-start | bytes 709640 | tf_op jit(solution)/shard_map/ppermute | solution.py:101
  110.1 3.6 %collective-permute-done.6 = bf16[924,128]{1,0:T(8,128)(2,1)S(1)} collective-permute-done((bf16[924,128]{1,0:T(8,128)(2,1)S(1)}, bf16[924,128]{1,0:T(8,128)(2,1)S(1)}, u32[]{:S(2)}, u32[]{:S(2)}) %collective-permute-start.6) | collective-permute-done | bytes 236576 | tf_op jit(solution)/shard_map/ppermute | solution.py:100
  113.7 3.4 %collective-permute-start.7 = (bf16[924,128]{1,0:T(8,128)(2,1)S(1)}, bf16[924,128]{1,0:T(8,128)(2,1)S(1)}, u32[]{:S(2)}, u32[]{:S(2)}) collective-permute-start(bf16[924,128]{1,0:T(8,128)(2,1)S(1)} %fusion.8), channel_id=1, source_target_pairs={{0,48},{48,96},{96,144},{144,192},{192,240},{240,288},{288,336},{3... | collective-permute-start | bytes 709640 | tf_op jit(solution)/shard_map/ppermute | solution.py:100
  117.4 2.4 %collective-permute-start.13 = (bf16[924,128]{1,0:T(8,128)(2,1)S(1)}, bf16[924,128]{1,0:T(8,128)(2,1)S(1)}, u32[]{:S(2)}, u32[]{:S(2)}) collective-permute-start(bf16[924,128]{1,0:T(8,128)(2,1)S(1)} %fusion.14), channel_id=1, source_target_pairs={{0,336},{48,0},{96,48},{144,96},{192,144},{240,192},{288,240},{336... | collective-permute-start | bytes 709640 | tf_op jit(solution)/shard_map/ppermute | solution.py:101
  119.8 2.7 %collective-permute-done.7 = bf16[924,128]{1,0:T(8,128)(2,1)S(1)} collective-permute-done((bf16[924,128]{1,0:T(8,128)(2,1)S(1)}, bf16[924,128]{1,0:T(8,128)(2,1)S(1)}, u32[]{:S(2)}, u32[]{:S(2)}) %collective-permute-start.7) | collective-permute-done | bytes 236576 | tf_op jit(solution)/shard_map/ppermute | solution.py:100
  122.6 4.9 %collective-permute-start.8 = (bf16[924,128]{1,0:T(8,128)(2,1)S(1)}, bf16[924,128]{1,0:T(8,128)(2,1)S(1)}, u32[]{:S(2)}, u32[]{:S(2)}) collective-permute-start(bf16[924,128]{1,0:T(8,128)(2,1)S(1)} %fusion.9), channel_id=1, source_target_pairs={{0,48},{48,96},{96,144},{144,192},{192,240},{240,288},{288,336},{3... | collective-permute-start | bytes 709640 | tf_op jit(solution)/shard_map/ppermute | solution.py:100
  128.5 1.9 %collective-permute-start.14 = (bf16[924,128]{1,0:T(8,128)(2,1)S(1)}, bf16[924,128]{1,0:T(8,128)(2,1)S(1)}, u32[]{:S(2)}, u32[]{:S(2)}) collective-permute-start(bf16[924,128]{1,0:T(8,128)(2,1)S(1)} %fusion.15), channel_id=1, source_target_pairs={{0,336},{48,0},{96,48},{144,96},{192,144},{240,192},{288,240},{336... | collective-permute-start | bytes 709640 | tf_op jit(solution)/shard_map/ppermute | solution.py:101
  131.4 5.6 %collective-permute-start.9 = (bf16[924,128]{1,0:T(8,128)(2,1)S(1)}, bf16[924,128]{1,0:T(8,128)(2,1)S(1)}, u32[]{:S(2)}, u32[]{:S(2)}) collective-permute-start(bf16[924,128]{1,0:T(8,128)(2,1)S(1)} %fusion.10), channel_id=1, source_target_pairs={{0,48},{48,96},{96,144},{144,192},{192,240},{240,288},{288,336},{3... | collective-permute-start | bytes 709640 | tf_op jit(solution)/shard_map/ppermute | solution.py:100
  141.9 5.1 %collective-permute-start.10 = (bf16[924,128]{1,0:T(8,128)(2,1)S(1)}, bf16[924,128]{1,0:T(8,128)(2,1)S(1)}, u32[]{:S(2)}, u32[]{:S(2)}) collective-permute-start(bf16[924,128]{1,0:T(8,128)(2,1)S(1)} %fusion.11), channel_id=1, source_target_pairs={{0,48},{48,96},{96,144},{144,192},{192,240},{240,288},{288,336},{3... | collective-permute-start | bytes 709640 | tf_op jit(solution)/shard_map/ppermute | solution.py:100
  147.2 3.9 %collective-permute-done.15 = bf16[924,128]{1,0:T(8,128)(2,1)S(1)} collective-permute-done((bf16[924,128]{1,0:T(8,128)(2,1)S(1)}, bf16[924,128]{1,0:T(8,128)(2,1)S(1)}, u32[]{:S(2)}, u32[]{:S(2)}) %collective-permute-start.15) | collective-permute-done | bytes 236576 | tf_op jit(solution)/shard_map/ppermute | solution.py:101
  153.2 5.1 %collective-permute-start.11 = (bf16[924,128]{1,0:T(8,128)(2,1)S(1)}, bf16[924,128]{1,0:T(8,128)(2,1)S(1)}, u32[]{:S(2)}, u32[]{:S(2)}) collective-permute-start(bf16[924,128]{1,0:T(8,128)(2,1)S(1)} %fusion.12), channel_id=1, source_target_pairs={{0,48},{48,96},{96,144},{144,192},{192,240},{240,288},{288,336},{3... | collective-permute-start | bytes 709640 | tf_op jit(solution)/shard_map/ppermute | solution.py:100
  158.6 3.1 %collective-permute-done.16 = bf16[924,128]{1,0:T(8,128)(2,1)S(1)} collective-permute-done((bf16[924,128]{1,0:T(8,128)(2,1)S(1)}, bf16[924,128]{1,0:T(8,128)(2,1)S(1)}, u32[]{:S(2)}, u32[]{:S(2)}) %collective-permute-start.16) | collective-permute-done | bytes 236576 | tf_op jit(solution)/shard_map/ppermute | solution.py:101
  163.7 7.6 %collective-permute-done.17 = bf16[924,128]{1,0:T(8,128)(2,1)S(1)} collective-permute-done((bf16[924,128]{1,0:T(8,128)(2,1)S(1)}, bf16[924,128]{1,0:T(8,128)(2,1)S(1)}, u32[]{:S(2)}, u32[]{:S(2)}) %collective-permute-start.17) | collective-permute-done | bytes 236576 | tf_op jit(solution)/shard_map/ppermute | solution.py:101
  172.4 2.3 %copy.127 = bf16[1,1,128,4096]{3,2,1,0:T(8,128)(2,1)} copy(bf16[1,1,128,4096]{3,2,1,0:T(8,128)(2,1)} %bitcast.256) | data formatting | bytes 2097152
  (93 shorter events, 33.0 us)
Async XLA Ops:
  0.6 68.3 %copy-start = (bf16[4096,308]{0,1:T(8,128)(2,1)S(1)}, bf16[4096,308]{0,1:T(8,128)(2,1)}, u32[]{:S(2)}) copy-start(bf16[4096,308]{0,1:T(8,128)(2,1)} %param.10) | copy-start | bytes 7569412
  8.1 1.5 copy-start.4
  9.7 3.4 %copy-start.3 = (bf16[1,1,128,4096]{2,3,1,0:T(8,128)(2,1)S(1)}, bf16[1,1,128,4096]{2,3,1,0:T(8,128)(2,1)}, u32[]{:S(2)}) copy-start(bf16[1,1,128,4096]{2,3,1,0:T(8,128)(2,1)} %copy.86) | copy-start | bytes 3145732
  11.2 52.7 %collective-permute-start = (bf16[2,128,4096]{1,2,0:T(8,128)(2,1)}, bf16[2,128,4096]{1,2,0:T(8,128)(2,1)}, u32[]{:S(2)}, u32[]{:S(2)}) collective-permute-start(bf16[2,128,4096]{1,2,0:T(8,128)(2,1)} %pad_maximum_fusion), channel_id=1, source_target_pairs={{47,0},{0,1},{1,2},{2,3},{3,4},{4,5},{5,6},{6,7},{7,8},{8,9},{9,10... | collective-permute-start | bytes 6291464 | tf_op jit(solution)/shard_map/ppermute | solution.py:13
  21.7 37.8 %collective-permute-start.2 = (bf16[2,128,2048]{2,1,0:T(8,128)(2,1)}, bf16[2,128,2048]{2,1,0:T(8,128)(2,1)}, u32[]{:S(2)}, u32[]{:S(2)}) collective-permute-start(bf16[2,128,2048]{2,1,0:T(8,128)(2,1)} %pad_maximum_fusion.1), channel_id=1, source_target_pairs={{0,385},{1,386},{2,387},{3,388},{4,389},{5,390},{6,391},{7,392},{8... | collective-permute-start | bytes 3145736 | tf_op jit(solution)/shard_map/ppermute | solution.py:127
  63.8 3.0 %copy-start.2 = (bf16[4096,308]{0,1:T(8,128)(2,1)S(1)}, bf16[4096,308]{0,1:T(8,128)(2,1)}, u32[]{:S(2)}) copy-start(bf16[4096,308]{0,1:T(8,128)(2,1)} %param.11) | copy-start | bytes 7569412
  71.1 10.6 %collective-permute-start.1 = (bf16[128,924]{0,1:T(8,128)(2,1)S(1)}, bf16[128,924]{0,1:T(8,128)(2,1)S(1)}, u32[]{:S(2)}, u32[]{:S(2)}) collective-permute-start(bf16[128,924]{0,1:T(8,128)(2,1)S(1)} %pad_maximum_fusion.3), channel_id=1, source_target_pairs={{0,384},{48,432},{96,480},{144,528},{192,576},{240,624},{288,672},... | collective-permute-start | bytes 709640 | tf_op jit(solution)/shard_map/ppermute | solution.py:62
  76.9 5.3 %copy-start.1 = (bf16[1,128,2048]{1,2,0:T(8,128)(2,1)S(1)}, bf16[1,128,2048]{1,2,0:T(8,128)(2,1)}, u32[]{:S(2)}) copy-start(bf16[1,128,2048]{1,2,0:T(8,128)(2,1)} %copy.90) | copy-start | bytes 1572868
  87.4 10.6 %collective-permute-start.3 = (bf16[924,128]{1,0:T(8,128)(2,1)S(1)}, bf16[924,128]{1,0:T(8,128)(2,1)S(1)}, u32[]{:S(2)}, u32[]{:S(2)}) collective-permute-start(bf16[924,128]{1,0:T(8,128)(2,1)S(1)} %pad_maximum_fusion.4), channel_id=1, source_target_pairs={{0,48},{48,96},{96,144},{144,192},{192,240},{240,288},{288,336},{3... | collective-permute-start | bytes 709640 | tf_op jit(solution)/shard_map/ppermute | solution.py:100
  92.1 11.7 %collective-permute-start.4 = (bf16[924,128]{1,0:T(8,128)(2,1)S(1)}, bf16[924,128]{1,0:T(8,128)(2,1)S(1)}, u32[]{:S(2)}, u32[]{:S(2)}) collective-permute-start(bf16[924,128]{1,0:T(8,128)(2,1)S(1)} %pad_maximum_fusion.5), channel_id=1, source_target_pairs={{0,336},{48,0},{96,48},{144,96},{192,144},{240,192},{288,240},{336... | collective-permute-start | bytes 709640 | tf_op jit(solution)/shard_map/ppermute | solution.py:101
  104.0 9.7 %collective-permute-start.6 = (bf16[924,128]{1,0:T(8,128)(2,1)S(1)}, bf16[924,128]{1,0:T(8,128)(2,1)S(1)}, u32[]{:S(2)}, u32[]{:S(2)}) collective-permute-start(bf16[924,128]{1,0:T(8,128)(2,1)S(1)} %fusion.7), channel_id=1, source_target_pairs={{0,48},{48,96},{96,144},{144,192},{192,240},{240,288},{288,336},{3... | collective-permute-start | bytes 709640 | tf_op jit(solution)/shard_map/ppermute | solution.py:100
  106.2 11.2 %collective-permute-start.12 = (bf16[924,128]{1,0:T(8,128)(2,1)S(1)}, bf16[924,128]{1,0:T(8,128)(2,1)S(1)}, u32[]{:S(2)}, u32[]{:S(2)}) collective-permute-start(bf16[924,128]{1,0:T(8,128)(2,1)S(1)} %fusion.13), channel_id=1, source_target_pairs={{0,336},{48,0},{96,48},{144,96},{192,144},{240,192},{288,240},{336... | collective-permute-start | bytes 709640 | tf_op jit(solution)/shard_map/ppermute | solution.py:101
  113.7 8.8 %collective-permute-start.7 = (bf16[924,128]{1,0:T(8,128)(2,1)S(1)}, bf16[924,128]{1,0:T(8,128)(2,1)S(1)}, u32[]{:S(2)}, u32[]{:S(2)}) collective-permute-start(bf16[924,128]{1,0:T(8,128)(2,1)S(1)} %fusion.8), channel_id=1, source_target_pairs={{0,48},{48,96},{96,144},{144,192},{192,240},{240,288},{288,336},{3... | collective-permute-start | bytes 709640 | tf_op jit(solution)/shard_map/ppermute | solution.py:100
  117.4 11.0 %collective-permute-start.13 = (bf16[924,128]{1,0:T(8,128)(2,1)S(1)}, bf16[924,128]{1,0:T(8,128)(2,1)S(1)}, u32[]{:S(2)}, u32[]{:S(2)}) collective-permute-start(bf16[924,128]{1,0:T(8,128)(2,1)S(1)} %fusion.14), channel_id=1, source_target_pairs={{0,336},{48,0},{96,48},{144,96},{192,144},{240,192},{288,240},{336... | collective-permute-start | bytes 709640 | tf_op jit(solution)/shard_map/ppermute | solution.py:101
  122.6 8.8 %collective-permute-start.8 = (bf16[924,128]{1,0:T(8,128)(2,1)S(1)}, bf16[924,128]{1,0:T(8,128)(2,1)S(1)}, u32[]{:S(2)}, u32[]{:S(2)}) collective-permute-start(bf16[924,128]{1,0:T(8,128)(2,1)S(1)} %fusion.9), channel_id=1, source_target_pairs={{0,48},{48,96},{96,144},{144,192},{192,240},{240,288},{288,336},{3... | collective-permute-start | bytes 709640 | tf_op jit(solution)/shard_map/ppermute | solution.py:100
  128.5 11.3 %collective-permute-start.14 = (bf16[924,128]{1,0:T(8,128)(2,1)S(1)}, bf16[924,128]{1,0:T(8,128)(2,1)S(1)}, u32[]{:S(2)}, u32[]{:S(2)}) collective-permute-start(bf16[924,128]{1,0:T(8,128)(2,1)S(1)} %fusion.15), channel_id=1, source_target_pairs={{0,336},{48,0},{96,48},{144,96},{192,144},{240,192},{288,240},{336... | collective-permute-start | bytes 709640 | tf_op jit(solution)/shard_map/ppermute | solution.py:101
  131.4 10.3 %collective-permute-start.9 = (bf16[924,128]{1,0:T(8,128)(2,1)S(1)}, bf16[924,128]{1,0:T(8,128)(2,1)S(1)}, u32[]{:S(2)}, u32[]{:S(2)}) collective-permute-start(bf16[924,128]{1,0:T(8,128)(2,1)S(1)} %fusion.10), channel_id=1, source_target_pairs={{0,48},{48,96},{96,144},{144,192},{192,240},{240,288},{288,336},{3... | collective-permute-start | bytes 709640 | tf_op jit(solution)/shard_map/ppermute | solution.py:100
  137.9 20.7 %collective-permute-start.5 = (bf16[128,4096]{1,0:T(8,128)(2,1)S(1)}, bf16[128,4096]{1,0:T(8,128)(2,1)S(1)}, u32[]{:S(2)}, u32[]{:S(2)}) collective-permute-start(bf16[128,4096]{1,0:T(8,128)(2,1)S(1)} %fusion), channel_id=1, source_target_pairs={{1,0},{2,1},{3,2},{4,3},{5,4},{6,5},{7,6},{8,7},{9,8},{10,9},{11,1... | collective-permute-start | bytes 3145736 | tf_op jit(solution)/shard_map/ppermute | solution.py:13
  139.9 11.3 %collective-permute-start.15 = (bf16[924,128]{1,0:T(8,128)(2,1)S(1)}, bf16[924,128]{1,0:T(8,128)(2,1)S(1)}, u32[]{:S(2)}, u32[]{:S(2)}) collective-permute-start(bf16[924,128]{1,0:T(8,128)(2,1)S(1)} %fusion.16), channel_id=1, source_target_pairs={{0,336},{48,0},{96,48},{144,96},{192,144},{240,192},{288,240},{336... | collective-permute-start | bytes 709640 | tf_op jit(solution)/shard_map/ppermute | solution.py:101
  141.9 11.3 %collective-permute-start.10 = (bf16[924,128]{1,0:T(8,128)(2,1)S(1)}, bf16[924,128]{1,0:T(8,128)(2,1)S(1)}, u32[]{:S(2)}, u32[]{:S(2)}) collective-permute-start(bf16[924,128]{1,0:T(8,128)(2,1)S(1)} %fusion.11), channel_id=1, source_target_pairs={{0,48},{48,96},{96,144},{144,192},{192,240},{240,288},{288,336},{3... | collective-permute-start | bytes 709640 | tf_op jit(solution)/shard_map/ppermute | solution.py:100
  151.2 10.4 %collective-permute-start.16 = (bf16[924,128]{1,0:T(8,128)(2,1)S(1)}, bf16[924,128]{1,0:T(8,128)(2,1)S(1)}, u32[]{:S(2)}, u32[]{:S(2)}) collective-permute-start(bf16[924,128]{1,0:T(8,128)(2,1)S(1)} %fusion.17), channel_id=1, source_target_pairs={{0,336},{48,0},{96,48},{144,96},{192,144},{240,192},{288,240},{336... | collective-permute-start | bytes 709640 | tf_op jit(solution)/shard_map/ppermute | solution.py:101
  153.2 10.4 %collective-permute-start.11 = (bf16[924,128]{1,0:T(8,128)(2,1)S(1)}, bf16[924,128]{1,0:T(8,128)(2,1)S(1)}, u32[]{:S(2)}, u32[]{:S(2)}) collective-permute-start(bf16[924,128]{1,0:T(8,128)(2,1)S(1)} %fusion.12), channel_id=1, source_target_pairs={{0,48},{48,96},{96,144},{144,192},{192,240},{240,288},{288,336},{3... | collective-permute-start | bytes 709640 | tf_op jit(solution)/shard_map/ppermute | solution.py:100
  158.6 12.8 %copy-start.5 = (bf16[128,4096]{1,0:T(8,128)(2,1)}, bf16[128,4096]{1,0:T(8,128)(2,1)S(1)}, u32[]{:S(2)}) copy-start(bf16[128,4096]{1,0:T(8,128)(2,1)S(1)} %collective-permute-done.5) | copy-start | bytes 3145732
  161.7 9.6 %collective-permute-start.17 = (bf16[924,128]{1,0:T(8,128)(2,1)S(1)}, bf16[924,128]{1,0:T(8,128)(2,1)S(1)}, u32[]{:S(2)}, u32[]{:S(2)}) collective-permute-start(bf16[924,128]{1,0:T(8,128)(2,1)S(1)} %fusion.18), channel_id=1, source_target_pairs={{0,336},{48,0},{96,48},{144,96},{192,144},{240,192},{288,240},{336... | collective-permute-start | bytes 709640 | tf_op jit(solution)/shard_map/ppermute | solution.py:101

commit v8 on v5

--- a/solution.py
+++ b/solution.py
@@ -69,7 +69,7 @@
     summed, grad_tok = reduce_over_y(
         tok_all, grad_all, mixed_all, hidden.shape[1], late, (d_gate, d_up)
     )
-    return (grad_tok, summed / n)
+    return (grad_tok, summed)
 
 
 def reduce_over_y(tok_all, grad_all, mixed_all, cols, late, late_args):
@@ -102,8 +102,9 @@
         if s == 0:
             recv_f, recv_b, late_args = lax.optimization_barrier((recv_f, recv_b, late_args))
             late_out = late(*late_args)
-        acc_f = recv_f.astype(jnp.float32) + chunk((y + 2 * ny - 2 - s) % ny, 0)
-        acc_b = recv_b.astype(jnp.float32) + chunk((y + 2 + s) % ny, 1)
+        scale = 1.0 / n if s == ny - 2 else 1.0
+        acc_f = (recv_f.astype(jnp.float32) + chunk((y + 2 * ny - 2 - s) % ny, 0)) * scale
+        acc_b = (recv_b.astype(jnp.float32) + chunk((y + 2 + s) % ny, 1)) * scale
     total = jnp.concatenate([acc_f, acc_b], axis=1).reshape(3, cols, 2 * lane)
     return jnp.transpose(total, (0, 2, 1)), late_out
 

time: 169 us -> 169 us (level)
  no operation moved by 1% of the time
where the time goes in v8:
time: 169 us; the launch traced here: 168 us
  starting transfers between devices  71.7 us (42%)
  waiting for transfers between devices  53 us (31%)
  local copies, waits for them, and re-layouts  19.6 us (12%)
  matrix products  16 us (9%)
  other arithmetic  5.56 us (3%)
  between operations  2.35 us (1%)
    ppermute x7, starting transfers between devices, reduce_over_y(): recv_f = lax.ppermute(acc_f.astype(jnp.bfloat16), 'dp', fwd)  37.4 us
    ppermute x2, waiting for transfers between devices, shards(): tok_peer, grad_peer = lax.ppermute(other, ('dp', 'blk'), diagonal)  28.3 us
    ppermute x7, waiting for transfers between devices, reduce_over_y(): recv_b = lax.ppermute(acc_b.astype(jnp.bfloat16), 'dp', bwd)  15 us
    ppermute x7, starting transfers between devices, reduce_over_y(): recv_b = lax.ppermute(acc_b.astype(jnp.bfloat16), 'dp', bwd)  14 us
    ppermute x2, starting transfers between devices, shards(): tok_peer, grad_peer = lax.ppermute(other, ('dp', 'blk'), diagonal)  9.43 us
    ppermute x3, starting transfers between devices, shifted(): return lax.ppermute(block, axis, route)  7.98 us
    unnamed x23, local copies, waits for them, and re-layouts  7.64 us
    ppermute x7, waiting for transfers between devices, reduce_over_y(): recv_f = lax.ppermute(acc_f.astype(jnp.bfloat16), 'dp', fwd)  7.45 us
  transfers between devices with their start and end apart: 20, of which 12 were waited for; matrix products, arithmetic and copies ran while one was open for 13% of the time, Pallas kernels for 0%

profile of v8, /device:TPU:24, one launch (start us, length us, event | category | flops | bytes accessed | tf_op | source)
XLA Modules:
  0.0 168.2 jit_solution(10648421609010790774)
XLA Ops:
  0.7 2.4 %copy.87 = bf16[1,1,128,4096]{2,3,1,0:T(8,128)(2,1)} copy(bf16[1,1,128,4096]{3,2,1,0:T(8,128)(2,1)} %param.8) | data formatting | bytes 2097152 | tf_op args[0]
  5.2 4.4 %collective-permute-start.3 = (bf16[128,2048]{1,0:T(8,128)(2,1)}, bf16[128,2048]{1,0:T(8,128)(2,1)}, u32[]{:S(2)}, u32[]{:S(2)}) collective-permute-start(bf16[128,2048]{1,0:T(8,128)(2,1)} %bitcast.248), channel_id=1, source_target_pairs={{0,385},{1,386},{2,387},{3,388},{4,389},{5,390},{6,391},{7,392},{8... | collective-permute-start | bytes 1572872 | tf_op jit(solution)/shard_map/ppermute | solution.py:128
  9.5 2.3 %collective-permute-start.1 = (bf16[128,4096]{1,0:T(8,128)(2,1)}, bf16[128,4096]{1,0:T(8,128)(2,1)}, u32[]{:S(2)}, u32[]{:S(2)}) collective-permute-start(bf16[128,4096]{1,0:T(8,128)(2,1)} %bitcast.245), channel_id=1, source_target_pairs={{47,0},{0,1},{1,2},{2,3},{3,4},{4,5},{5,6},{6,7},{7,8},{8,9},{9,10... | collective-permute-start | bytes 3145736 | tf_op jit(solution)/shard_map/ppermute | solution.py:13
  12.8 2.3 %copy.85 = bf16[1,1,128,4096]{2,3,1,0:T(8,128)(2,1)} copy(bf16[1,1,128,4096]{3,2,1,0:T(8,128)(2,1)} %param.9) | data formatting | bytes 2097152 | tf_op args[1]
  15.0 2.5 %fusion.251 = bf16[128,4096]{0,1:T(8,128)(2,1)} fusion(f32[128]{0:T(128)S(1)} %select_reduce_fusion, bf16[1,1,128,4096]{2,3,1,0:T(8,128)(2,1)} %copy.85), kind=kLoop, calls=%fused_computation.296 | loop fusion | flops 1572864 | bytes 2097664 | tf_op jit(solution)/shard_map/reshape | solution.py:117
  17.5 2.2 %collective-permute-start = (bf16[128,4096]{0,1:T(8,128)(2,1)}, bf16[128,4096]{0,1:T(8,128)(2,1)}, u32[]{:S(2)}, u32[]{:S(2)}) collective-permute-start(bf16[128,4096]{0,1:T(8,128)(2,1)} %fusion.251), channel_id=1, source_target_pairs={{47,0},{0,1},{1,2},{2,3},{3,4},{4,5},{5,6},{6,7},{7,8},{8,9},{9,10... | collective-permute-start | bytes 3145736 | tf_op jit(solution)/shard_map/ppermute | solution.py:13
  21.0 5.1 %collective-permute-start.4 = (bf16[128,2048]{1,0:T(8,128)(2,1)}, bf16[128,2048]{1,0:T(8,128)(2,1)}, u32[]{:S(2)}, u32[]{:S(2)}) collective-permute-start(bf16[128,2048]{1,0:T(8,128)(2,1)} %bitcast.249), channel_id=1, source_target_pairs={{0,385},{1,386},{2,387},{3,388},{4,389},{5,390},{6,391},{7,392},{8... | collective-permute-start | bytes 1572872 | tf_op jit(solution)/shard_map/ppermute | solution.py:128
  26.4 2.2 %collective-permute-done.3 = bf16[128,2048]{1,0:T(8,128)(2,1)} collective-permute-done((bf16[128,2048]{1,0:T(8,128)(2,1)}, bf16[128,2048]{1,0:T(8,128)(2,1)}, u32[]{:S(2)}, u32[]{:S(2)}) %collective-permute-start.3) | collective-permute-done | bytes 524320 | tf_op jit(solution)/shard_map/ppermute | solution.py:128
  28.6 2.0 %copy.89 = bf16[128,2048]{0,1:T(8,128)(2,1)} copy(bf16[128,2048]{1,0:T(8,128)(2,1)} %collective-permute-done.3) | data formatting | bytes 1048576 | tf_op jit(solution)/shard_map/ppermute | solution.py:128
  30.6 26.1 %collective-permute-done.4 = bf16[128,2048]{1,0:T(8,128)(2,1)} collective-permute-done((bf16[128,2048]{1,0:T(8,128)(2,1)}, bf16[128,2048]{1,0:T(8,128)(2,1)}, u32[]{:S(2)}, u32[]{:S(2)}) %collective-permute-start.4) | collective-permute-done | bytes 524320 | tf_op jit(solution)/shard_map/ppermute | solution.py:128
  58.0 3.0 %fusion.222 = f32[128,308]{0,1:T(8,128)S(1)} fusion(bf16[128,4096]{0,1:T(8,128)(2,1)} %collective-permute-done, bf16[4096,308]{0,1:T(8,128)(2,1)} %param.12), kind=kOutput, calls=%fused_computation.293 | convolution fusion | flops 322961408 | bytes 3729408 | tf_op jit(solution)/shard_map/dot_general | solution.py:56
  61.1 2.1 %fusion.223 = f32[128,308]{0,1:T(8,128)S(1)} fusion(bf16[128,4096]{1,0:T(8,128)(2,1)} %collective-permute-done.1, bf16[4096,308]{0,1:T(8,128)(2,1)S(1)} %copy-done.2), kind=kOutput, calls=%fused_computation.294 | convolution fusion | flops 322961408 | bytes 3729408 | tf_op jit(solution)/shard_map/dot_general | solution.py:52
  63.2 2.1 %multiply_convert_fusion.3 = (bf16[128,308]{0,1:T(8,128)(2,1)S(1)}, bf16[128,308]{0,1:T(8,128)(2,1)S(1)}, bf16[128,308]{0,1:T(8,128)(2,1)S(1)}) fusion(f32[128,308]{0,1:T(8,128)S(1)} %fusion.222, f32[128,308]{0,1:T(8,128)S(1)} %fusion.223, bf16[128,4096]{1,0:T(8,128)(2,1)} %collective-permute-done.1, bf16[4096,308]{0,1:T(8,128)(2,1)S(1)} %copy-done), kind=kOutput, calls=%fused_computation.107 | convolution fusion | flops 323552768 | bytes 4123648 | tf_op jit(solution)/shard_map/dot_general | solution.py:51
  66.7 2.9 %collective-permute-start.2 = (bf16[128,924]{0,1:T(8,128)(2,1)}, bf16[128,924]{0,1:T(8,128)(2,1)S(1)}, u32[]{:S(2)}, u32[]{:S(2)}) collective-permute-start(bf16[128,924]{0,1:T(8,128)(2,1)} %pad_maximum_fusion.2), channel_id=1, source_target_pairs={{0,384},{48,432},{96,480},{144,528},{192,576},{240,624},{288,672},... | collective-permute-start | bytes 709640 | tf_op jit(solution)/shard_map/ppermute | solution.py:62
  69.6 2.3 %copy.86 = bf16[128,4096]{0,1:T(8,128)(2,1)} copy(bf16[128,4096]{1,0:T(8,128)(2,1)} %collective-permute-done.1) | data formatting | bytes 2097152 | tf_op jit(solution)/shard_map/ppermute | solution.py:13
  74.1 2.3 %collective-permute-done.2 = bf16[128,924]{0,1:T(8,128)(2,1)S(1)} collective-permute-done((bf16[128,924]{0,1:T(8,128)(2,1)}, bf16[128,924]{0,1:T(8,128)(2,1)S(1)}, u32[]{:S(2)}, u32[]{:S(2)}) %collective-permute-start.2) | collective-permute-done | bytes 236576 | tf_op jit(solution)/shard_map/ppermute | solution.py:62
  83.0 2.4 %collective-permute-start.6 = (bf16[924,128]{1,0:T(8,128)(2,1)S(1)}, bf16[924,128]{1,0:T(8,128)(2,1)S(1)}, u32[]{:S(2)}, u32[]{:S(2)}) collective-permute-start(bf16[924,128]{1,0:T(8,128)(2,1)S(1)} %pad_maximum_fusion.4), channel_id=1, source_target_pairs={{0,336},{48,0},{96,48},{144,96},{192,144},{240,192},{288,240},{336... | collective-permute-start | bytes 709640 | tf_op jit(solution)/shard_map/ppermute | solution.py:101
  85.4 4.7 %collective-permute-start.5 = (bf16[924,128]{1,0:T(8,128)(2,1)S(1)}, bf16[924,128]{1,0:T(8,128)(2,1)S(1)}, u32[]{:S(2)}, u32[]{:S(2)}) collective-permute-start(bf16[924,128]{1,0:T(8,128)(2,1)S(1)} %pad_maximum_fusion.3), channel_id=1, source_target_pairs={{0,48},{48,96},{96,144},{144,192},{192,240},{240,288},{288,336},{3... | collective-permute-start | bytes 709640 | tf_op jit(solution)/shard_map/ppermute | solution.py:100
  91.1 3.2 %collective-permute-done.6 = bf16[924,128]{1,0:T(8,128)(2,1)S(1)} collective-permute-done((bf16[924,128]{1,0:T(8,128)(2,1)S(1)}, bf16[924,128]{1,0:T(8,128)(2,1)S(1)}, u32[]{:S(2)}, u32[]{:S(2)}) %collective-permute-start.6) | collective-permute-done | bytes 236576 | tf_op jit(solution)/shard_map/ppermute | solution.py:101
  95.8 5.6 %collective-permute-start.8 = (bf16[924,128]{1,0:T(8,128)(2,1)S(1)}, bf16[924,128]{1,0:T(8,128)(2,1)S(1)}, u32[]{:S(2)}, u32[]{:S(2)}) collective-permute-start(bf16[924,128]{1,0:T(8,128)(2,1)S(1)} %fusion.1), channel_id=1, source_target_pairs={{0,48},{48,96},{96,144},{144,192},{192,240},{240,288},{288,336},{3... | collective-permute-start | bytes 709640 | tf_op jit(solution)/shard_map/ppermute | solution.py:100
  101.7 2.1 %collective-permute-start.14 = (bf16[924,128]{1,0:T(8,128)(2,1)S(1)}, bf16[924,128]{1,0:T(8,128)(2,1)S(1)}, u32[]{:S(2)}, u32[]{:S(2)}) collective-permute-start(bf16[924,128]{1,0:T(8,128)(2,1)S(1)} %fusion.8), channel_id=1, source_target_pairs={{0,336},{48,0},{96,48},{144,96},{192,144},{240,192},{288,240},{336... | collective-permute-start | bytes 709640 | tf_op jit(solution)/shard_map/ppermute | solution.py:101
  103.8 3.1 %collective-permute-done.8 = bf16[924,128]{1,0:T(8,128)(2,1)S(1)} collective-permute-done((bf16[924,128]{1,0:T(8,128)(2,1)S(1)}, bf16[924,128]{1,0:T(8,128)(2,1)S(1)}, u32[]{:S(2)}, u32[]{:S(2)}) %collective-permute-start.8) | collective-permute-done | bytes 236576 | tf_op jit(solution)/shard_map/ppermute | solution.py:100
  106.9 5.6 %collective-permute-start.9 = (bf16[924,128]{1,0:T(8,128)(2,1)S(1)}, bf16[924,128]{1,0:T(8,128)(2,1)S(1)}, u32[]{:S(2)}, u32[]{:S(2)}) collective-permute-start(bf16[924,128]{1,0:T(8,128)(2,1)S(1)} %fusion.2), channel_id=1, source_target_pairs={{0,48},{48,96},{96,144},{144,192},{192,240},{240,288},{288,336},{3... | collective-permute-start | bytes 709640 | tf_op jit(solution)/shard_map/ppermute | solution.py:100
  115.1 2.0 %collective-permute-done.9 = bf16[924,128]{1,0:T(8,128)(2,1)S(1)} collective-permute-done((bf16[924,128]{1,0:T(8,128)(2,1)S(1)}, bf16[924,128]{1,0:T(8,128)(2,1)S(1)}, u32[]{:S(2)}, u32[]{:S(2)}) %collective-permute-start.9) | collective-permute-done | bytes 236576 | tf_op jit(solution)/shard_map/ppermute | solution.py:100
  117.2 5.6 %collective-permute-start.10 = (bf16[924,128]{1,0:T(8,128)(2,1)S(1)}, bf16[924,128]{1,0:T(8,128)(2,1)S(1)}, u32[]{:S(2)}, u32[]{:S(2)}) collective-permute-start(bf16[924,128]{1,0:T(8,128)(2,1)S(1)} %fusion.3), channel_id=1, source_target_pairs={{0,48},{48,96},{96,144},{144,192},{192,240},{240,288},{288,336},{3... | collective-permute-start | bytes 709640 | tf_op jit(solution)/shard_map/ppermute | solution.py:100
  126.5 5.6 %collective-permute-start.11 = (bf16[924,128]{1,0:T(8,128)(2,1)S(1)}, bf16[924,128]{1,0:T(8,128)(2,1)S(1)}, u32[]{:S(2)}, u32[]{:S(2)}) collective-permute-start(bf16[924,128]{1,0:T(8,128)(2,1)S(1)} %fusion.4), channel_id=1, source_target_pairs={{0,48},{48,96},{96,144},{144,192},{192,240},{240,288},{288,336},{3... | collective-permute-start | bytes 709640 | tf_op jit(solution)/shard_map/ppermute | solution.py:100
  132.9 3.5 %collective-permute-start.7 = (bf16[128,4096]{1,0:T(8,128)(2,1)S(1)}, bf16[128,4096]{1,0:T(8,128)(2,1)S(1)}, u32[]{:S(2)}, u32[]{:S(2)}) collective-permute-start(bf16[128,4096]{1,0:T(8,128)(2,1)S(1)} %fusion), channel_id=1, source_target_pairs={{1,0},{2,1},{3,2},{4,3},{5,4},{6,5},{7,6},{8,7},{9,8},{10,9},{11,1... | collective-permute-start | bytes 3145736 | tf_op jit(solution)/shard_map/ppermute | solution.py:13
  138.4 5.1 %collective-permute-start.12 = (bf16[924,128]{1,0:T(8,128)(2,1)S(1)}, bf16[924,128]{1,0:T(8,128)(2,1)S(1)}, u32[]{:S(2)}, u32[]{:S(2)}) collective-permute-start(bf16[924,128]{1,0:T(8,128)(2,1)S(1)} %fusion.5), channel_id=1, source_target_pairs={{0,48},{48,96},{96,144},{144,192},{192,240},{240,288},{288,336},{3... | collective-permute-start | bytes 709640 | tf_op jit(solution)/shard_map/ppermute | solution.py:100
  143.8 2.4 %collective-permute-done.17 = bf16[924,128]{1,0:T(8,128)(2,1)S(1)} collective-permute-done((bf16[924,128]{1,0:T(8,128)(2,1)S(1)}, bf16[924,128]{1,0:T(8,128)(2,1)S(1)}, u32[]{:S(2)}, u32[]{:S(2)}) %collective-permute-start.17) | collective-permute-done | bytes 236576 | tf_op jit(solution)/shard_map/ppermute | solution.py:101
  148.2 5.1 %collective-permute-start.13 = (bf16[924,128]{1,0:T(8,128)(2,1)S(1)}, bf16[924,128]{1,0:T(8,128)(2,1)S(1)}, u32[]{:S(2)}, u32[]{:S(2)}) collective-permute-start(bf16[924,128]{1,0:T(8,128)(2,1)S(1)} %fusion.6), channel_id=1, source_target_pairs={{0,48},{48,96},{96,144},{144,192},{192,240},{240,288},{288,336},{3... | collective-permute-start | bytes 709640 | tf_op jit(solution)/shard_map/ppermute | solution.py:100
  157.5 7.2 %collective-permute-done.19 = bf16[924,128]{1,0:T(8,128)(2,1)S(1)} collective-permute-done((bf16[924,128]{1,0:T(8,128)(2,1)S(1)}, bf16[924,128]{1,0:T(8,128)(2,1)S(1)}, u32[]{:S(2)}, u32[]{:S(2)}) %collective-permute-start.19) | collective-permute-done | bytes 236576 | tf_op jit(solution)/shard_map/ppermute | solution.py:101
  165.9 2.3 %copy.126 = bf16[1,1,128,4096]{3,2,1,0:T(8,128)(2,1)} copy(bf16[1,1,128,4096]{3,2,1,0:T(8,128)(2,1)} %bitcast.246) | data formatting | bytes 2097152
  (104 shorter events, 34.3 us)
Async XLA Ops:
  0.6 62.6 %copy-start = (bf16[4096,308]{0,1:T(8,128)(2,1)S(1)}, bf16[4096,308]{0,1:T(8,128)(2,1)}, u32[]{:S(2)}) copy-start(bf16[4096,308]{0,1:T(8,128)(2,1)} %param.10) | copy-start | bytes 7569412
  0.6 11.9 %copy-start.8 = (s32[1,1,128]{2,1,0:T(1,128)S(1)}, s32[1,1,128]{2,1,0:T(1,128)}, u32[]{:S(2)}) copy-start(s32[1,1,128]{2,1,0:T(1,128)} %param.14) | copy-start | bytes 1540
  0.7 12.0 %copy-start.9 = (s32[1,1,4]{2,1,0:T(1,128)S(1)}, s32[1,1,4]{2,1,0:T(1,128)}, u32[]{:S(2)}) copy-start(s32[1,1,4]{2,1,0:T(1,128)} %param.15) | copy-start | bytes 52
  5.2 23.4 %collective-permute-start.3 = (bf16[128,2048]{1,0:T(8,128)(2,1)}, bf16[128,2048]{1,0:T(8,128)(2,1)}, u32[]{:S(2)}, u32[]{:S(2)}) collective-permute-start(bf16[128,2048]{1,0:T(8,128)(2,1)} %bitcast.248), channel_id=1, source_target_pairs={{0,385},{1,386},{2,387},{3,388},{4,389},{5,390},{6,391},{7,392},{8... | collective-permute-start | bytes 1572872 | tf_op jit(solution)/shard_map/ppermute | solution.py:128
  9.5 51.5 %collective-permute-start.1 = (bf16[128,4096]{1,0:T(8,128)(2,1)}, bf16[128,4096]{1,0:T(8,128)(2,1)}, u32[]{:S(2)}, u32[]{:S(2)}) collective-permute-start(bf16[128,4096]{1,0:T(8,128)(2,1)} %bitcast.245), channel_id=1, source_target_pairs={{47,0},{0,1},{1,2},{2,3},{3,4},{4,5},{5,6},{6,7},{7,8},{8,9},{9,10... | collective-permute-start | bytes 3145736 | tf_op jit(solution)/shard_map/ppermute | solution.py:13
  15.0 4.7 %copy-start.4 = (bf16[1,1,128,4096]{2,3,1,0:T(8,128)(2,1)S(1)}, bf16[1,1,128,4096]{2,3,1,0:T(8,128)(2,1)}, u32[]{:S(2)}) copy-start(bf16[1,1,128,4096]{2,3,1,0:T(8,128)(2,1)} %copy.85) | copy-start | bytes 3145732
  17.5 40.5 %collective-permute-start = (bf16[128,4096]{0,1:T(8,128)(2,1)}, bf16[128,4096]{0,1:T(8,128)(2,1)}, u32[]{:S(2)}, u32[]{:S(2)}) collective-permute-start(bf16[128,4096]{0,1:T(8,128)(2,1)} %fusion.251), channel_id=1, source_target_pairs={{47,0},{0,1},{1,2},{2,3},{3,4},{4,5},{5,6},{6,7},{7,8},{8,9},{9,10... | collective-permute-start | bytes 3145736 | tf_op jit(solution)/shard_map/ppermute | solution.py:13
  21.0 35.7 %collective-permute-start.4 = (bf16[128,2048]{1,0:T(8,128)(2,1)}, bf16[128,2048]{1,0:T(8,128)(2,1)}, u32[]{:S(2)}, u32[]{:S(2)}) collective-permute-start(bf16[128,2048]{1,0:T(8,128)(2,1)} %bitcast.249), channel_id=1, source_target_pairs={{0,385},{1,386},{2,387},{3,388},{4,389},{5,390},{6,391},{7,392},{8... | collective-permute-start | bytes 1572872 | tf_op jit(solution)/shard_map/ppermute | solution.py:128
  58.0 3.1 %copy-start.2 = (bf16[4096,308]{0,1:T(8,128)(2,1)S(1)}, bf16[4096,308]{0,1:T(8,128)(2,1)}, u32[]{:S(2)}) copy-start(bf16[4096,308]{0,1:T(8,128)(2,1)} %param.11) | copy-start | bytes 7569412
  65.3 0.6 copy-start.6
  66.7 9.7 %collective-permute-start.2 = (bf16[128,924]{0,1:T(8,128)(2,1)}, bf16[128,924]{0,1:T(8,128)(2,1)S(1)}, u32[]{:S(2)}, u32[]{:S(2)}) collective-permute-start(bf16[128,924]{0,1:T(8,128)(2,1)} %pad_maximum_fusion.2), channel_id=1, source_target_pairs={{0,384},{48,432},{96,480},{144,528},{192,576},{240,624},{288,672},... | collective-permute-start | bytes 709640 | tf_op jit(solution)/shard_map/ppermute | solution.py:62
  71.8 5.5 %copy-start.1 = (bf16[128,2048]{0,1:T(8,128)(2,1)S(1)}, bf16[128,2048]{0,1:T(8,128)(2,1)}, u32[]{:S(2)}) copy-start(bf16[128,2048]{0,1:T(8,128)(2,1)} %copy.89) | copy-start | bytes 1572868
  73.0 4.9 %copy-start.7 = (bf16[128,308]{0,1:T(8,128)(2,1)S(1)}, bf16[128,308]{0,1:T(8,128)(2,1)}, u32[]{:S(2)}) copy-start(bf16[128,308]{0,1:T(8,128)(2,1)} %copy-done.6) | copy-start | bytes 236548
  83.0 11.3 %collective-permute-start.6 = (bf16[924,128]{1,0:T(8,128)(2,1)S(1)}, bf16[924,128]{1,0:T(8,128)(2,1)S(1)}, u32[]{:S(2)}, u32[]{:S(2)}) collective-permute-start(bf16[924,128]{1,0:T(8,128)(2,1)S(1)} %pad_maximum_fusion.4), channel_id=1, source_target_pairs={{0,336},{48,0},{96,48},{144,96},{192,144},{240,192},{288,240},{336... | collective-permute-start | bytes 709640 | tf_op jit(solution)/shard_map/ppermute | solution.py:101
  85.4 10.4 %collective-permute-start.5 = (bf16[924,128]{1,0:T(8,128)(2,1)S(1)}, bf16[924,128]{1,0:T(8,128)(2,1)S(1)}, u32[]{:S(2)}, u32[]{:S(2)}) collective-permute-start(bf16[924,128]{1,0:T(8,128)(2,1)S(1)} %pad_maximum_fusion.3), channel_id=1, source_target_pairs={{0,48},{48,96},{96,144},{144,192},{192,240},{240,288},{288,336},{3... | collective-permute-start | bytes 709640 | tf_op jit(solution)/shard_map/ppermute | solution.py:100
  95.8 11.0 %collective-permute-start.8 = (bf16[924,128]{1,0:T(8,128)(2,1)S(1)}, bf16[924,128]{1,0:T(8,128)(2,1)S(1)}, u32[]{:S(2)}, u32[]{:S(2)}) collective-permute-start(bf16[924,128]{1,0:T(8,128)(2,1)S(1)} %fusion.1), channel_id=1, source_target_pairs={{0,48},{48,96},{96,144},{144,192},{192,240},{240,288},{288,336},{3... | collective-permute-start | bytes 709640 | tf_op jit(solution)/shard_map/ppermute | solution.py:100
  101.7 21.1 %copy-start.3 = (bf16[4096,308]{0,1:T(8,128)(2,1)S(1)}, bf16[4096,308]{0,1:T(8,128)(2,1)}, u32[]{:S(2)}) copy-start(bf16[4096,308]{0,1:T(8,128)(2,1)} %param.11) | copy-start | bytes 7569412
  101.7 11.4 %collective-permute-start.14 = (bf16[924,128]{1,0:T(8,128)(2,1)S(1)}, bf16[924,128]{1,0:T(8,128)(2,1)S(1)}, u32[]{:S(2)}, u32[]{:S(2)}) collective-permute-start(bf16[924,128]{1,0:T(8,128)(2,1)S(1)} %fusion.8), channel_id=1, source_target_pairs={{0,336},{48,0},{96,48},{144,96},{192,144},{240,192},{288,240},{336... | collective-permute-start | bytes 709640 | tf_op jit(solution)/shard_map/ppermute | solution.py:101
  106.9 10.2 %collective-permute-start.9 = (bf16[924,128]{1,0:T(8,128)(2,1)S(1)}, bf16[924,128]{1,0:T(8,128)(2,1)S(1)}, u32[]{:S(2)}, u32[]{:S(2)}) collective-permute-start(bf16[924,128]{1,0:T(8,128)(2,1)S(1)} %fusion.2), channel_id=1, source_target_pairs={{0,48},{48,96},{96,144},{144,192},{192,240},{240,288},{288,336},{3... | collective-permute-start | bytes 709640 | tf_op jit(solution)/shard_map/ppermute | solution.py:100
  113.2 10.4 %collective-permute-start.15 = (bf16[924,128]{1,0:T(8,128)(2,1)S(1)}, bf16[924,128]{1,0:T(8,128)(2,1)S(1)}, u32[]{:S(2)}, u32[]{:S(2)}) collective-permute-start(bf16[924,128]{1,0:T(8,128)(2,1)S(1)} %fusion.9), channel_id=1, source_target_pairs={{0,336},{48,0},{96,48},{144,96},{192,144},{240,192},{288,240},{336... | collective-permute-start | bytes 709640 | tf_op jit(solution)/shard_map/ppermute | solution.py:101
  117.2 9.2 %collective-permute-start.10 = (bf16[924,128]{1,0:T(8,128)(2,1)S(1)}, bf16[924,128]{1,0:T(8,128)(2,1)S(1)}, u32[]{:S(2)}, u32[]{:S(2)}) collective-permute-start(bf16[924,128]{1,0:T(8,128)(2,1)S(1)} %fusion.3), channel_id=1, source_target_pairs={{0,48},{48,96},{96,144},{144,192},{192,240},{240,288},{288,336},{3... | collective-permute-start | bytes 709640 | tf_op jit(solution)/shard_map/ppermute | solution.py:100
  123.7 12.7 %collective-permute-start.16 = (bf16[924,128]{1,0:T(8,128)(2,1)S(1)}, bf16[924,128]{1,0:T(8,128)(2,1)S(1)}, u32[]{:S(2)}, u32[]{:S(2)}) collective-permute-start(bf16[924,128]{1,0:T(8,128)(2,1)S(1)} %fusion.10), channel_id=1, source_target_pairs={{0,336},{48,0},{96,48},{144,96},{192,144},{240,192},{288,240},{336... | collective-permute-start | bytes 709640 | tf_op jit(solution)/shard_map/ppermute | solution.py:101
  126.5 11.9 %collective-permute-start.11 = (bf16[924,128]{1,0:T(8,128)(2,1)S(1)}, bf16[924,128]{1,0:T(8,128)(2,1)S(1)}, u32[]{:S(2)}, u32[]{:S(2)}) collective-permute-start(bf16[924,128]{1,0:T(8,128)(2,1)S(1)} %fusion.4), channel_id=1, source_target_pairs={{0,48},{48,96},{96,144},{144,192},{192,240},{240,288},{288,336},{3... | collective-permute-start | bytes 709640 | tf_op jit(solution)/shard_map/ppermute | solution.py:100
  132.9 20.7 %collective-permute-start.7 = (bf16[128,4096]{1,0:T(8,128)(2,1)S(1)}, bf16[128,4096]{1,0:T(8,128)(2,1)S(1)}, u32[]{:S(2)}, u32[]{:S(2)}) collective-permute-start(bf16[128,4096]{1,0:T(8,128)(2,1)S(1)} %fusion), channel_id=1, source_target_pairs={{1,0},{2,1},{3,2},{4,3},{5,4},{6,5},{7,6},{8,7},{9,8},{10,9},{11,1... | collective-permute-start | bytes 3145736 | tf_op jit(solution)/shard_map/ppermute | solution.py:13
  136.4 9.7 %collective-permute-start.17 = (bf16[924,128]{1,0:T(8,128)(2,1)S(1)}, bf16[924,128]{1,0:T(8,128)(2,1)S(1)}, u32[]{:S(2)}, u32[]{:S(2)}) collective-permute-start(bf16[924,128]{1,0:T(8,128)(2,1)S(1)} %fusion.11), channel_id=1, source_target_pairs={{0,336},{48,0},{96,48},{144,96},{192,144},{240,192},{288,240},{336... | collective-permute-start | bytes 709640 | tf_op jit(solution)/shard_map/ppermute | solution.py:101
  138.4 9.7 %collective-permute-start.12 = (bf16[924,128]{1,0:T(8,128)(2,1)S(1)}, bf16[924,128]{1,0:T(8,128)(2,1)S(1)}, u32[]{:S(2)}, u32[]{:S(2)}) collective-permute-start(bf16[924,128]{1,0:T(8,128)(2,1)S(1)} %fusion.5), channel_id=1, source_target_pairs={{0,48},{48,96},{96,144},{144,192},{192,240},{240,288},{288,336},{3... | collective-permute-start | bytes 709640 | tf_op jit(solution)/shard_map/ppermute | solution.py:100
  146.2 9.2 %collective-permute-start.18 = (bf16[924,128]{1,0:T(8,128)(2,1)S(1)}, bf16[924,128]{1,0:T(8,128)(2,1)S(1)}, u32[]{:S(2)}, u32[]{:S(2)}) collective-permute-start(bf16[924,128]{1,0:T(8,128)(2,1)S(1)} %fusion.12), channel_id=1, source_target_pairs={{0,336},{48,0},{96,48},{144,96},{192,144},{240,192},{288,240},{336... | collective-permute-start | bytes 709640 | tf_op jit(solution)/shard_map/ppermute | solution.py:101
  148.2 9.2 %collective-permute-start.13 = (bf16[924,128]{1,0:T(8,128)(2,1)S(1)}, bf16[924,128]{1,0:T(8,128)(2,1)S(1)}, u32[]{:S(2)}, u32[]{:S(2)}) collective-permute-start(bf16[924,128]{1,0:T(8,128)(2,1)S(1)} %fusion.6), channel_id=1, source_target_pairs={{0,48},{48,96},{96,144},{144,192},{192,240},{240,288},{288,336},{3... | collective-permute-start | bytes 709640 | tf_op jit(solution)/shard_map/ppermute | solution.py:100
  153.6 11.2 %copy-start.5 = (bf16[128,4096]{1,0:T(8,128)(2,1)}, bf16[128,4096]{1,0:T(8,128)(2,1)S(1)}, u32[]{:S(2)}) copy-start(bf16[128,4096]{1,0:T(8,128)(2,1)S(1)} %collective-permute-done.7) | copy-start | bytes 3145732
  155.5 9.2 %collective-permute-start.19 = (bf16[924,128]{1,0:T(8,128)(2,1)S(1)}, bf16[924,128]{1,0:T(8,128)(2,1)S(1)}, u32[]{:S(2)}, u32[]{:S(2)}) collective-permute-start(bf16[924,128]{1,0:T(8,128)(2,1)S(1)} %fusion.13), channel_id=1, source_target_pairs={{0,336},{48,0},{96,48},{144,96},{192,144},{240,192},{288,240},{336... | collective-permute-start | bytes 709640 | tf_op jit(solution)/shard_map/ppermute | solution.py:101

commit v9 on v8

--- a/solution.py
+++ b/solution.py
@@ -79,23 +79,23 @@
     y = lax.axis_index("dp") % ny
     rows, width = tok_all.shape
     lane = width // ny // 2
-    tok_view = tok_all.reshape(rows, ny * 2, lane)
-    grad_view = grad_all.reshape(rows, ny * 2, lane)
+    tok_view = tok_all.reshape(rows, ny, 2 * lane)
+    grad_view = grad_all.reshape(rows, ny, 2 * lane)
     d_both = mixed_all[:, : 2 * cols]
     hidden = mixed_all[:, 2 * cols :]
 
-    def chunk(c, h):
-        b = c * 2 + h
-        tok_part = lax.dynamic_index_in_dim(tok_view, b, axis=1, keepdims=False)
-        grad_part = lax.dynamic_index_in_dim(grad_view, b, axis=1, keepdims=False)
-        first = contract_rows(d_both, tok_part)
-        second = contract_rows(hidden, grad_part)
-        return jnp.concatenate([first, second], axis=0)
+    def part_f(c):
+        tok_part = lax.dynamic_index_in_dim(tok_view, c, axis=1, keepdims=False)
+        return contract_rows(d_both, tok_part)
+
+    def part_b(c):
+        grad_part = lax.dynamic_index_in_dim(grad_view, c, axis=1, keepdims=False)
+        return contract_rows(hidden, grad_part)
 
     fwd = [(a * ny + b, a * ny + (b + 1) % ny) for a in range(nx) for b in range(ny)]
     bwd = [(a * ny + b, a * ny + (b - 1) % ny) for a in range(nx) for b in range(ny)]
-    acc_f = chunk((y + ny - 1) % ny, 0)
-    acc_b = chunk((y + 1) % ny, 1)
+    acc_f = part_f((y + ny - 1) % ny)
+    acc_b = part_b((y + 1) % ny)
     for s in range(ny - 1):
         recv_f = lax.ppermute(acc_f.astype(jnp.bfloat16), "dp", fwd)
         recv_b = lax.ppermute(acc_b.astype(jnp.bfloat16), "dp", bwd)
@@ -103,9 +103,9 @@
             recv_f, recv_b, late_args = lax.optimization_barrier((recv_f, recv_b, late_args))
             late_out = late(*late_args)
         scale = 1.0 / n if s == ny - 2 else 1.0
-        acc_f = (recv_f.astype(jnp.float32) + chunk((y + 2 * ny - 2 - s) % ny, 0)) * scale
-        acc_b = (recv_b.astype(jnp.float32) + chunk((y + 2 + s) % ny, 1)) * scale
-    total = jnp.concatenate([acc_f, acc_b], axis=1).reshape(3, cols, 2 * lane)
+        acc_f = (recv_f.astype(jnp.float32) + part_f((y + 2 * ny - 2 - s) % ny)) * scale
+        acc_b = (recv_b.astype(jnp.float32) + part_b((y + 2 + s) % ny)) * scale
+    total = jnp.concatenate([acc_f, acc_b], axis=0).reshape(3, cols, 2 * lane)
     return jnp.transpose(total, (0, 2, 1)), late_out
 
 

time: 169 us -> 189 us (1.12)
  the two profiles are of different devices: /device:TPU:24 before, /device:TPU:32 now
where the time goes in v9:
time: 189 us; the launch traced here: 187 us
  starting transfers between devices  70 us (37%)
  waiting for transfers between devices  53.9 us (29%)
  matrix products  31.4 us (17%)
  local copies, waits for them, and re-layouts  20.7 us (11%)
  other arithmetic  8.8 us (5%)
  between operations  2.29 us (1%)
    ppermute x7, starting transfers between devices, reduce_over_y(): recv_b = lax.ppermute(acc_b.astype(jnp.bfloat16), 'dp', bwd)  36.1 us
    ppermute x2, waiting for transfers between devices, shards(): tok_peer, grad_peer = lax.ppermute(other, ('dp', 'blk'), diagonal)  28.7 us
    dot_general x16, matrix products, contract_rows(): lax.dot_general(left, right, (((0,), (0,)), ((), ())), preferred_element_...  21.6 us
    ppermute x7, waiting for transfers between devices, reduce_over_y(): recv_f = lax.ppermute(acc_f.astype(jnp.bfloat16), 'dp', fwd)  18.9 us
    ppermute x7, starting transfers between devices, reduce_over_y(): recv_f = lax.ppermute(acc_f.astype(jnp.bfloat16), 'dp', fwd)  14.2 us
    ppermute x2, starting transfers between devices, shards(): tok_peer, grad_peer = lax.ppermute(other, ('dp', 'blk'), diagonal)  11.2 us
    unnamed x43, local copies, waits for them, and re-layouts  6.9 us
    ppermute x3, starting transfers between devices, shifted(): return lax.ppermute(block, axis, route)  5.74 us
  transfers between devices with their start and end apart: 20, of which 10 were waited for; matrix products, arithmetic and copies ran while one was open for 21% of the time, Pallas kernels for 0%

profile of v9, /device:TPU:32, one launch (start us, length us, event | category | flops | bytes accessed | tf_op | source)
XLA Modules:
  0.0 187.1 jit_solution(12100795711037136773)
XLA Ops:
  3.6 2.3 %copy.53 = bf16[1,1,128,4096]{2,3,1,0:T(8,128)(2,1)} copy(bf16[1,1,128,4096]{3,2,1,0:T(8,128)(2,1)} %param.9) | data formatting | bytes 2097152 | tf_op args[1]
  5.9 2.5 %fusion.155 = bf16[128,4096]{0,1:T(8,128)(2,1)} fusion(f32[128]{0:T(128)S(1)} %select_reduce_fusion, bf16[1,1,128,4096]{2,3,1,0:T(8,128)(2,1)} %copy.53), kind=kLoop, calls=%fused_computation.160 | loop fusion | flops 1572864 | bytes 2097664 | tf_op jit(solution)/shard_map/reshape | solution.py:117
  13.6 5.8 %collective-permute-start.5 = (bf16[128,2048]{1,0:T(8,128)(2,1)}, bf16[128,2048]{1,0:T(8,128)(2,1)}, u32[]{:S(2)}, u32[]{:S(2)}) collective-permute-start(bf16[128,2048]{1,0:T(8,128)(2,1)} %bitcast.171), channel_id=1, source_target_pairs={{0,385},{1,386},{2,387},{3,388},{4,389},{5,390},{6,391},{7,392},{8... | collective-permute-start | bytes 1572872 | tf_op jit(solution)/shard_map/ppermute | solution.py:128
  21.4 2.3 %copy.55 = bf16[1,1,128,4096]{2,3,1,0:T(8,128)(2,1)} copy(bf16[1,1,128,4096]{3,2,1,0:T(8,128)(2,1)} %param.8) | data formatting | bytes 2097152 | tf_op args[0]
  25.7 5.4 %collective-permute-start.3 = (bf16[128,2048]{1,0:T(8,128)(2,1)}, bf16[128,2048]{1,0:T(8,128)(2,1)}, u32[]{:S(2)}, u32[]{:S(2)}) collective-permute-start(bf16[128,2048]{1,0:T(8,128)(2,1)} %bitcast.172), channel_id=1, source_target_pairs={{0,385},{1,386},{2,387},{3,388},{4,389},{5,390},{6,391},{7,392},{8... | collective-permute-start | bytes 1572872 | tf_op jit(solution)/shard_map/ppermute | solution.py:128
  31.1 15.3 %collective-permute-done.5 = bf16[128,2048]{1,0:T(8,128)(2,1)} collective-permute-done((bf16[128,2048]{1,0:T(8,128)(2,1)}, bf16[128,2048]{1,0:T(8,128)(2,1)}, u32[]{:S(2)}, u32[]{:S(2)}) %collective-permute-start.5) | collective-permute-done | bytes 524320 | tf_op jit(solution)/shard_map/ppermute | solution.py:128
  46.5 2.0 %copy.60 = bf16[128,2048]{0,1:T(8,128)(2,1)} copy(bf16[128,2048]{1,0:T(8,128)(2,1)} %collective-permute-done.5) | data formatting | bytes 1048576 | tf_op jit(solution)/shard_map/ppermute | solution.py:128
  48.5 13.4 %collective-permute-done.3 = bf16[128,2048]{1,0:T(8,128)(2,1)} collective-permute-done((bf16[128,2048]{1,0:T(8,128)(2,1)}, bf16[128,2048]{1,0:T(8,128)(2,1)}, u32[]{:S(2)}, u32[]{:S(2)}) %collective-permute-start.3) | collective-permute-done | bytes 524320 | tf_op jit(solution)/shard_map/ppermute | solution.py:128
  63.2 3.0 %fusion.134 = f32[128,308]{0,1:T(8,128)S(1)} fusion(bf16[128,4096]{0,1:T(8,128)(2,1)} %collective-permute-done, bf16[4096,308]{0,1:T(8,128)(2,1)} %param.12), kind=kOutput, calls=%fused_computation.157 | convolution fusion | flops 322961408 | bytes 3729408 | tf_op jit(solution)/shard_map/dot_general | solution.py:56
  66.3 2.1 %fusion.135 = f32[128,308]{0,1:T(8,128)S(1)} fusion(bf16[128,4096]{1,0:T(8,128)(2,1)} %collective-permute-done.1, bf16[4096,308]{0,1:T(8,128)(2,1)S(1)} %copy-done.9), kind=kOutput, calls=%fused_computation.158 | convolution fusion | flops 322961408 | bytes 3729408 | tf_op jit(solution)/shard_map/dot_general | solution.py:52
  68.4 2.1 %multiply_convert_fusion.3 = (bf16[128,308]{0,1:T(8,128)(2,1)S(1)}, bf16[128,308]{0,1:T(8,128)(2,1)S(1)}, bf16[128,308]{0,1:T(8,128)(2,1)S(1)}) fusion(f32[128,308]{0,1:T(8,128)S(1)} %fusion.134, f32[128,308]{0,1:T(8,128)S(1)} %fusion.135, bf16[128,4096]{1,0:T(8,128)(2,1)} %collective-permute-done.1, bf16[4096,308]{0,1:T(8,128)(2,1)S(1)} %copy-done), kind=kOutput, calls=%fused_computation.57 | convolution fusion | flops 323552768 | bytes 4123648 | tf_op jit(solution)/shard_map/dot_general | solution.py:51
  71.3 2.7 %collective-permute-start.2 = (bf16[128,924]{0,1:T(8,128)(2,1)}, bf16[128,924]{0,1:T(8,128)(2,1)}, u32[]{:S(2)}, u32[]{:S(2)}) collective-permute-start(bf16[128,924]{0,1:T(8,128)(2,1)} %pad_maximum_fusion.2), channel_id=1, source_target_pairs={{0,384},{48,432},{96,480},{144,528},{192,576},{240,624},{288,672},... | collective-permute-start | bytes 709640 | tf_op jit(solution)/shard_map/ppermute | solution.py:62
  75.9 2.3 %copy.54 = bf16[128,4096]{0,1:T(8,128)(2,1)} copy(bf16[128,4096]{1,0:T(8,128)(2,1)} %collective-permute-done.1) | data formatting | bytes 2097152 | tf_op jit(solution)/shard_map/ppermute | solution.py:13
  83.3 2.6 %collective-permute-start.4 = (bf16[616,256]{1,0:T(8,128)(2,1)}, bf16[616,256]{1,0:T(8,128)(2,1)}, u32[]{:S(2)}, u32[]{:S(2)}) collective-permute-start(bf16[616,256]{1,0:T(8,128)(2,1)} %convolution_convert_fusion), channel_id=1, source_target_pairs={{0,48},{48,96},{96,144},{144,192},{192,240},{240,288},{288,336},{3... | collective-permute-start | bytes 946184 | tf_op jit(solution)/shard_map/ppermute | solution.py:100
  87.8 4.5 %collective-permute-start.6 = (bf16[308,256]{1,0:T(8,128)(2,1)}, bf16[308,256]{1,0:T(8,128)(2,1)}, u32[]{:S(2)}, u32[]{:S(2)}) collective-permute-start(bf16[308,256]{1,0:T(8,128)(2,1)} %convolution_convert_fusion.1), channel_id=1, source_target_pairs={{0,336},{48,0},{96,48},{144,96},{192,144},{240,192},{288,240},{336... | collective-permute-start | bytes 473096 | tf_op jit(solution)/shard_map/ppermute | solution.py:101
  92.3 3.1 %collective-permute-done.6 = bf16[308,256]{1,0:T(8,128)(2,1)} collective-permute-done((bf16[308,256]{1,0:T(8,128)(2,1)}, bf16[308,256]{1,0:T(8,128)(2,1)}, u32[]{:S(2)}, u32[]{:S(2)}) %collective-permute-start.6) | collective-permute-done | bytes 157728 | tf_op jit(solution)/shard_map/ppermute | solution.py:101
  97.3 5.6 %collective-permute-start.14 = (bf16[308,256]{1,0:T(8,128)(2,1)}, bf16[308,256]{1,0:T(8,128)(2,1)}, u32[]{:S(2)}, u32[]{:S(2)}) collective-permute-start(bf16[308,256]{1,0:T(8,128)(2,1)} %add_convert_fusion.11), channel_id=1, source_target_pairs={{0,336},{48,0},{96,48},{144,96},{192,144},{240,192},{288,240},{336... | collective-permute-start | bytes 473096 | tf_op jit(solution)/shard_map/ppermute | solution.py:101
  102.9 2.0 %add_convert_fusion.5 = bf16[616,256]{1,0:T(8,128)(2,1)} fusion(bf16[616,256]{1,0:T(8,128)(2,1)} %collective-permute-done.4, s32[]{:T(128)S(6)} %select_n.135, bf16[128,8,256]{0,2,1:T(8,128)(2,1)} %bitcast.151, bf16[128,8,256]{0,2,1:T(8,128)(2,1)S(1)} %bitcast.135, bf16[256,924]{0,1:T(8,128)(2,1)S(1)} %pad_maximum_fusion.1), kind=kOutput, calls=%fused_computation.44 | convolution fusion | flops 81475584 | bytes 1994756 | tf_op jit(solution)/shard_map/dot_general | solution.py:28
  106.9 2.0 %add_convert_fusion.10 = bf16[308,256]{1,0:T(8,128)(2,1)} fusion(bf16[308,256]{1,0:T(8,128)(2,1)} %collective-permute-done.14, bf16[256,308]{0,1:T(8,128)(2,1)} %copy-done.7, s32[]{:T(128)S(6)} %select_n.151, bf16[128,8,256]{0,2,1:T(8,128)(2,1)} %bitcast.159, bf16[128,8,256]{0,2,1:T(8,128)(2,1)} %bitcast.143), kind=kOutput, calls=%fused_computation.51 | convolution fusion | flops 40868864 | bytes 1521668 | tf_op jit(solution)/shard_map/dot_general | solution.py:28
  108.9 5.1 %collective-permute-start.15 = (bf16[308,256]{1,0:T(8,128)(2,1)}, bf16[308,256]{1,0:T(8,128)(2,1)}, u32[]{:S(2)}, u32[]{:S(2)}) collective-permute-start(bf16[308,256]{1,0:T(8,128)(2,1)} %add_convert_fusion.10), channel_id=1, source_target_pairs={{0,336},{48,0},{96,48},{144,96},{192,144},{240,192},{288,240},{336... | collective-permute-start | bytes 473096 | tf_op jit(solution)/shard_map/ppermute | solution.py:101
  115.3 2.0 %add_convert_fusion.4 = bf16[616,256]{1,0:T(8,128)(2,1)} fusion(bf16[616,256]{1,0:T(8,128)(2,1)} %collective-permute-done.8, s32[]{:T(128)S(6)} %select_n.137, bf16[128,8,256]{0,2,1:T(8,128)(2,1)} %bitcast.152, bf16[128,8,256]{0,2,1:T(8,128)(2,1)S(1)} %bitcast.136, bf16[256,924]{0,1:T(8,128)(2,1)S(1)} %pad_maximum_fusion.1), kind=kOutput, calls=%fused_computation.43 | convolution fusion | flops 81475584 | bytes 1994756 | tf_op jit(solution)/shard_map/dot_general | solution.py:28
  120.8 5.1 %collective-permute-start.16 = (bf16[308,256]{1,0:T(8,128)(2,1)S(1)}, bf16[308,256]{1,0:T(8,128)(2,1)S(1)}, u32[]{:S(2)}, u32[]{:S(2)}) collective-permute-start(bf16[308,256]{1,0:T(8,128)(2,1)S(1)} %add_convert_fusion.9), channel_id=1, source_target_pairs={{0,336},{48,0},{96,48},{144,96},{192,144},{240,192},{288,240},{336... | collective-permute-start | bytes 473096 | tf_op jit(solution)/shard_map/ppermute | solution.py:101
  126.0 4.8 %collective-permute-done.9 = bf16[616,256]{1,0:T(8,128)(2,1)} collective-permute-done((bf16[616,256]{1,0:T(8,128)(2,1)}, bf16[616,256]{1,0:T(8,128)(2,1)}, u32[]{:S(2)}, u32[]{:S(2)}) %collective-permute-start.9) | collective-permute-done | bytes 315424 | tf_op jit(solution)/shard_map/ppermute | solution.py:100
  132.1 2.1 %collective-permute-start.10 = (bf16[616,256]{1,0:T(8,128)(2,1)S(1)}, bf16[616,256]{1,0:T(8,128)(2,1)S(1)}, u32[]{:S(2)}, u32[]{:S(2)}) collective-permute-start(bf16[616,256]{1,0:T(8,128)(2,1)S(1)} %add_convert_fusion.3), channel_id=1, source_target_pairs={{0,48},{48,96},{96,144},{144,192},{192,240},{240,288},{288,336},{3... | collective-permute-start | bytes 946184 | tf_op jit(solution)/shard_map/ppermute | solution.py:100
  135.3 5.1 %collective-permute-start.17 = (bf16[308,256]{1,0:T(8,128)(2,1)S(1)}, bf16[308,256]{1,0:T(8,128)(2,1)S(1)}, u32[]{:S(2)}, u32[]{:S(2)}) collective-permute-start(bf16[308,256]{1,0:T(8,128)(2,1)S(1)} %add_convert_fusion.8), channel_id=1, source_target_pairs={{0,336},{48,0},{96,48},{144,96},{192,144},{240,192},{288,240},{336... | collective-permute-start | bytes 473096 | tf_op jit(solution)/shard_map/ppermute | solution.py:101
  149.1 5.1 %collective-permute-start.18 = (bf16[308,256]{1,0:T(8,128)(2,1)}, bf16[308,256]{1,0:T(8,128)(2,1)}, u32[]{:S(2)}, u32[]{:S(2)}) collective-permute-start(bf16[308,256]{1,0:T(8,128)(2,1)} %add_convert_fusion.7), channel_id=1, source_target_pairs={{0,336},{48,0},{96,48},{144,96},{192,144},{240,192},{288,240},{336... | collective-permute-start | bytes 473096 | tf_op jit(solution)/shard_map/ppermute | solution.py:101
  158.6 2.0 %add_convert_fusion.6 = bf16[308,256]{1,0:T(8,128)(2,1)} fusion(bf16[308,256]{1,0:T(8,128)(2,1)} %collective-permute-done.18, bf16[256,308]{0,1:T(8,128)(2,1)} %copy-done.7, s32[]{:T(128)S(6)} %select_n.131, bf16[128,8,256]{0,2,1:T(8,128)(2,1)} %bitcast.161, bf16[128,8,256]{0,2,1:T(8,128)(2,1)} %bitcast.145), kind=kOutput, calls=%fused_computation.47 | convolution fusion | flops 40868864 | bytes 1521668 | tf_op jit(solution)/shard_map/dot_general | solution.py:28
  160.5 5.6 %collective-permute-start.19 = (bf16[308,256]{1,0:T(8,128)(2,1)}, bf16[308,256]{1,0:T(8,128)(2,1)}, u32[]{:S(2)}, u32[]{:S(2)}) collective-permute-start(bf16[308,256]{1,0:T(8,128)(2,1)} %add_convert_fusion.6), channel_id=1, source_target_pairs={{0,336},{48,0},{96,48},{144,96},{192,144},{240,192},{288,240},{336... | collective-permute-start | bytes 473096 | tf_op jit(solution)/shard_map/ppermute | solution.py:101
  166.1 2.1 %collective-permute-done.12 = bf16[616,256]{1,0:T(8,128)(2,1)} collective-permute-done((bf16[616,256]{1,0:T(8,128)(2,1)}, bf16[616,256]{1,0:T(8,128)(2,1)}, u32[]{:S(2)}, u32[]{:S(2)}) %collective-permute-start.12) | collective-permute-done | bytes 315424 | tf_op jit(solution)/shard_map/ppermute | solution.py:100
  168.3 2.0 %add_convert_fusion = bf16[616,256]{1,0:T(8,128)(2,1)} fusion(bf16[616,256]{1,0:T(8,128)(2,1)} %collective-permute-done.12, s32[]{:T(128)S(6)} %select_n.145, bf16[128,8,256]{0,2,1:T(8,128)(2,1)} %bitcast.154, bf16[128,8,256]{0,2,1:T(8,128)(2,1)S(1)} %bitcast.140, bf16[256,924]{0,1:T(8,128)(2,1)S(1)} %pad_maximum_fusion.1), kind=kOutput, calls=%fused_computation.39 | convolution fusion | flops 81475584 | bytes 1994756 | tf_op jit(solution)/shard_map/dot_general | solution.py:28
  173.5 8.9 %collective-permute-done.13 = bf16[616,256]{1,0:T(8,128)(2,1)} collective-permute-done((bf16[616,256]{1,0:T(8,128)(2,1)}, bf16[616,256]{1,0:T(8,128)(2,1)}, u32[]{:S(2)}, u32[]{:S(2)}) %collective-permute-start.13) | collective-permute-done | bytes 315424 | tf_op jit(solution)/shard_map/ppermute | solution.py:100
  184.8 2.3 %copy.78 = bf16[1,1,128,4096]{3,2,1,0:T(8,128)(2,1)} copy(bf16[1,1,128,4096]{3,2,1,0:T(8,128)(2,1)} %bitcast.18) | data formatting | bytes 2097152
  (92 shorter events, 51.8 us)
Async XLA Ops:
  0.6 67.8 %copy-start = (bf16[4096,308]{0,1:T(8,128)(2,1)S(1)}, bf16[4096,308]{0,1:T(8,128)(2,1)}, u32[]{:S(2)}) copy-start(bf16[4096,308]{0,1:T(8,128)(2,1)} %param.10) | copy-start | bytes 7569412
  8.4 54.8 %collective-permute-start = (bf16[128,4096]{0,1:T(8,128)(2,1)}, bf16[128,4096]{0,1:T(8,128)(2,1)}, u32[]{:S(2)}, u32[]{:S(2)}) collective-permute-start(bf16[128,4096]{0,1:T(8,128)(2,1)} %fusion.155), channel_id=1, source_target_pairs={{47,0},{0,1},{1,2},{2,3},{3,4},{4,5},{5,6},{6,7},{7,8},{8,9},{9,10... | collective-permute-start | bytes 3145736 | tf_op jit(solution)/shard_map/ppermute | solution.py:13
  13.6 32.9 %collective-permute-start.5 = (bf16[128,2048]{1,0:T(8,128)(2,1)}, bf16[128,2048]{1,0:T(8,128)(2,1)}, u32[]{:S(2)}, u32[]{:S(2)}) collective-permute-start(bf16[128,2048]{1,0:T(8,128)(2,1)} %bitcast.171), channel_id=1, source_target_pairs={{0,385},{1,386},{2,387},{3,388},{4,389},{5,390},{6,391},{7,392},{8... | collective-permute-start | bytes 1572872 | tf_op jit(solution)/shard_map/ppermute | solution.py:128
  19.4 46.8 %collective-permute-start.1 = (bf16[128,4096]{1,0:T(8,128)(2,1)}, bf16[128,4096]{1,0:T(8,128)(2,1)}, u32[]{:S(2)}, u32[]{:S(2)}) collective-permute-start(bf16[128,4096]{1,0:T(8,128)(2,1)} %bitcast.169), channel_id=1, source_target_pairs={{47,0},{0,1},{1,2},{2,3},{3,4},{4,5},{5,6},{6,7},{7,8},{8,9},{9,10... | collective-permute-start | bytes 3145736 | tf_op jit(solution)/shard_map/ppermute | solution.py:13
  25.7 36.2 %collective-permute-start.3 = (bf16[128,2048]{1,0:T(8,128)(2,1)}, bf16[128,2048]{1,0:T(8,128)(2,1)}, u32[]{:S(2)}, u32[]{:S(2)}) collective-permute-start(bf16[128,2048]{1,0:T(8,128)(2,1)} %bitcast.172), channel_id=1, source_target_pairs={{0,385},{1,386},{2,387},{3,388},{4,389},{5,390},{6,391},{7,392},{8... | collective-permute-start | bytes 1572872 | tf_op jit(solution)/shard_map/ppermute | solution.py:128
  70.5 8.8 %copy-start.12 = (bf16[128,308]{0,1:T(8,128)(2,1)}, bf16[128,308]{0,1:T(8,128)(2,1)S(1)}, u32[]{:S(2)}) copy-start(bf16[128,308]{0,1:T(8,128)(2,1)S(1)} %get-tuple-element.6) | copy-start | bytes 236548
  70.5 8.8 %copy-start.15 = (bf16[128,308]{0,1:T(8,128)(2,1)}, bf16[128,308]{0,1:T(8,128)(2,1)S(1)}, u32[]{:S(2)}) copy-start(bf16[128,308]{0,1:T(8,128)(2,1)S(1)} %get-tuple-element.7) | copy-start | bytes 236548
  70.5 8.8 %copy-start.18 = (bf16[128,308]{0,1:T(8,128)(2,1)}, bf16[128,308]{0,1:T(8,128)(2,1)S(1)}, u32[]{:S(2)}) copy-start(bf16[128,308]{0,1:T(8,128)(2,1)S(1)} %get-tuple-element.11) | copy-start | bytes 236548
  71.3 9.8 %collective-permute-start.2 = (bf16[128,924]{0,1:T(8,128)(2,1)}, bf16[128,924]{0,1:T(8,128)(2,1)}, u32[]{:S(2)}, u32[]{:S(2)}) collective-permute-start(bf16[128,924]{0,1:T(8,128)(2,1)} %pad_maximum_fusion.2), channel_id=1, source_target_pairs={{0,384},{48,432},{96,480},{144,528},{192,576},{240,624},{288,672},... | collective-permute-start | bytes 709640 | tf_op jit(solution)/shard_map/ppermute | solution.py:62
  78.2 8.7 %copy-start.1 = (bf16[128,2048]{0,1:T(8,128)(2,1)S(1)}, bf16[128,2048]{0,1:T(8,128)(2,1)}, u32[]{:S(2)}) copy-start(bf16[128,2048]{0,1:T(8,128)(2,1)} %copy.60) | copy-start | bytes 1572868
  78.2 8.7 %copy-start.5 = (bf16[128,1,2048]{0,2,1:T(8,128)(2,1)S(1)}, bf16[128,1,2048]{0,2,1:T(8,128)(2,1)}, u32[]{:S(2)}) copy-start(bf16[128,1,2048]{0,2,1:T(8,128)(2,1)} %constant_dynamic-slice_fusion.1) | copy-start | bytes 1572868
  79.4 8.4 %copy-start.3 = (bf16[128,1,2048]{0,2,1:T(8,128)(2,1)}, bf16[128,1,2048]{0,2,1:T(8,128)(2,1)S(1)}, u32[]{:S(2)}) copy-start(bf16[128,1,2048]{0,2,1:T(8,128)(2,1)S(1)} %constant_dynamic-slice_fusion.3) | copy-start | bytes 1572868
  81.1 4.8 %copy-start.19 = (bf16[128,308]{0,1:T(8,128)(2,1)S(1)}, bf16[128,308]{0,1:T(8,128)(2,1)}, u32[]{:S(2)}) copy-start(bf16[128,308]{0,1:T(8,128)(2,1)} %copy-done.18) | copy-start | bytes 236548
  83.3 12.0 %collective-permute-start.4 = (bf16[616,256]{1,0:T(8,128)(2,1)}, bf16[616,256]{1,0:T(8,128)(2,1)}, u32[]{:S(2)}, u32[]{:S(2)}) collective-permute-start(bf16[616,256]{1,0:T(8,128)(2,1)} %convolution_convert_fusion), channel_id=1, source_target_pairs={{0,48},{48,96},{96,144},{144,192},{192,240},{240,288},{288,336},{3... | collective-permute-start | bytes 946184 | tf_op jit(solution)/shard_map/ppermute | solution.py:100
  87.8 7.6 %collective-permute-start.6 = (bf16[308,256]{1,0:T(8,128)(2,1)}, bf16[308,256]{1,0:T(8,128)(2,1)}, u32[]{:S(2)}, u32[]{:S(2)}) collective-permute-start(bf16[308,256]{1,0:T(8,128)(2,1)} %convolution_convert_fusion.1), channel_id=1, source_target_pairs={{0,336},{48,0},{96,48},{144,96},{192,144},{240,192},{288,240},{336... | collective-permute-start | bytes 473096 | tf_op jit(solution)/shard_map/ppermute | solution.py:101
  97.3 9.6 %collective-permute-start.14 = (bf16[308,256]{1,0:T(8,128)(2,1)}, bf16[308,256]{1,0:T(8,128)(2,1)}, u32[]{:S(2)}, u32[]{:S(2)}) collective-permute-start(bf16[308,256]{1,0:T(8,128)(2,1)} %add_convert_fusion.11), channel_id=1, source_target_pairs={{0,336},{48,0},{96,48},{144,96},{192,144},{240,192},{288,240},{336... | collective-permute-start | bytes 473096 | tf_op jit(solution)/shard_map/ppermute | solution.py:101
  105.0 10.4 %collective-permute-start.8 = (bf16[616,256]{1,0:T(8,128)(2,1)}, bf16[616,256]{1,0:T(8,128)(2,1)}, u32[]{:S(2)}, u32[]{:S(2)}) collective-permute-start(bf16[616,256]{1,0:T(8,128)(2,1)} %add_convert_fusion.5), channel_id=1, source_target_pairs={{0,48},{48,96},{96,144},{144,192},{192,240},{240,288},{288,336},{3... | collective-permute-start | bytes 946184 | tf_op jit(solution)/shard_map/ppermute | solution.py:100
  108.9 10.5 %collective-permute-start.15 = (bf16[308,256]{1,0:T(8,128)(2,1)}, bf16[308,256]{1,0:T(8,128)(2,1)}, u32[]{:S(2)}, u32[]{:S(2)}) collective-permute-start(bf16[308,256]{1,0:T(8,128)(2,1)} %add_convert_fusion.10), channel_id=1, source_target_pairs={{0,336},{48,0},{96,48},{144,96},{192,144},{240,192},{288,240},{336... | collective-permute-start | bytes 473096 | tf_op jit(solution)/shard_map/ppermute | solution.py:101
  117.3 13.4 %collective-permute-start.9 = (bf16[616,256]{1,0:T(8,128)(2,1)}, bf16[616,256]{1,0:T(8,128)(2,1)}, u32[]{:S(2)}, u32[]{:S(2)}) collective-permute-start(bf16[616,256]{1,0:T(8,128)(2,1)} %add_convert_fusion.4), channel_id=1, source_target_pairs={{0,48},{48,96},{96,144},{144,192},{192,240},{240,288},{288,336},{3... | collective-permute-start | bytes 946184 | tf_op jit(solution)/shard_map/ppermute | solution.py:100
  119.3 14.8 %copy-start.10 = (bf16[4096,308]{0,1:T(8,128)(2,1)S(1)}, bf16[4096,308]{0,1:T(8,128)(2,1)}, u32[]{:S(2)}) copy-start(bf16[4096,308]{0,1:T(8,128)(2,1)} %param.11) | copy-start | bytes 7569412
  119.4 14.8 %copy-start.17 = (bf16[128,308]{0,1:T(8,128)(2,1)S(1)}, bf16[128,308]{0,1:T(8,128)(2,1)}, u32[]{:S(2)}) copy-start(bf16[128,308]{0,1:T(8,128)(2,1)} %copy-done.15) | copy-start | bytes 236548
  120.8 14.2 %collective-permute-start.16 = (bf16[308,256]{1,0:T(8,128)(2,1)S(1)}, bf16[308,256]{1,0:T(8,128)(2,1)S(1)}, u32[]{:S(2)}, u32[]{:S(2)}) collective-permute-start(bf16[308,256]{1,0:T(8,128)(2,1)S(1)} %add_convert_fusion.9), channel_id=1, source_target_pairs={{0,336},{48,0},{96,48},{144,96},{192,144},{240,192},{288,240},{336... | collective-permute-start | bytes 473096 | tf_op jit(solution)/shard_map/ppermute | solution.py:101
  132.1 10.2 %copy-start.4 = (bf16[128,1,2048]{0,2,1:T(8,128)(2,1)S(1)}, bf16[128,1,2048]{0,2,1:T(8,128)(2,1)}, u32[]{:S(2)}) copy-start(bf16[128,1,2048]{0,2,1:T(8,128)(2,1)} %copy-done.3) | copy-start | bytes 1572868
  132.1 10.2 %collective-permute-start.10 = (bf16[616,256]{1,0:T(8,128)(2,1)S(1)}, bf16[616,256]{1,0:T(8,128)(2,1)S(1)}, u32[]{:S(2)}, u32[]{:S(2)}) collective-permute-start(bf16[616,256]{1,0:T(8,128)(2,1)S(1)} %add_convert_fusion.3), channel_id=1, source_target_pairs={{0,48},{48,96},{96,144},{144,192},{192,240},{240,288},{288,336},{3... | collective-permute-start | bytes 946184 | tf_op jit(solution)/shard_map/ppermute | solution.py:100
  135.0 9.5 %copy-start.14 = (bf16[128,308]{0,1:T(8,128)(2,1)S(1)}, bf16[128,308]{0,1:T(8,128)(2,1)}, u32[]{:S(2)}) copy-start(bf16[128,308]{0,1:T(8,128)(2,1)} %copy-done.12) | copy-start | bytes 236548
  135.3 12.9 %collective-permute-start.17 = (bf16[308,256]{1,0:T(8,128)(2,1)S(1)}, bf16[308,256]{1,0:T(8,128)(2,1)S(1)}, u32[]{:S(2)}, u32[]{:S(2)}) collective-permute-start(bf16[308,256]{1,0:T(8,128)(2,1)S(1)} %add_convert_fusion.8), channel_id=1, source_target_pairs={{0,336},{48,0},{96,48},{144,96},{192,144},{240,192},{288,240},{336... | collective-permute-start | bytes 473096 | tf_op jit(solution)/shard_map/ppermute | solution.py:101
  142.6 11.7 %collective-permute-start.11 = (bf16[616,256]{1,0:T(8,128)(2,1)S(1)}, bf16[616,256]{1,0:T(8,128)(2,1)S(1)}, u32[]{:S(2)}, u32[]{:S(2)}) collective-permute-start(bf16[616,256]{1,0:T(8,128)(2,1)S(1)} %add_convert_fusion.2), channel_id=1, source_target_pairs={{0,48},{48,96},{96,144},{144,192},{192,240},{240,288},{288,336},{3... | collective-permute-start | bytes 946184 | tf_op jit(solution)/shard_map/ppermute | solution.py:100
  146.3 27.3 %collective-permute-start.7 = (bf16[128,4096]{1,0:T(8,128)(2,1)}, bf16[128,4096]{1,0:T(8,128)(2,1)}, u32[]{:S(2)}, u32[]{:S(2)}) collective-permute-start(bf16[128,4096]{1,0:T(8,128)(2,1)} %fusion), channel_id=1, source_target_pairs={{1,0},{2,1},{3,2},{4,3},{5,4},{6,5},{7,6},{8,7},{9,8},{10,9},{11,1... | collective-permute-start | bytes 3145736 | tf_op jit(solution)/shard_map/ppermute | solution.py:13
  149.1 9.5 %collective-permute-start.18 = (bf16[308,256]{1,0:T(8,128)(2,1)}, bf16[308,256]{1,0:T(8,128)(2,1)}, u32[]{:S(2)}, u32[]{:S(2)}) collective-permute-start(bf16[308,256]{1,0:T(8,128)(2,1)} %add_convert_fusion.7), channel_id=1, source_target_pairs={{0,336},{48,0},{96,48},{144,96},{192,144},{240,192},{288,240},{336... | collective-permute-start | bytes 473096 | tf_op jit(solution)/shard_map/ppermute | solution.py:101
  155.3 13.0 %collective-permute-start.12 = (bf16[616,256]{1,0:T(8,128)(2,1)}, bf16[616,256]{1,0:T(8,128)(2,1)}, u32[]{:S(2)}, u32[]{:S(2)}) collective-permute-start(bf16[616,256]{1,0:T(8,128)(2,1)} %add_convert_fusion.1), channel_id=1, source_target_pairs={{0,48},{48,96},{96,144},{144,192},{192,240},{240,288},{288,336},{3... | collective-permute-start | bytes 946184 | tf_op jit(solution)/shard_map/ppermute | solution.py:100
  160.5 11.7 %collective-permute-start.19 = (bf16[308,256]{1,0:T(8,128)(2,1)}, bf16[308,256]{1,0:T(8,128)(2,1)}, u32[]{:S(2)}, u32[]{:S(2)}) collective-permute-start(bf16[308,256]{1,0:T(8,128)(2,1)} %add_convert_fusion.6), channel_id=1, source_target_pairs={{0,336},{48,0},{96,48},{144,96},{192,144},{240,192},{288,240},{336... | collective-permute-start | bytes 473096 | tf_op jit(solution)/shard_map/ppermute | solution.py:101
  170.3 12.1 %collective-permute-start.13 = (bf16[616,256]{1,0:T(8,128)(2,1)}, bf16[616,256]{1,0:T(8,128)(2,1)}, u32[]{:S(2)}, u32[]{:S(2)}) collective-permute-start(bf16[616,256]{1,0:T(8,128)(2,1)} %add_convert_fusion), channel_id=1, source_target_pairs={{0,48},{48,96},{96,144},{144,192},{192,240},{240,288},{288,336},{3... | collective-permute-start | bytes 946184 | tf_op jit(solution)/shard_map/ppermute | solution.py:100
  (8 other events, 26.8 us)

commit v10 on v7

--- a/solution.py
+++ b/solution.py
@@ -110,11 +110,12 @@
 
 def shards(tokens, cotangent, gate_weight, up_weight, down_weight, counts, seg_ids, pair_side):
     weights = token_weights(counts, seg_ids, pair_side)
-    upstream = (cotangent.astype(jnp.float32) * weights[..., None]).astype(jnp.bfloat16)
     width = tokens.shape[-1]
     tok_rows = tokens.reshape(-1, width)
-    grad_rows = upstream.reshape(-1, width)
-    moved_rows, moved_grads = shifted(jnp.stack([tok_rows, grad_rows]), "blk", 1)
+    grad_rows = cotangent.reshape(-1, width)
+    scale_rows = weights.reshape(-1, 1)
+    moved_rows, moved_cot, moved_scale = shifted((tok_rows, grad_rows, scale_rows), "blk", 1)
+    moved_grads = (moved_cot.astype(jnp.float32) * moved_scale).astype(jnp.bfloat16)
     n = lax.axis_size("dp")
     nb = lax.axis_size("blk")
     ny = n // 2
@@ -124,7 +125,8 @@
     diagonal = [
         (d * nb + j, ((d + ny) % n) * nb + (j + 1) % nb) for d in range(n) for j in range(nb)
     ]
-    tok_peer, grad_peer = lax.ppermute(jnp.stack(other), ("dp", "blk"), diagonal)
+    tok_peer, cot_peer, scale_peer = lax.ppermute(other + (scale_rows,), ("dp", "blk"), diagonal)
+    grad_peer = (cot_peer.astype(jnp.float32) * scale_peer).astype(jnp.bfloat16)
     grad_moved, panel_grads = backward_core(
         moved_rows, moved_grads, tok_peer, grad_peer, gate_weight, up_weight, down_weight
     )

time: 176 us -> 180 us (1.023)
  the two profiles are of different devices: /device:TPU:26 before, /device:TPU:24 now
where the time goes in v10:
time: 180 us; the launch traced here: 179 us
  starting transfers between devices  77.2 us (43%)
  waiting for transfers between devices  53.4 us (30%)
  local copies, waits for them, and re-layouts  23.9 us (13%)
  matrix products  15.9 us (9%)
  other arithmetic  6.23 us (3%)
  between operations  2.3 us (1%)
    ppermute x7, starting transfers between devices, reduce_over_y(): recv_f = lax.ppermute(acc_f.astype(jnp.bfloat16), 'dp', fwd)  37.4 us
    ppermute x3, waiting for transfers between devices, shards(): lax.ppermute(other + (scale_rows,), ('dp', 'blk'), diagonal)  20.6 us
    ppermute x7, waiting for transfers between devices, reduce_over_y(): recv_b = lax.ppermute(acc_b.astype(jnp.bfloat16), 'dp', bwd)  17.8 us
    ppermute x3, starting transfers between devices, shards(): lax.ppermute(other + (scale_rows,), ('dp', 'blk'), diagonal)  14.7 us
    ppermute x7, starting transfers between devices, reduce_over_y(): recv_b = lax.ppermute(acc_b.astype(jnp.bfloat16), 'dp', bwd)  14 us
    ppermute x4, starting transfers between devices, shifted(): return lax.ppermute(block, axis, route)  8.54 us
    ppermute x7, waiting for transfers between devices, reduce_over_y(): recv_f = lax.ppermute(acc_f.astype(jnp.bfloat16), 'dp', fwd)  7.77 us
    unnamed x21, local copies, waits for them, and re-layouts  7.64 us
  transfers between devices with their start and end apart: 22, of which 12 were waited for; matrix products, arithmetic and copies ran while one was open for 12% of the time, Pallas kernels for 0%

profile of v10, /device:TPU:24, one launch (start us, length us, event | category | flops | bytes accessed | tf_op | source)
XLA Modules:
  0.0 178.9 jit_solution(8459178033605621417)
XLA Ops:
  0.7 2.4 %copy.87 = bf16[1,1,128,4096]{2,3,1,0:T(8,128)(2,1)} copy(bf16[1,1,128,4096]{3,2,1,0:T(8,128)(2,1)} %param.8) | data formatting | bytes 2097152 | tf_op args[0]
  3.1 2.3 %copy.92 = bf16[1,1,128,4096]{2,3,1,0:T(8,128)(2,1)} copy(bf16[1,1,128,4096]{3,2,1,0:T(8,128)(2,1)} %param.9) | data formatting | bytes 2097152 | tf_op args[1]
  5.4 2.1 %constant_dynamic-slice_fusion = (bf16[128,1,2048]{0,2,1:T(8,128)(2,1)S(1)}, bf16[128,1,2048]{0,2,1:T(8,128)(2,1)}) fusion(bf16[128,2,2048]{0,2,1:T(8,128)(2,1)} %bitcast.245, s32[]{:T(128)S(6)} %select_n.148, bf16[128,2,2048]{0,2,1:T(8,128)(2,1)} %bitcast.244), kind=kLoop, calls=%fused_computation.232 | loop fusion | bytes 2097156 | tf_op jit(solution)/shard_map/jit(dynamic_index_in_dim)/dynamic_slice | solution.py:124
  9.5 4.4 %collective-permute-start.4 = (bf16[128,2048]{1,0:T(8,128)(2,1)}, bf16[128,2048]{1,0:T(8,128)(2,1)}, u32[]{:S(2)}, u32[]{:S(2)}) collective-permute-start(bf16[128,2048]{1,0:T(8,128)(2,1)} %bitcast.252), channel_id=1, source_target_pairs={{0,385},{1,386},{2,387},{3,388},{4,389},{5,390},{6,391},{7,392},{8... | collective-permute-start | bytes 1572872 | tf_op jit(solution)/shard_map/ppermute | solution.py:128
  13.9 2.3 %collective-permute-start = (bf16[128,4096]{1,0:T(8,128)(2,1)}, bf16[128,4096]{1,0:T(8,128)(2,1)}, u32[]{:S(2)}, u32[]{:S(2)}) collective-permute-start(bf16[128,4096]{1,0:T(8,128)(2,1)} %bitcast.248), channel_id=1, source_target_pairs={{47,0},{0,1},{1,2},{2,3},{3,4},{4,5},{5,6},{6,7},{7,8},{8,9},{9,10... | collective-permute-start | bytes 3145736 | tf_op jit(solution)/shard_map/ppermute | solution.py:13
  17.2 3.8 %collective-permute-start.5 = (bf16[128,2048]{1,0:T(8,128)(2,1)}, bf16[128,2048]{1,0:T(8,128)(2,1)S(1)}, u32[]{:S(2)}, u32[]{:S(2)}) collective-permute-start(bf16[128,2048]{1,0:T(8,128)(2,1)} %bitcast.253), channel_id=1, source_target_pairs={{0,385},{1,386},{2,387},{3,388},{4,389},{5,390},{6,391},{7,392},{8... | collective-permute-start | bytes 1572872 | tf_op jit(solution)/shard_map/ppermute | solution.py:128
  21.9 2.4 %collective-permute-start.1 = (f32[128,1]{0,1:T(1,128)S(1)}, f32[128,1]{0,1:T(1,128)S(1)}, u32[]{:S(2)}, u32[]{:S(2)}) collective-permute-start(f32[128,1]{0,1:T(1,128)S(1)} %bitcast.258), channel_id=1, source_target_pairs={{47,0},{0,1},{1,2},{2,3},{3,4},{4,5},{5,6},{6,7},{7,8},{8,9},{9,10... | collective-permute-start | bytes 1544 | tf_op jit(solution)/shard_map/ppermute | solution.py:13
  24.3 6.5 %collective-permute-start.6 = (f32[128,1]{0,1:T(1,128)S(1)}, f32[128,1]{0,1:T(1,128)S(1)}, u32[]{:S(2)}, u32[]{:S(2)}) collective-permute-start(f32[128,1]{0,1:T(1,128)S(1)} %bitcast.259), channel_id=1, source_target_pairs={{0,385},{1,386},{2,387},{3,388},{4,389},{5,390},{6,391},{7,392},{8... | collective-permute-start | bytes 1544 | tf_op jit(solution)/shard_map/ppermute | solution.py:128
  31.1 20.6 %collective-permute-done.6 = f32[128,1]{0,1:T(1,128)S(1)} collective-permute-done((f32[128,1]{0,1:T(1,128)S(1)}, f32[128,1]{0,1:T(1,128)S(1)}, u32[]{:S(2)}, u32[]{:S(2)}) %collective-permute-start.6) | collective-permute-done | bytes 544 | tf_op jit(solution)/shard_map/ppermute | solution.py:128
  57.9 2.5 %multiply_convert_fusion = bf16[128,4096]{1,0:T(8,128)(2,1)} fusion(bf16[128,4096]{1,0:T(8,128)(2,1)} %collective-permute-done, f32[128]{0:T(128)S(1)} %bitcast.254), kind=kLoop, calls=%fused_computation.66 | loop fusion | flops 1572864 | bytes 2097664 | tf_op jit(solution)/shard_map/convert_element_type | solution.py:118
  60.4 2.3 %copy.91 = bf16[128,4096]{0,1:T(8,128)(2,1)} copy(bf16[128,4096]{1,0:T(8,128)(2,1)} %multiply_convert_fusion) | data formatting | bytes 2097152 | tf_op jit(solution)/shard_map/convert_element_type | solution.py:118
  62.6 3.0 %fusion.220 = f32[128,308]{0,1:T(8,128)S(1)} fusion(bf16[128,4096]{1,0:T(8,128)(2,1)} %multiply_convert_fusion, bf16[4096,308]{0,1:T(8,128)(2,1)} %param.12), kind=kOutput, calls=%fused_computation.292 | convolution fusion | flops 322961408 | bytes 3729408 | tf_op jit(solution)/shard_map/dot_general | solution.py:56
  65.6 4.6 %collective-permute-done.2 = bf16[128,4096]{1,0:T(8,128)(2,1)} collective-permute-done((bf16[128,4096]{1,0:T(8,128)(2,1)}, bf16[128,4096]{1,0:T(8,128)(2,1)}, u32[]{:S(2)}, u32[]{:S(2)}) %collective-permute-start.2) | collective-permute-done | bytes 1048608 | tf_op jit(solution)/shard_map/ppermute | solution.py:13
  72.4 2.1 %multiply_convert_fusion.4 = (bf16[128,308]{0,1:T(8,128)(2,1)S(1)}, bf16[128,308]{0,1:T(8,128)(2,1)S(1)}, bf16[128,308]{0,1:T(8,128)(2,1)S(1)}) fusion(f32[128,308]{0,1:T(8,128)S(1)} %fusion.220, f32[128,308]{0,1:T(8,128)S(1)} %fusion.221, bf16[128,4096]{1,0:T(8,128)(2,1)} %collective-permute-done.2, bf16[4096,308]{0,1:T(8,128)(2,1)S(1)} %copy-done), kind=kOutput, calls=%fused_computation.106 | convolution fusion | flops 323552768 | bytes 4123648 | tf_op jit(solution)/shard_map/dot_general | solution.py:51
  75.8 2.6 %collective-permute-start.3 = (bf16[128,924]{0,1:T(8,128)(2,1)}, bf16[128,924]{0,1:T(8,128)(2,1)S(1)}, u32[]{:S(2)}, u32[]{:S(2)}) collective-permute-start(bf16[128,924]{0,1:T(8,128)(2,1)} %pad_maximum_fusion.1), channel_id=1, source_target_pairs={{0,384},{48,432},{96,480},{144,528},{192,576},{240,624},{288,672},... | collective-permute-start | bytes 709640 | tf_op jit(solution)/shard_map/ppermute | solution.py:62
  78.4 2.3 %copy.86 = bf16[128,4096]{0,1:T(8,128)(2,1)} copy(bf16[128,4096]{1,0:T(8,128)(2,1)} %collective-permute-done.2) | data formatting | bytes 2097152 | tf_op jit(solution)/shard_map/ppermute | solution.py:13
  83.0 2.6 %collective-permute-done.3 = bf16[128,924]{0,1:T(8,128)(2,1)S(1)} collective-permute-done((bf16[128,924]{0,1:T(8,128)(2,1)}, bf16[128,924]{0,1:T(8,128)(2,1)S(1)}, u32[]{:S(2)}, u32[]{:S(2)}) %collective-permute-start.3) | collective-permute-done | bytes 236576 | tf_op jit(solution)/shard_map/ppermute | solution.py:62
  92.1 2.4 %collective-permute-start.8 = (bf16[924,128]{1,0:T(8,128)(2,1)S(1)}, bf16[924,128]{1,0:T(8,128)(2,1)S(1)}, u32[]{:S(2)}, u32[]{:S(2)}) collective-permute-start(bf16[924,128]{1,0:T(8,128)(2,1)S(1)} %pad_maximum_fusion.3), channel_id=1, source_target_pairs={{0,336},{48,0},{96,48},{144,96},{192,144},{240,192},{288,240},{336... | collective-permute-start | bytes 709640 | tf_op jit(solution)/shard_map/ppermute | solution.py:101
  94.5 4.7 %collective-permute-start.7 = (bf16[924,128]{1,0:T(8,128)(2,1)S(1)}, bf16[924,128]{1,0:T(8,128)(2,1)S(1)}, u32[]{:S(2)}, u32[]{:S(2)}) collective-permute-start(bf16[924,128]{1,0:T(8,128)(2,1)S(1)} %pad_maximum_fusion.2), channel_id=1, source_target_pairs={{0,48},{48,96},{96,144},{144,192},{192,240},{240,288},{288,336},{3... | collective-permute-start | bytes 709640 | tf_op jit(solution)/shard_map/ppermute | solution.py:100
  100.2 2.9 %collective-permute-done.8 = bf16[924,128]{1,0:T(8,128)(2,1)S(1)} collective-permute-done((bf16[924,128]{1,0:T(8,128)(2,1)S(1)}, bf16[924,128]{1,0:T(8,128)(2,1)S(1)}, u32[]{:S(2)}, u32[]{:S(2)}) %collective-permute-start.8) | collective-permute-done | bytes 236576 | tf_op jit(solution)/shard_map/ppermute | solution.py:101
  103.1 2.1 %collective-permute-done.7 = bf16[924,128]{1,0:T(8,128)(2,1)S(1)} collective-permute-done((bf16[924,128]{1,0:T(8,128)(2,1)S(1)}, bf16[924,128]{1,0:T(8,128)(2,1)S(1)}, u32[]{:S(2)}, u32[]{:S(2)}) %collective-permute-start.7) | collective-permute-done | bytes 236576 | tf_op jit(solution)/shard_map/ppermute | solution.py:100
  105.3 5.6 %collective-permute-start.10 = (bf16[924,128]{1,0:T(8,128)(2,1)S(1)}, bf16[924,128]{1,0:T(8,128)(2,1)S(1)}, u32[]{:S(2)}, u32[]{:S(2)}) collective-permute-start(bf16[924,128]{1,0:T(8,128)(2,1)S(1)} %fusion.1), channel_id=1, source_target_pairs={{0,48},{48,96},{96,144},{144,192},{192,240},{240,288},{288,336},{3... | collective-permute-start | bytes 709640 | tf_op jit(solution)/shard_map/ppermute | solution.py:100
  113.3 2.9 %collective-permute-done.10 = bf16[924,128]{1,0:T(8,128)(2,1)S(1)} collective-permute-done((bf16[924,128]{1,0:T(8,128)(2,1)S(1)}, bf16[924,128]{1,0:T(8,128)(2,1)S(1)}, u32[]{:S(2)}, u32[]{:S(2)}) %collective-permute-start.10) | collective-permute-done | bytes 236576 | tf_op jit(solution)/shard_map/ppermute | solution.py:100
  116.3 5.6 %collective-permute-start.11 = (bf16[924,128]{1,0:T(8,128)(2,1)S(1)}, bf16[924,128]{1,0:T(8,128)(2,1)S(1)}, u32[]{:S(2)}, u32[]{:S(2)}) collective-permute-start(bf16[924,128]{1,0:T(8,128)(2,1)S(1)} %fusion.2), channel_id=1, source_target_pairs={{0,48},{48,96},{96,144},{144,192},{192,240},{240,288},{288,336},{3... | collective-permute-start | bytes 709640 | tf_op jit(solution)/shard_map/ppermute | solution.py:100
  126.4 5.6 %collective-permute-start.12 = (bf16[924,128]{1,0:T(8,128)(2,1)S(1)}, bf16[924,128]{1,0:T(8,128)(2,1)S(1)}, u32[]{:S(2)}, u32[]{:S(2)}) collective-permute-start(bf16[924,128]{1,0:T(8,128)(2,1)S(1)} %fusion.3), channel_id=1, source_target_pairs={{0,48},{48,96},{96,144},{144,192},{192,240},{240,288},{288,336},{3... | collective-permute-start | bytes 709640 | tf_op jit(solution)/shard_map/ppermute | solution.py:100
  135.6 5.6 %collective-permute-start.13 = (bf16[924,128]{1,0:T(8,128)(2,1)S(1)}, bf16[924,128]{1,0:T(8,128)(2,1)S(1)}, u32[]{:S(2)}, u32[]{:S(2)}) collective-permute-start(bf16[924,128]{1,0:T(8,128)(2,1)S(1)} %fusion.4), channel_id=1, source_target_pairs={{0,48},{48,96},{96,144},{144,192},{192,240},{240,288},{288,336},{3... | collective-permute-start | bytes 709640 | tf_op jit(solution)/shard_map/ppermute | solution.py:100
  146.0 5.1 %collective-permute-start.14 = (bf16[924,128]{1,0:T(8,128)(2,1)S(1)}, bf16[924,128]{1,0:T(8,128)(2,1)S(1)}, u32[]{:S(2)}, u32[]{:S(2)}) collective-permute-start(bf16[924,128]{1,0:T(8,128)(2,1)S(1)} %fusion.5), channel_id=1, source_target_pairs={{0,48},{48,96},{96,144},{144,192},{192,240},{240,288},{288,336},{3... | collective-permute-start | bytes 709640 | tf_op jit(solution)/shard_map/ppermute | solution.py:100
  151.4 3.9 %collective-permute-done.19 = bf16[924,128]{1,0:T(8,128)(2,1)S(1)} collective-permute-done((bf16[924,128]{1,0:T(8,128)(2,1)S(1)}, bf16[924,128]{1,0:T(8,128)(2,1)S(1)}, u32[]{:S(2)}, u32[]{:S(2)}) %collective-permute-start.19) | collective-permute-done | bytes 236576 | tf_op jit(solution)/shard_map/ppermute | solution.py:101
  157.4 5.1 %collective-permute-start.15 = (bf16[924,128]{1,0:T(8,128)(2,1)S(1)}, bf16[924,128]{1,0:T(8,128)(2,1)S(1)}, u32[]{:S(2)}, u32[]{:S(2)}) collective-permute-start(bf16[924,128]{1,0:T(8,128)(2,1)S(1)} %fusion.6), channel_id=1, source_target_pairs={{0,48},{48,96},{96,144},{144,192},{192,240},{240,288},{288,336},{3... | collective-permute-start | bytes 709640 | tf_op jit(solution)/shard_map/ppermute | solution.py:100
  162.8 3.1 %collective-permute-done.20 = bf16[924,128]{1,0:T(8,128)(2,1)S(1)} collective-permute-done((bf16[924,128]{1,0:T(8,128)(2,1)S(1)}, bf16[924,128]{1,0:T(8,128)(2,1)S(1)}, u32[]{:S(2)}, u32[]{:S(2)}) %collective-permute-start.20) | collective-permute-done | bytes 236576 | tf_op jit(solution)/shard_map/ppermute | solution.py:101
  167.9 7.6 %collective-permute-done.21 = bf16[924,128]{1,0:T(8,128)(2,1)S(1)} collective-permute-done((bf16[924,128]{1,0:T(8,128)(2,1)S(1)}, bf16[924,128]{1,0:T(8,128)(2,1)S(1)}, u32[]{:S(2)}, u32[]{:S(2)}) %collective-permute-start.21) | collective-permute-done | bytes 236576 | tf_op jit(solution)/shard_map/ppermute | solution.py:101
  176.6 2.3 %copy.128 = bf16[1,1,128,4096]{3,2,1,0:T(8,128)(2,1)} copy(bf16[1,1,128,4096]{3,2,1,0:T(8,128)(2,1)} %bitcast.250) | data formatting | bytes 2097152
  (106 shorter events, 43.5 us)
Async XLA Ops:
  0.6 71.7 %copy-start = (bf16[4096,308]{0,1:T(8,128)(2,1)S(1)}, bf16[4096,308]{0,1:T(8,128)(2,1)}, u32[]{:S(2)}) copy-start(bf16[4096,308]{0,1:T(8,128)(2,1)} %param.10) | copy-start | bytes 7569412
  5.4 16.3 %copy-start.7 = (s32[1,1,128]{2,1,0:T(1,128)S(1)}, s32[1,1,128]{2,1,0:T(1,128)}, u32[]{:S(2)}) copy-start(s32[1,1,128]{2,1,0:T(1,128)} %param.14) | copy-start | bytes 1540
  5.4 16.4 %copy-start.8 = (s32[1,1,4]{2,1,0:T(1,128)S(1)}, s32[1,1,4]{2,1,0:T(1,128)}, u32[]{:S(2)}) copy-start(s32[1,1,4]{2,1,0:T(1,128)} %param.15) | copy-start | bytes 52
  9.5 46.4 %collective-permute-start.4 = (bf16[128,2048]{1,0:T(8,128)(2,1)}, bf16[128,2048]{1,0:T(8,128)(2,1)}, u32[]{:S(2)}, u32[]{:S(2)}) collective-permute-start(bf16[128,2048]{1,0:T(8,128)(2,1)} %bitcast.252), channel_id=1, source_target_pairs={{0,385},{1,386},{2,387},{3,388},{4,389},{5,390},{6,391},{7,392},{8... | collective-permute-start | bytes 1572872 | tf_op jit(solution)/shard_map/ppermute | solution.py:128
  13.9 44.0 %collective-permute-start = (bf16[128,4096]{1,0:T(8,128)(2,1)}, bf16[128,4096]{1,0:T(8,128)(2,1)}, u32[]{:S(2)}, u32[]{:S(2)}) collective-permute-start(bf16[128,4096]{1,0:T(8,128)(2,1)} %bitcast.248), channel_id=1, source_target_pairs={{47,0},{0,1},{1,2},{2,3},{3,4},{4,5},{5,6},{6,7},{7,8},{8,9},{9,10... | collective-permute-start | bytes 3145736 | tf_op jit(solution)/shard_map/ppermute | solution.py:13
  17.2 36.4 %collective-permute-start.5 = (bf16[128,2048]{1,0:T(8,128)(2,1)}, bf16[128,2048]{1,0:T(8,128)(2,1)S(1)}, u32[]{:S(2)}, u32[]{:S(2)}) collective-permute-start(bf16[128,2048]{1,0:T(8,128)(2,1)} %bitcast.253), channel_id=1, source_target_pairs={{0,385},{1,386},{2,387},{3,388},{4,389},{5,390},{6,391},{7,392},{8... | collective-permute-start | bytes 1572872 | tf_op jit(solution)/shard_map/ppermute | solution.py:128
  21.9 36.0 %collective-permute-start.1 = (f32[128,1]{0,1:T(1,128)S(1)}, f32[128,1]{0,1:T(1,128)S(1)}, u32[]{:S(2)}, u32[]{:S(2)}) collective-permute-start(f32[128,1]{0,1:T(1,128)S(1)} %bitcast.258), channel_id=1, source_target_pairs={{47,0},{0,1},{1,2},{2,3},{3,4},{4,5},{5,6},{6,7},{7,8},{8,9},{9,10... | collective-permute-start | bytes 1544 | tf_op jit(solution)/shard_map/ppermute | solution.py:13
  24.3 27.4 %collective-permute-start.6 = (f32[128,1]{0,1:T(1,128)S(1)}, f32[128,1]{0,1:T(1,128)S(1)}, u32[]{:S(2)}, u32[]{:S(2)}) collective-permute-start(f32[128,1]{0,1:T(1,128)S(1)} %bitcast.259), channel_id=1, source_target_pairs={{0,385},{1,386},{2,387},{3,388},{4,389},{5,390},{6,391},{7,392},{8... | collective-permute-start | bytes 1544 | tf_op jit(solution)/shard_map/ppermute | solution.py:128
  51.7 18.6 %collective-permute-start.2 = (bf16[128,4096]{1,0:T(8,128)(2,1)}, bf16[128,4096]{1,0:T(8,128)(2,1)}, u32[]{:S(2)}, u32[]{:S(2)}) collective-permute-start(bf16[128,4096]{1,0:T(8,128)(2,1)} %bitcast.249), channel_id=1, source_target_pairs={{47,0},{0,1},{1,2},{2,3},{3,4},{4,5},{5,6},{6,7},{7,8},{8,9},{9,10... | collective-permute-start | bytes 3145736 | tf_op jit(solution)/shard_map/ppermute | solution.py:13
  62.6 7.7 %copy-start.2 = (bf16[4096,308]{0,1:T(8,128)(2,1)S(1)}, bf16[4096,308]{0,1:T(8,128)(2,1)}, u32[]{:S(2)}) copy-start(bf16[4096,308]{0,1:T(8,128)(2,1)} %param.11) | copy-start | bytes 7569412
  74.5 0.6 copy-start.5
  75.8 9.7 %collective-permute-start.3 = (bf16[128,924]{0,1:T(8,128)(2,1)}, bf16[128,924]{0,1:T(8,128)(2,1)S(1)}, u32[]{:S(2)}, u32[]{:S(2)}) collective-permute-start(bf16[128,924]{0,1:T(8,128)(2,1)} %pad_maximum_fusion.1), channel_id=1, source_target_pairs={{0,384},{48,432},{96,480},{144,528},{192,576},{240,624},{288,672},... | collective-permute-start | bytes 709640 | tf_op jit(solution)/shard_map/ppermute | solution.py:62
  80.7 5.8 %copy-start.1 = (bf16[128,2048]{0,1:T(8,128)(2,1)S(1)}, bf16[128,2048]{0,1:T(8,128)(2,1)}, u32[]{:S(2)}) copy-start(bf16[128,2048]{0,1:T(8,128)(2,1)} %copy.89) | copy-start | bytes 1572868
  81.9 5.2 %copy-start.6 = (bf16[128,308]{0,1:T(8,128)(2,1)S(1)}, bf16[128,308]{0,1:T(8,128)(2,1)}, u32[]{:S(2)}) copy-start(bf16[128,308]{0,1:T(8,128)(2,1)} %copy-done.5) | copy-start | bytes 236548
  92.1 11.0 %collective-permute-start.8 = (bf16[924,128]{1,0:T(8,128)(2,1)S(1)}, bf16[924,128]{1,0:T(8,128)(2,1)S(1)}, u32[]{:S(2)}, u32[]{:S(2)}) collective-permute-start(bf16[924,128]{1,0:T(8,128)(2,1)S(1)} %pad_maximum_fusion.3), channel_id=1, source_target_pairs={{0,336},{48,0},{96,48},{144,96},{192,144},{240,192},{288,240},{336... | collective-permute-start | bytes 709640 | tf_op jit(solution)/shard_map/ppermute | solution.py:101
  94.5 10.7 %collective-permute-start.7 = (bf16[924,128]{1,0:T(8,128)(2,1)S(1)}, bf16[924,128]{1,0:T(8,128)(2,1)S(1)}, u32[]{:S(2)}, u32[]{:S(2)}) collective-permute-start(bf16[924,128]{1,0:T(8,128)(2,1)S(1)} %pad_maximum_fusion.2), channel_id=1, source_target_pairs={{0,48},{48,96},{96,144},{144,192},{192,240},{240,288},{288,336},{3... | collective-permute-start | bytes 709640 | tf_op jit(solution)/shard_map/ppermute | solution.py:100
  105.3 10.9 %collective-permute-start.10 = (bf16[924,128]{1,0:T(8,128)(2,1)S(1)}, bf16[924,128]{1,0:T(8,128)(2,1)S(1)}, u32[]{:S(2)}, u32[]{:S(2)}) collective-permute-start(bf16[924,128]{1,0:T(8,128)(2,1)S(1)} %fusion.1), channel_id=1, source_target_pairs={{0,48},{48,96},{96,144},{144,192},{192,240},{240,288},{288,336},{3... | collective-permute-start | bytes 709640 | tf_op jit(solution)/shard_map/ppermute | solution.py:100
  111.1 20.9 %copy-start.3 = (bf16[4096,308]{0,1:T(8,128)(2,1)S(1)}, bf16[4096,308]{0,1:T(8,128)(2,1)}, u32[]{:S(2)}) copy-start(bf16[4096,308]{0,1:T(8,128)(2,1)} %param.11) | copy-start | bytes 7569412
  111.2 11.2 %collective-permute-start.16 = (bf16[924,128]{1,0:T(8,128)(2,1)S(1)}, bf16[924,128]{1,0:T(8,128)(2,1)S(1)}, u32[]{:S(2)}, u32[]{:S(2)}) collective-permute-start(bf16[924,128]{1,0:T(8,128)(2,1)S(1)} %fusion.7), channel_id=1, source_target_pairs={{0,336},{48,0},{96,48},{144,96},{192,144},{240,192},{288,240},{336... | collective-permute-start | bytes 709640 | tf_op jit(solution)/shard_map/ppermute | solution.py:101
  116.3 10.0 %collective-permute-start.11 = (bf16[924,128]{1,0:T(8,128)(2,1)S(1)}, bf16[924,128]{1,0:T(8,128)(2,1)S(1)}, u32[]{:S(2)}, u32[]{:S(2)}) collective-permute-start(bf16[924,128]{1,0:T(8,128)(2,1)S(1)} %fusion.2), channel_id=1, source_target_pairs={{0,48},{48,96},{96,144},{144,192},{192,240},{240,288},{288,336},{3... | collective-permute-start | bytes 709640 | tf_op jit(solution)/shard_map/ppermute | solution.py:100
  122.5 10.3 %collective-permute-start.17 = (bf16[924,128]{1,0:T(8,128)(2,1)S(1)}, bf16[924,128]{1,0:T(8,128)(2,1)S(1)}, u32[]{:S(2)}, u32[]{:S(2)}) collective-permute-start(bf16[924,128]{1,0:T(8,128)(2,1)S(1)} %fusion.8), channel_id=1, source_target_pairs={{0,336},{48,0},{96,48},{144,96},{192,144},{240,192},{288,240},{336... | collective-permute-start | bytes 709640 | tf_op jit(solution)/shard_map/ppermute | solution.py:101
  126.4 9.2 %collective-permute-start.12 = (bf16[924,128]{1,0:T(8,128)(2,1)S(1)}, bf16[924,128]{1,0:T(8,128)(2,1)S(1)}, u32[]{:S(2)}, u32[]{:S(2)}) collective-permute-start(bf16[924,128]{1,0:T(8,128)(2,1)S(1)} %fusion.3), channel_id=1, source_target_pairs={{0,48},{48,96},{96,144},{144,192},{192,240},{240,288},{288,336},{3... | collective-permute-start | bytes 709640 | tf_op jit(solution)/shard_map/ppermute | solution.py:100
  132.8 11.1 %collective-permute-start.18 = (bf16[924,128]{1,0:T(8,128)(2,1)S(1)}, bf16[924,128]{1,0:T(8,128)(2,1)S(1)}, u32[]{:S(2)}, u32[]{:S(2)}) collective-permute-start(bf16[924,128]{1,0:T(8,128)(2,1)S(1)} %fusion.9), channel_id=1, source_target_pairs={{0,336},{48,0},{96,48},{144,96},{192,144},{240,192},{288,240},{336... | collective-permute-start | bytes 709640 | tf_op jit(solution)/shard_map/ppermute | solution.py:101
  135.6 10.3 %collective-permute-start.13 = (bf16[924,128]{1,0:T(8,128)(2,1)S(1)}, bf16[924,128]{1,0:T(8,128)(2,1)S(1)}, u32[]{:S(2)}, u32[]{:S(2)}) collective-permute-start(bf16[924,128]{1,0:T(8,128)(2,1)S(1)} %fusion.4), channel_id=1, source_target_pairs={{0,48},{48,96},{96,144},{144,192},{192,240},{240,288},{288,336},{3... | collective-permute-start | bytes 709640 | tf_op jit(solution)/shard_map/ppermute | solution.py:100
  142.0 20.7 %collective-permute-start.9 = (bf16[128,4096]{1,0:T(8,128)(2,1)S(1)}, bf16[128,4096]{1,0:T(8,128)(2,1)S(1)}, u32[]{:S(2)}, u32[]{:S(2)}) collective-permute-start(bf16[128,4096]{1,0:T(8,128)(2,1)S(1)} %fusion), channel_id=1, source_target_pairs={{1,0},{2,1},{3,2},{4,3},{5,4},{6,5},{7,6},{8,7},{9,8},{10,9},{11,1... | collective-permute-start | bytes 3145736 | tf_op jit(solution)/shard_map/ppermute | solution.py:13
  144.1 11.3 %collective-permute-start.19 = (bf16[924,128]{1,0:T(8,128)(2,1)S(1)}, bf16[924,128]{1,0:T(8,128)(2,1)S(1)}, u32[]{:S(2)}, u32[]{:S(2)}) collective-permute-start(bf16[924,128]{1,0:T(8,128)(2,1)S(1)} %fusion.10), channel_id=1, source_target_pairs={{0,336},{48,0},{96,48},{144,96},{192,144},{240,192},{288,240},{336... | collective-permute-start | bytes 709640 | tf_op jit(solution)/shard_map/ppermute | solution.py:101
  146.0 11.3 %collective-permute-start.14 = (bf16[924,128]{1,0:T(8,128)(2,1)S(1)}, bf16[924,128]{1,0:T(8,128)(2,1)S(1)}, u32[]{:S(2)}, u32[]{:S(2)}) collective-permute-start(bf16[924,128]{1,0:T(8,128)(2,1)S(1)} %fusion.5), channel_id=1, source_target_pairs={{0,48},{48,96},{96,144},{144,192},{192,240},{240,288},{288,336},{3... | collective-permute-start | bytes 709640 | tf_op jit(solution)/shard_map/ppermute | solution.py:100
  155.4 10.4 %collective-permute-start.20 = (bf16[924,128]{1,0:T(8,128)(2,1)S(1)}, bf16[924,128]{1,0:T(8,128)(2,1)S(1)}, u32[]{:S(2)}, u32[]{:S(2)}) collective-permute-start(bf16[924,128]{1,0:T(8,128)(2,1)S(1)} %fusion.11), channel_id=1, source_target_pairs={{0,336},{48,0},{96,48},{144,96},{192,144},{240,192},{288,240},{336... | collective-permute-start | bytes 709640 | tf_op jit(solution)/shard_map/ppermute | solution.py:101
  157.4 10.4 %collective-permute-start.15 = (bf16[924,128]{1,0:T(8,128)(2,1)S(1)}, bf16[924,128]{1,0:T(8,128)(2,1)S(1)}, u32[]{:S(2)}, u32[]{:S(2)}) collective-permute-start(bf16[924,128]{1,0:T(8,128)(2,1)S(1)} %fusion.6), channel_id=1, source_target_pairs={{0,48},{48,96},{96,144},{144,192},{192,240},{240,288},{288,336},{3... | collective-permute-start | bytes 709640 | tf_op jit(solution)/shard_map/ppermute | solution.py:100
  162.8 12.8 %copy-start.4 = (bf16[128,4096]{1,0:T(8,128)(2,1)}, bf16[128,4096]{1,0:T(8,128)(2,1)S(1)}, u32[]{:S(2)}) copy-start(bf16[128,4096]{1,0:T(8,128)(2,1)S(1)} %collective-permute-done.9) | copy-start | bytes 3145732
  165.9 9.6 %collective-permute-start.21 = (bf16[924,128]{1,0:T(8,128)(2,1)S(1)}, bf16[924,128]{1,0:T(8,128)(2,1)S(1)}, u32[]{:S(2)}, u32[]{:S(2)}) collective-permute-start(bf16[924,128]{1,0:T(8,128)(2,1)S(1)} %fusion.12), channel_id=1, source_target_pairs={{0,336},{48,0},{96,48},{144,96},{192,144},{240,192},{288,240},{336... | collective-permute-start | bytes 709640 | tf_op jit(solution)/shard_map/ppermute | solution.py:101
